TPU v7x, 32 devices: a whole 2x2x4 slice. The times are simulated.
32 devices in a mesh: parts: 2 (over y), pix: 4 (over z), ang: 2 (over x), sl: 2 (over core).
Axes of the slice: x: 2, y: 2, z: 4, core: 2. Of those that a mesh axis runs over, the one named last changes fastest.
Arguments:
- volume: float32 [512, 1024], P(('parts', 'pix'), 'sl'), parts along dimension 0, may hold values from 0 to 2
- sinogram: float32 [4, 32, 1024], P(('parts', 'ang'), 'pix', 'sl'), parts along dimension 0, may hold values from 0 to 5632
- table: bfloat16 [32, 4096], replicated, may hold values from 0.015 to 1
- blk_ray: int32 [2, 4, 1408], P('ang', 'pix'), may hold values from 0 to 31, as said below
- blk_pix: int32 [2, 4, 1408], P('ang', 'pix'), may hold values from 0 to 63, as said below
Outputs:
- volume_out: float32 [512, 1024], P(('parts', 'pix'), 'sl'), parts along dimension 0
- residual: float32 [4, 32, 1024], P(('parts', 'ang'), 'pix', 'sl'), parts along dimension 0
There are 2 independent parts, one for each index of `parts`. A program takes and returns all parts, laid end to end along the dimension named above; an argument that names none is the same for every part. Nothing has to cross between parts.
Inputs may be any that keep to these rules, and one draw needn't show every extreme that they name: `blk_ray`: entry [g, p, b] is a ray tile of group g. The blocks of each (g, p) name every ray tile from 8 * p to 8 * p + 7, and at most 4 distinct ray tiles of any other such range of 8 tiles; in each group some range has exactly 4 of its tiles named by every other p. `blk_pix`: the blocks of each (g, p) name every pixel tile from 0 to 63.
All inputs are finite; a program needn't handle non-finite values.
Results may differ from a plain program's by a relative error of at most 0.0003.
Values may be sent and summed in bfloat16 or wider, within the bound.
No kernel may reach another device: no remote copies, remote signals or barrier semaphores. Data moves between devices by JAX's collectives and lax.ppermute only.
A program may use at most 64 MiB of HBM per device.

v0:
```python
import jax
import jax.numpy as jnp
from jax import lax
from jax.sharding import PartitionSpec as P

TILE = 64
KINDS = 32
ITERS = 2
PER_KIND = 44


def project_local(low_volume, pattern, pixel_list, ray_list, ray_total):
    tiles_dev = low_volume.shape[0]
    slices = low_volume.shape[1] // TILE
    low_tiles = low_volume.reshape(tiles_dev, slices, TILE)
    kinds_each = KINDS // 4

    def project_one_group(running, inputs):
        patterns, pix_ids, ray_ids = inputs
        picked = jnp.take(low_tiles, pix_ids, axis=0).reshape(kinds_each, PER_KIND, slices, TILE)
        images = jnp.einsum("kbsj,kij->kbsi", picked, patterns, preferred_element_type=jnp.float32)
        images = images.reshape(kinds_each * PER_KIND, slices * TILE)
        return (running + jax.ops.segment_sum(images, ray_ids, ray_total), None)

    inputs = (
        pattern.reshape(4, kinds_each, TILE, TILE),
        pixel_list.reshape(4, -1),
        ray_list.reshape(4, -1),
    )
    initial = jnp.zeros((ray_total, slices * TILE), jnp.float32)
    running, unused = lax.scan(project_one_group, initial, inputs)
    return running


def back_local(row_table, pattern, pixel_list, row_index, tiles_dev):
    slices = row_table.shape[1] // TILE
    table_tiles = row_table.reshape(row_table.shape[0], slices, TILE)
    kinds_each = KINDS // 4

    def back_one_group(running, inputs):
        patterns, pix_ids, row_ids = inputs
        picked = jnp.take(table_tiles, row_ids, axis=0).reshape(kinds_each, PER_KIND, slices, TILE)
        images = jnp.einsum("kbsi,kij->kbsj", picked, patterns, preferred_element_type=jnp.float32)
        images = images.reshape(kinds_each * PER_KIND, slices * TILE)
        return (running + jax.ops.segment_sum(images, pix_ids, tiles_dev), None)

    inputs = (
        pattern.reshape(4, kinds_each, TILE, TILE),
        pixel_list.reshape(4, -1),
        row_index.reshape(4, -1),
    )
    initial = jnp.zeros((tiles_dev, slices * TILE), jnp.float32)
    running, unused = lax.scan(back_one_group, initial, inputs)
    return running


def per_device(volume, sinogram, table, blk_ray, blk_pix):
    pix_count = lax.axis_size("pix")
    tiles_dev = volume.shape[0]
    row_width = volume.shape[1]
    slices = row_width // TILE
    rays_dev = sinogram.shape[1]
    ray_total = rays_dev * pix_count
    ray_list = blk_ray.reshape(-1)
    pixel_list = blk_pix.reshape(-1)
    pattern = table.reshape(KINDS, TILE, TILE)
    pattern_wide = table.astype(jnp.float32).reshape(KINDS, TILE, TILE)
    row_block = jnp.broadcast_to(
        jnp.sum(pattern_wide, axis=2)[:, None, :], (KINDS, PER_KIND, TILE)
    ).reshape(-1, TILE)
    col_block = jnp.broadcast_to(
        jnp.sum(pattern_wide, axis=1)[:, None, :], (KINDS, PER_KIND, TILE)
    ).reshape(-1, TILE)
    row_part = jax.ops.segment_sum(row_block, ray_list, ray_total)
    col_part = jax.ops.segment_sum(col_block, pixel_list, tiles_dev)
    measured = sinogram[0]
    col_weight = lax.psum(col_part, "ang")
    current = volume
    scaled = measured
    for iteration in range(ITERS):
        low_volume = current.astype(jnp.bfloat16)
        partial_rows = project_local(low_volume, pattern, pixel_list, ray_list, ray_total)
        if iteration == 0:
            summed, row_weight = (
                lax.psum_scatter(partial_rows, "pix", scatter_dimension=0, tiled=True),
                lax.psum_scatter(row_part, "pix", scatter_dimension=0, tiled=True),
            )
        else:
            summed = lax.psum_scatter(partial_rows, "pix", scatter_dimension=0, tiled=True)
        scaled = (measured - summed) / jnp.tile(row_weight, (1, slices))
        scaled_low = scaled.astype(jnp.bfloat16)
        row_table = lax.all_gather(scaled_low, "pix", axis=0, tiled=True)
        back_sum = back_local(row_table, pattern, pixel_list, ray_list, tiles_dev)
        summed_update = lax.psum(back_sum, "ang")
        current = current + summed_update / jnp.tile(col_weight, (1, slices))
    return (current, scaled[None])


def solution(mesh):
    return jax.shard_map(
        per_device,
        mesh=mesh,
        in_specs=(
            P(("parts", "pix"), "sl"),
            P(("parts", "ang"), "pix", "sl"),
            P(),
            P("ang", "pix", None),
            P("ang", "pix", None),
        ),
        out_specs=(P(("parts", "pix"), "sl"), P(("parts", "ang"), "pix", "sl")),
        check_vma=False,
    )
```

profile of v0, /device:TPU:0, one launch (start us, length us, event | category | flops | bytes accessed | tf_op | source)
XLA Modules:
  0.0 257.0 jit_solution(8087572826325011818)
XLA Ops:
  11.4 28.3 %while.40 = (s32[]{:T(128)}, f32[32,512]{1,0:T(8,128)S(1)}, s32[4,352]{1,0:T(4,128)S(1)}, s32[4,352]{1,0:T(4,128)S(1)}, bf16[64,8,64]{2,1,0:T(8,128)(2,1)S(1)}, /*index=5*/bf16[4,8,64,64]{3,2,1,0:T(8,128)(2,1)S(1)}, s32[]{:T(128)}) while((s32[]{:T(128)}, f32[32,512]{1,0:T(8,128)S(1)}, s32[4,352]{1,0:T(4,128)S(1)}, s32[4,352]{1,0:T(4,128)S(1)}, ...), condition=%wide.region_2.4_spmd, body=%wide.region_0.3_spmd.sunk | while | flops 23433312 | bytes 8079893 | solution.py:31
  15.7 2.7 %scatter_fusion = f32[32,512]{1,0:T(8,128)S(1)} fusion(f32[32,512]{1,0:T(8,128)S(1)} %get-tuple-element.368, s32[352]{0:T(512)S(1)} %get-tuple-element.334, f32[352,512]{1,0:T(8,128)S(1)} %reshape.229), kind=kCustom, calls=%fused_computation.4.clone.1 | custom fusion | flops 180224 | bytes 2164096 | tf_op jit(solution)/shard_map/while/body/eval_jaxpr/scatter-add | solution.py:23
  36.9 2.7 %scatter_fusion = f32[32,512]{1,0:T(8,128)S(1)} fusion(f32[32,512]{1,0:T(8,128)S(1)} %get-tuple-element.368, s32[352]{0:T(512)S(1)} %get-tuple-element.334, f32[352,512]{1,0:T(8,128)S(1)} %reshape.229), kind=kCustom, calls=%fused_computation.4.clone.1 | custom fusion | flops 180224 | bytes 2164096 | tf_op jit(solution)/shard_map/while/body/eval_jaxpr/scatter-add | solution.py:23
  42.4 9.0 %scatter_custom_fusion.4 = f32[32,64]{1,0:T(8,128)S(1)} fusion(s32[1408]{0:T(1024)S(1)} %reduce.9, f32[1408,64]{1,0:T(8,128)S(1)} %copy.38, f32[]{:T(128)} %constant.65.clone.1), kind=kCustom, calls=%fused_computation.63 | custom fusion | flops 90112 | bytes 8196 | tf_op jit(solution)/shard_map/scatter-add | solution.py:74
  52.6 20.5 %all-reduce = f32[32,64]{1,0:T(8,128)S(1)} all-reduce(f32[32,64]{1,0:T(8,128)S(1)} %scatter_custom_fusion.4), channel_id=3, replica_groups=mesh['parts'=2,'pix'=4,'ang'=2,'sl'=2] {'pix'}, use_global_device_ids=true, to_apply=%region_6.8.clone | all-reduce | flops 2048 | bytes 16384
  73.9 13.3 %all_gather.6 = bf16[32,512]{1,0:T(8,128)(2,1)S(1)} all-gather(bf16[8,512]{1,0:T(8,128)(2,1)S(1)} %fusion.21), channel_id=1, replica_groups=mesh['parts'=2,'pix'=4,'ang'=2,'sl'=2] {'pix'}, dimensions={0}, use_global_device_ids=true | all-gather | bytes 40960 | tf_op jit(solution)/shard_map/all_gather | solution.py:92
  87.3 28.3 %while.41 = (s32[]{:T(128)}, f32[64,512]{1,0:T(8,128)S(1)}, s32[4,352]{1,0:T(4,128)S(1)}, s32[4,352]{1,0:T(4,128)S(1)}, bf16[32,8,64]{2,1,0:T(8,128)(2,1)S(1)}, /*index=5*/bf16[4,8,64,64]{3,2,1,0:T(8,128)(2,1)S(1)}, s32[]{:T(128)}) while((s32[]{:T(128)}, f32[64,512]{1,0:T(8,128)S(1)}, s32[4,352]{1,0:T(4,128)S(1)}, s32[4,352]{1,0:T(4,128)S(1)}, ...), condition=%wide.region_9.12_spmd, body=%wide.region_7.0_spmd.sunk | while | flops 23433312 | bytes 8079893 | solution.py:53
  91.6 2.7 %scatter_fusion.1 = f32[64,512]{1,0:T(8,128)S(1)} fusion(f32[64,512]{1,0:T(8,128)S(1)} %get-tuple-element.389, s32[352]{0:T(512)S(1)} %get-tuple-element.342, f32[352,512]{1,0:T(8,128)S(1)} %reshape.234), kind=kCustom, calls=%fused_computation.5.clone.1 | custom fusion | flops 180224 | bytes 2164096 | tf_op jit(solution)/shard_map/while/body/eval_jaxpr/scatter-add | solution.py:45
  98.7 2.7 %scatter_fusion.1 = f32[64,512]{1,0:T(8,128)S(1)} fusion(f32[64,512]{1,0:T(8,128)S(1)} %get-tuple-element.389, s32[352]{0:T(512)S(1)} %get-tuple-element.342, f32[352,512]{1,0:T(8,128)S(1)} %reshape.234), kind=kCustom, calls=%fused_computation.5.clone.1 | custom fusion | flops 180224 | bytes 2164096 | tf_op jit(solution)/shard_map/while/body/eval_jaxpr/scatter-add | solution.py:45
  105.8 2.7 %scatter_fusion.1 = f32[64,512]{1,0:T(8,128)S(1)} fusion(f32[64,512]{1,0:T(8,128)S(1)} %get-tuple-element.389, s32[352]{0:T(512)S(1)} %get-tuple-element.342, f32[352,512]{1,0:T(8,128)S(1)} %reshape.234), kind=kCustom, calls=%fused_computation.5.clone.1 | custom fusion | flops 180224 | bytes 2164096 | tf_op jit(solution)/shard_map/while/body/eval_jaxpr/scatter-add | solution.py:45
  112.9 2.7 %scatter_fusion.1 = f32[64,512]{1,0:T(8,128)S(1)} fusion(f32[64,512]{1,0:T(8,128)S(1)} %get-tuple-element.389, s32[352]{0:T(512)S(1)} %get-tuple-element.342, f32[352,512]{1,0:T(8,128)S(1)} %reshape.234), kind=kCustom, calls=%fused_computation.5.clone.1 | custom fusion | flops 180224 | bytes 2164096 | tf_op jit(solution)/shard_map/while/body/eval_jaxpr/scatter-add | solution.py:45
  117.6 9.0 %scatter_custom_fusion.5 = f32[64,64]{1,0:T(8,128)S(1)} fusion(s32[1408]{0:T(1024)S(1)} %reduce.8, f32[1408,64]{1,0:T(8,128)S(1)} %copy.40, f32[]{:T(128)} %constant.65.clone.1), kind=kCustom, calls=%fused_computation.61 | custom fusion | flops 90112 | bytes 16388 | tf_op jit(solution)/shard_map/scatter-add | solution.py:75
  126.7 8.6 %psum.22 = f32[64,64]{1,0:T(8,128)S(1)} all-reduce(f32[64,64]{1,0:T(8,128)S(1)} %scatter_custom_fusion.5), channel_id=1, replica_groups=mesh['parts'=2,'pix'=4,'ang'=2,'sl'=2] {'ang'}, use_global_device_ids=true, to_apply=%region_13.16 | all-reduce | flops 4096 | bytes 32768 | tf_op jit(solution)/shard_map/psum | solution.py:77
  137.4 28.3 %while.42 = (s32[]{:T(128)}, f32[32,512]{1,0:T(8,128)S(1)}, s32[4,352]{1,0:T(4,128)S(1)}, s32[4,352]{1,0:T(4,128)S(1)}, bf16[64,8,64]{2,1,0:T(8,128)(2,1)S(1)}, /*index=5*/bf16[4,8,64,64]{3,2,1,0:T(8,128)(2,1)S(1)}, s32[]{:T(128)}) while((s32[]{:T(128)}, f32[32,512]{1,0:T(8,128)S(1)}, s32[4,352]{1,0:T(4,128)S(1)}, s32[4,352]{1,0:T(4,128)S(1)}, ...), condition=%wide.region_16.19_spmd, body=%wide.region_14.18_spmd.sunk | while | flops 23433312 | bytes 8079893 | solution.py:31
  141.7 2.7 %scatter_fusion.2 = f32[32,512]{1,0:T(8,128)S(1)} fusion(f32[32,512]{1,0:T(8,128)S(1)} %get-tuple-element.410, s32[352]{0:T(512)S(1)} %get-tuple-element.350, f32[352,512]{1,0:T(8,128)S(1)} %reshape.239), kind=kCustom, calls=%fused_computation.6.clone.1 | custom fusion | flops 180224 | bytes 2164096 | tf_op jit(solution)/shard_map/while/body/eval_jaxpr/scatter-add | solution.py:23
  148.8 2.7 %scatter_fusion.2 = f32[32,512]{1,0:T(8,128)S(1)} fusion(f32[32,512]{1,0:T(8,128)S(1)} %get-tuple-element.410, s32[352]{0:T(512)S(1)} %get-tuple-element.350, f32[352,512]{1,0:T(8,128)S(1)} %reshape.239), kind=kCustom, calls=%fused_computation.6.clone.1 | custom fusion | flops 180224 | bytes 2164096 | tf_op jit(solution)/shard_map/while/body/eval_jaxpr/scatter-add | solution.py:23
  166.4 19.1 %reduce-scatter.5.cloned.1.call-done = f32[8,512]{1,0:T(8,128)} async-done(((f32[32,512]{1,0:T(8,128)}), f32[8,512]{1,0:T(8,128)}) %reduce-scatter.5.cloned.1.call-update) | async-done | bytes 16400 | tf_op jit(solution)/shard_map/reduce_scatter | solution.py:89
  186.8 13.1 %all_gather.7 = bf16[32,512]{1,0:T(8,128)(2,1)S(1)} all-gather(bf16[8,512]{1,0:T(8,128)(2,1)S(1)} %get-tuple-element.195), channel_id=1, replica_groups=mesh['parts'=2,'pix'=4,'ang'=2,'sl'=2] {'pix'}, dimensions={0}, use_global_device_ids=true | all-gather | bytes 40960 | tf_op jit(solution)/shard_map/all_gather | solution.py:92
  200.1 28.3 %while.43 = (s32[]{:T(128)}, f32[64,512]{1,0:T(8,128)S(1)}, s32[4,352]{1,0:T(4,128)S(1)}, s32[4,352]{1,0:T(4,128)S(1)}, bf16[32,8,64]{2,1,0:T(8,128)(2,1)S(1)}, /*index=5*/bf16[4,8,64,64]{3,2,1,0:T(8,128)(2,1)S(1)}, s32[]{:T(128)}) while((s32[]{:T(128)}, f32[64,512]{1,0:T(8,128)S(1)}, s32[4,352]{1,0:T(4,128)S(1)}, s32[4,352]{1,0:T(4,128)S(1)}, ...), condition=%wide.region_20.23_spmd, body=%wide.region_18.22_spmd.sunk | while | flops 23433312 | bytes 8079893 | solution.py:53
  204.4 2.7 %scatter_fusion.3 = f32[64,512]{1,0:T(8,128)S(1)} fusion(f32[64,512]{1,0:T(8,128)S(1)} %get-tuple-element.431, s32[352]{0:T(512)S(1)} %get-tuple-element.358, f32[352,512]{1,0:T(8,128)S(1)} %reshape.244), kind=kCustom, calls=%fused_computation.7.clone.1 | custom fusion | flops 180224 | bytes 2164096 | tf_op jit(solution)/shard_map/while/body/eval_jaxpr/scatter-add | solution.py:45
  211.5 2.7 %scatter_fusion.3 = f32[64,512]{1,0:T(8,128)S(1)} fusion(f32[64,512]{1,0:T(8,128)S(1)} %get-tuple-element.431, s32[352]{0:T(512)S(1)} %get-tuple-element.358, f32[352,512]{1,0:T(8,128)S(1)} %reshape.244), kind=kCustom, calls=%fused_computation.7.clone.1 | custom fusion | flops 180224 | bytes 2164096 | tf_op jit(solution)/shard_map/while/body/eval_jaxpr/scatter-add | solution.py:45
  218.6 2.7 %scatter_fusion.3 = f32[64,512]{1,0:T(8,128)S(1)} fusion(f32[64,512]{1,0:T(8,128)S(1)} %get-tuple-element.431, s32[352]{0:T(512)S(1)} %get-tuple-element.358, f32[352,512]{1,0:T(8,128)S(1)} %reshape.244), kind=kCustom, calls=%fused_computation.7.clone.1 | custom fusion | flops 180224 | bytes 2164096 | tf_op jit(solution)/shard_map/while/body/eval_jaxpr/scatter-add | solution.py:45
  225.6 2.7 %scatter_fusion.3 = f32[64,512]{1,0:T(8,128)S(1)} fusion(f32[64,512]{1,0:T(8,128)S(1)} %get-tuple-element.431, s32[352]{0:T(512)S(1)} %get-tuple-element.358, f32[352,512]{1,0:T(8,128)S(1)} %reshape.244), kind=kCustom, calls=%fused_computation.7.clone.1 | custom fusion | flops 180224 | bytes 2164096 | tf_op jit(solution)/shard_map/while/body/eval_jaxpr/scatter-add | solution.py:45
  229.1 19.8 %all-reduce.6.cloned.1.call-done = f32[64,512]{1,0:T(8,128)} async-done(((f32[64,512]{1,0:T(8,128)}), f32[64,512]{1,0:T(8,128)}) %all-reduce.6.cloned.1.call-update) | async-done | bytes 131088 | tf_op jit(solution)/shard_map/psum | solution.py:94
  (210 shorter events, 96.0 us)
Async XLA Ops:
  7.2 66.0 %reduce-scatter.3.cloned.1.call-start = ((), (), s32[]{:S(2)}) async-start(), calls=%async_computation.2 | async-start | bytes 81920 | tf_op jit(solution)/shard_map/reduce_scatter | solution.py:85
  11.3 29.0 %copy-start.5 = (bf16[32,4096]{1,0:T(8,128)(2,1)S(1)}, bf16[32,4096]{1,0:T(8,128)(2,1)}, u32[]{:S(2)}) copy-start(bf16[32,4096]{1,0:T(8,128)(2,1)} %param.19) | copy-start | bytes 786436
  39.6 0.6 copy-start
  40.3 96.0 %all-reduce.4.cloned.1.call-start = ((), (), s32[]{:S(2)}) async-start(), calls=%async_computation.3 | async-start | bytes 262144 | tf_op jit(solution)/shard_map/psum | solution.py:94
  41.2 10.2 %copy-start.8 = (u32[32]{0:T(128)S(1)}, u32[32]{0:T(128)}, u32[]{:S(2)}) copy-start(u32[32]{0:T(128)} %constant.71) | copy-start | bytes 388
  41.6 31.6 %copy-start.7 = (f32[1,8,512]{2,1,0:T(8,128)S(1)}, f32[1,8,512]{2,1,0:T(8,128)}, u32[]{:S(2)}) copy-start(f32[1,8,512]{2,1,0:T(8,128)} %param.18) | copy-start | bytes 49156
  115.6 0.7 copy-start.3
  116.3 69.2 %reduce-scatter.5.cloned.1.call-start = ((), (), s32[]{:S(2)}) async-start(), calls=%async_computation.4 | async-start | bytes 81920 | tf_op jit(solution)/shard_map/reduce_scatter | solution.py:89
  116.8 19.5 %copy-start.4 = (f32[64,512]{1,0:T(8,128)S(1)}, f32[64,512]{1,0:T(8,128)}, u32[]{:S(2)}) copy-start(f32[64,512]{1,0:T(8,128)} %param.17) | copy-start | bytes 393220
  165.7 0.6 copy-start.1
  166.3 82.5 %all-reduce.6.cloned.1.call-start = ((), (), s32[]{:S(2)}) async-start(), calls=%async_computation.5 | async-start | bytes 262144 | tf_op jit(solution)/shard_map/psum | solution.py:94
  200.1 48.8 %copy-start.6 = (f32[64,512]{1,0:T(8,128)S(1)}, f32[64,512]{1,0:T(8,128)}, u32[]{:S(2)}) copy-start(f32[64,512]{1,0:T(8,128)} %all-reduce.4.cloned.1.call-done) | copy-start | bytes 393220
  228.4 0.7 copy-start.2
Sparse Core Ops, SparseCore 0:
  40.4 21.7 reduce-scatter.2
  116.4 19.7 all-reduce.3
  166.4 19.0 reduce-scatter.4
  229.2 19.5 all-reduce.5
where the time goes:
time: 257 us
  other arithmetic  88.3 us (34%)
  blocking collectives  55.5 us (22%)
  local copies, waits for them, and re-layouts  51.6 us (20%)
  waiting for transfers between devices  39.8 us (15%)
  between operations  14.6 us (6%)
  matrix products  5.68 us (2%)
    all_gather x2, blocking collectives, per_device(): row_table = lax.all_gather(scaled_low, 'pix', axis=0, tiled=True)  26.4 us
    scatter-add x8, other arithmetic, back_one_group(): return (running + jax.ops.segment_sum(images, pix_ids, tiles_dev), None)  21.9 us
    scatter-add x8, other arithmetic, project_one_group(): return (running + jax.ops.segment_sum(images, ray_ids, ray_total), None)  21.7 us
    psum x2, waiting for transfers between devices, per_device(): summed_update = lax.psum(back_sum, 'ang')  20.6 us
    unnamed x1, blocking collectives  20.5 us
    reduce_scatter x2, waiting for transfers between devices, per_device(): lax.psum_scatter(partial_rows, 'pix', scatter_dimension=0, tiled=True)  19.1 us
    gather x8, local copies, waits for them, and re-layouts, back_one_group(): jnp.take(table_tiles, row_ids, axis=0)  15.1 us
    gather x8, local copies, waits for them, and re-layouts, project_one_group(): jnp.take(low_tiles, pix_ids, axis=0)  15.1 us
  transfers between devices with their start and end apart: 4, of which 3 were waited for; matrix products, arithmetic and copies ran while one was open for 9% of the time, Pallas kernels for 0%

commit v1 on v0

--- a/solution.py
+++ b/solution.py
@@ -54,7 +54,7 @@
     return running
 
 
-def per_device(volume, sinogram, table, blk_ray, blk_pix):
+def per_device_base(volume, sinogram, table, blk_ray, blk_pix):
     pix_count = lax.axis_size("pix")
     tiles_dev = volume.shape[0]
     row_width = volume.shape[1]
@@ -96,9 +96,100 @@
     return (current, scaled[None])
 
 
+def split3(x):
+    hi = lax.reduce_precision(x, exponent_bits=8, mantissa_bits=7)
+    rest = x - hi
+    mid = lax.reduce_precision(rest, exponent_bits=8, mantissa_bits=7)
+    low = rest - mid
+    return (hi.astype(jnp.bfloat16), mid.astype(jnp.bfloat16), low.astype(jnp.bfloat16))
+
+
+def per_device_split(volume, sinogram, table, blk_ray, blk_pix, n_pix, n_ang):
+    n_grp = n_pix * n_ang
+    tiles_dev = volume.shape[0]
+    slices = volume.shape[1] // TILE
+    per_dev = slices // n_grp
+    rays_dev = sinogram.shape[1]
+    nbd = blk_ray.shape[-1]
+    ray_total = rays_dev * n_pix
+    pix_total = tiles_dev * n_pix
+    width = per_dev * TILE
+
+    vol_send = volume.reshape(tiles_dev, n_grp, width).transpose(1, 0, 2)
+    sino_send = sinogram[0].reshape(rays_dev, n_grp, width).transpose(1, 0, 2)
+    lists = jnp.stack([blk_ray.reshape(-1), blk_pix.reshape(-1)]).astype(jnp.float32)
+    list_rows = (2 * nbd + width - 1) // width
+    lists = jnp.pad(lists.reshape(-1), (0, list_rows * width - 2 * nbd)).reshape(list_rows, width)
+    list_send = jnp.broadcast_to(lists[None], (n_grp, list_rows, width))
+    send = jnp.concatenate([vol_send, sino_send, list_send], axis=1)
+    recv = lax.all_to_all(send, ("pix", "ang"), 0, 0, tiled=False)
+    recv = recv.reshape(n_pix, n_ang, tiles_dev + rays_dev + list_rows, width)
+
+    current = recv[:, 0, :tiles_dev].reshape(pix_total, width)
+    measured = recv[:, :, tiles_dev:tiles_dev + rays_dev].transpose(1, 0, 2, 3).reshape(n_ang, ray_total, width)
+    got = recv[:, :, tiles_dev + rays_dev:].reshape(n_pix, n_ang, -1)[:, :, :2 * nbd]
+    got = got.reshape(n_pix, n_ang, 2, nbd).transpose(2, 1, 0, 3).astype(jnp.int32)
+    ray_ids = got[0].reshape(n_ang, n_pix, KINDS, nbd // KINDS)
+    pix_ids = got[1].reshape(n_ang, n_pix, KINDS, nbd // KINDS)
+
+    one_ray = (ray_ids[..., None] == jnp.arange(ray_total, dtype=jnp.int32)).astype(jnp.bfloat16)
+    one_pix = (pix_ids[..., None] == jnp.arange(tiles_dev, dtype=jnp.int32)).astype(jnp.bfloat16)
+    counts = jnp.einsum("gpkbv,gpkbu->gkvpu", one_ray, one_pix, preferred_element_type=jnp.float32)
+    counts = counts.reshape(n_ang, KINDS, ray_total, pix_total)
+    count_low = counts.astype(jnp.bfloat16)
+    ray_count = jnp.sum(counts, axis=3)
+    pix_count = jnp.sum(counts, axis=2)
+
+    pattern = table.reshape(KINDS, TILE, TILE)
+    pattern_wide = pattern.astype(jnp.float32)
+    hi = lax.Precision.HIGHEST
+    ray_weight = jnp.einsum("gkv,ki->gvi", ray_count, jnp.sum(pattern_wide, axis=2), precision=hi)
+    pixel_weight = jnp.einsum("gku,kj->uj", pix_count, jnp.sum(pattern_wide, axis=1), precision=hi)
+    ray_weight = jnp.tile(ray_weight, (1, 1, per_dev))
+    pixel_weight = jnp.tile(pixel_weight, (1, per_dev))
+
+    cur = current.reshape(pix_total, per_dev, TILE)
+    meas = measured.reshape(n_ang, ray_total, per_dev, TILE)
+    rw = ray_weight.reshape(n_ang, ray_total, per_dev, TILE)
+    pw = pixel_weight.reshape(pix_total, per_dev, TILE)
+    scaled = meas
+    for iteration in range(ITERS):
+        low = cur.astype(jnp.bfloat16)
+        gathered = jnp.einsum("gkvu,usj->gkvsj", count_low, low, preferred_element_type=jnp.float32)
+        proj = sum(
+            jnp.einsum("gkvsj,kij->gvsi", part, pattern, preferred_element_type=jnp.float32)
+            for part in split3(gathered)
+        )
+        scaled = (meas - proj) / rw
+        scaled_low = scaled.astype(jnp.bfloat16)
+        spread = jnp.einsum("gvsi,kij->gkvsj", scaled_low, pattern, preferred_element_type=jnp.float32)
+        update = sum(
+            jnp.einsum("gkvu,gkvsj->usj", count_low, part, preferred_element_type=jnp.float32)
+            for part in split3(spread)
+        )
+        cur = cur + update / pw
+
+    vol_back = cur.reshape(n_pix, tiles_dev, width)
+    vol_back = jnp.broadcast_to(vol_back[:, None], (n_pix, n_ang, tiles_dev, width))
+    res_back = scaled.reshape(n_ang, n_pix, rays_dev, width).transpose(1, 0, 2, 3)
+    back = jnp.concatenate([vol_back, res_back], axis=2).reshape(n_grp, tiles_dev + rays_dev, width)
+    got_back = lax.all_to_all(back, ("pix", "ang"), 0, 0, tiled=False)
+    vol_out = got_back[:, :tiles_dev].transpose(1, 0, 2).reshape(tiles_dev, slices * TILE)
+    res_out = got_back[:, tiles_dev:].transpose(1, 0, 2).reshape(1, rays_dev, slices * TILE)
+    return (vol_out, res_out)
+
+
 def solution(mesh):
+    n_pix = mesh.shape["pix"]
+    n_ang = mesh.shape["ang"]
+
+    def body(volume, sinogram, table, blk_ray, blk_pix):
+        if (volume.shape[1] // TILE) % (n_pix * n_ang) == 0:
+            return per_device_split(volume, sinogram, table, blk_ray, blk_pix, n_pix, n_ang)
+        return per_device_base(volume, sinogram, table, blk_ray, blk_pix)
+
     return jax.shard_map(
-        per_device,
+        body,
         mesh=mesh,
         in_specs=(
             P(("parts", "pix"), "sl"),

time: 257 us -> 54.7 us (0.21)
  other arithmetic: 88.3 us -> 2.28 us
  blocking collectives: 55.5 us -> 11.9 us
  local copies, waits for them, and re-layouts: 51.6 us -> 13.5 us
  waiting for transfers between devices: 39.8 us -> 7.47 us
  between operations: 14.6 us -> 0.95 us
  starting transfers between devices: 0.16 us -> 7.25 us
  matrix products: 5.68 us -> 10.9 us
    scatter-add x18 -> x0, other arithmetic: 61.6 us -> none  [the longest x8 21.9 us: back_one_group(): return (running + jax.ops.segment_sum(images, pix_ids, tiles_dev), None)]
    gather x16 -> x0, local copies, waits for them, and re-layouts: 30.1 us -> none  [the longest x8 15.1 us: back_one_group(): jnp.take(table_tiles, row_ids, axis=0)]
    all_gather x2 -> x0, blocking collectives: 26.4 us -> none  [per_device(): row_table = lax.all_gather(scaled_low, 'pix', axis=0, tiled=True)]
    psum x2 -> x0, waiting for transfers between devices: 20.6 us -> none  [per_device(): summed_update = lax.psum(back_sum, 'ang')]
    unnamed x1 -> x0, blocking collectives: 20.5 us -> none
    select_n x32 -> x0, other arithmetic: 19.2 us -> none  [the longest x16 9.6 us: back_one_group(): jnp.take(table_tiles, row_ids, axis=0)]
    reduce_scatter x2 -> x0, waiting for transfers between devices: 19.1 us -> none  [per_device(): lax.psum_scatter(partial_rows, 'pix', scatter_dimension=0, tiled=True)]
    all_to_all x0 -> x1, blocking collectives: none -> 11.9 us  [per_device_split(): got_back = lax.all_to_all(back, ('pix', 'ang'), 0, 0, tiled=False)]
  transfers between devices with their start and end apart: 4 -> 1, of which waited for: 3 -> 1; matrix products, arithmetic and copies ran while one was open for 9% -> 3% of each run, Pallas kernels for 0% -> 0%
where the time goes in v1:
time: 54.7 us; the launch traced here: 54.2 us
  local copies, waits for them, and re-layouts  13.5 us (25%)
  blocking collectives  11.9 us (22%)
  matrix products  10.9 us (20%)
  waiting for transfers between devices  7.47 us (14%)
  starting transfers between devices  7.25 us (13%)
  other arithmetic  2.28 us (4%)
  between operations  0.95 us (2%)
    all_to_all x1, blocking collectives, per_device_split(): got_back = lax.all_to_all(back, ('pix', 'ang'), 0, 0, tiled=False)  11.9 us
    all_to_all x1, waiting for transfers between devices, per_device_split(): recv = lax.all_to_all(send, ('pix', 'ang'), 0, 0, tiled=False)  7.47 us
    all_to_all x1, starting transfers between devices, per_device_split(): recv = lax.all_to_all(send, ('pix', 'ang'), 0, 0, tiled=False)  7.25 us
    convert_element_type x2, local copies, waits for them, and re-layouts, per_device_split(): count_low = counts.astype(jnp.bfloat16)  5.91 us
    dot_general x1, matrix products, per_device_split(): jnp.einsum('gpkbv,gpkbu->gkvpu', one_ray, one_pix, preferred_element_type...  4.06 us
    unnamed x8, local copies, waits for them, and re-layouts  4.04 us
    dot_general x2, matrix products, per_device_split(): jnp.einsum('gvsi,kij->gkvsj', scaled_low, pattern, preferred_element_type...  2.05 us
    dot_general x6, matrix products, per_device_split(): jnp.einsum('gkvu,gkvsj->usj', count_low, part, preferred_element_type=jnp...  1.97 us
  transfers between devices with their start and end apart: 1, of which 1 were waited for; matrix products, arithmetic and copies ran while one was open for 3% of the time, Pallas kernels for 0%

profile of v1, /device:TPU:0, one launch (start us, length us, event | category | flops | bytes accessed | tf_op | source)
XLA Modules:
  0.0 54.2 jit_solution(15400631715420090016)
XLA Ops:
  0.6 0.8 %add_convert_fusion = f32[2,1408]{1,0:T(2,128)S(1)} fusion(s32[1,1408]{1,0:T(1,128)} %bitcast.207, s32[1,1408]{1,0:T(1,128)} %bitcast.208), kind=kLoop, calls=%fused_computation.84 | loop fusion | flops 5632 | bytes 22528 | tf_op jit(solution)/shard_map/convert_element_type | solution.py:120
  1.6 1.0 %copy.37 = f32[64,512]{0,1:T(8,128)S(1)} copy(f32[64,512]{1,0:T(8,128)} %param.5) | data formatting | bytes 262144 | tf_op args[0]
  2.6 0.8 %copy.38 = f32[1,8,512]{1,2,0:T(8,128)S(1)} copy(f32[1,8,512]{2,1,0:T(8,128)} %param.6) | data formatting | bytes 32768 | tf_op args[1]
  3.5 0.9 %pad_maximum_fusion = f32[8,116,64]{1,2,0:T(8,128)} fusion(f32[8,44,64]{1,2,0:T(8,128)S(1)} %broadcast_in_dim.6, f32[8,8,64]{1,2,0:T(8,128)S(1)} %bitcast.204, f32[8,64,64]{1,2,0:T(8,128)S(1)} %bitcast.203), kind=kLoop, calls=%fused_computation.70 | loop fusion | flops 118784 | bytes 475136 | tf_op jit(solution)/shard_map/concatenate | solution.py:124
  4.4 7.3 %all-to-all-start = ((f32[8,116,64]{1,2,0:T(8,128)}), f32[8,116,64]{1,2,0:T(8,128)S(1)}, u32[]{:S(2)}, u32[]{:S(2)}) async-start(f32[8,116,64]{1,2,0:T(8,128)} %pad_maximum_fusion), calls=%async_computation | async-start | bytes 524288 | tf_op jit(solution)/shard_map/all_to_all | solution.py:125
  11.7 0.5 reshape.157
  12.2 0.5 reshape.145
  12.7 0.3 convert_reduce_fusion
  13.1 7.5 %all-to-all-done = f32[8,116,64]{1,2,0:T(8,128)S(1)} async-done(((f32[8,116,64]{1,2,0:T(8,128)}), f32[8,116,64]{1,2,0:T(8,128)S(1)}, u32[]{:S(2)}, u32[]{:S(2)}) %all-to-all-start) | async-done | bytes 237600 | tf_op jit(solution)/shard_map/all_to_all | solution.py:125
  21.9 4.1 %bitcast_reduce_fusion = (f32[32,4,64]{2,1,0:T(4,128)S(1)}, f32[2,32,32]{2,1,0:T(8,128)S(1)}, bf16[2,32,4,64,32]{3,4,2,1,0:T(8,128)(2,1)S(1)}) fusion(s32[2,4,32,44]{3,1,2,0:T(4,128)S(1)} %copy.45, s32[2,4,32,44]{3,1,2,0:T(4,128)S(1)} %copy.43), kind=kOutput, calls=%fused_computation.2 | convolution fusion | flops 48781312 | bytes 1179648 | tf_op jit(solution)/shard_map/gpkbv,gpkbu->gkvpu/dot_general | solution.py:137
  25.9 2.4 %copy.46 = bf16[2,32,32,4,64]{4,3,2,1,0:T(4,128)(2,1)} copy(bf16[2,32,32,4,64]{4,2,3,1,0:T(8,128)(2,1)S(1)} %bitcast.200) | data formatting | bytes 2097152 | tf_op jit(solution)/shard_map/convert_element_type | solution.py:139
  28.4 3.5 %convert_element_type.106 = bf16[2,32,32,256]{3,2,1,0:T(8,128)(2,1)S(1)} reshape(bf16[2,32,32,4,64]{4,3,2,1,0:T(4,128)(2,1)} %copy.46) | data formatting | bytes 2097152 | tf_op jit(solution)/shard_map/convert_element_type | solution.py:139
  32.0 0.4 fusion.41
  32.7 0.7 %copy-done = f32[2,32,32,64]{3,2,1,0:T(8,128)} copy-done((f32[2,32,32,64]{3,2,1,0:T(8,128)}, f32[2,32,32,64]{3,2,1,0:T(8,128)S(1)}, u32[]{:S(2)}) %copy-start) | copy-done | bytes 524312
  34.2 1.8 %convolution_bitcast_fusion.1 = f32[2,32,32,1,64]{4,2,1,0,3:T(8,128)S(1)} fusion(bf16[32,64,64,1]{2,1,0,3:T(8,128)(2,1)S(1)} %reshape.157, f32[2,32,64]{2,1,0:T(8,128)S(1)} %fusion.46, f32[2,32,64]{2,1,0:T(8,128)S(1)} %convolution_bitcast_fusion.11, f32[2,32,64]{2,1,0:T(8,128)S(1)} %convolution_bitcast_fusion.12, f32[2,32,32,64]{3,2,1,0:T(8,128)} %copy-done, ...), kind=kOutput, calls=%fused_computation.25 | convolution fusion | flops 33837056 | bytes 1376256 | tf_op jit(solution)/shard_map/gvsi,kij->gkvsj/dot_general | solution.py:165
  36.0 0.3 convolution_bitcast_fusion.6
  36.3 0.3 convolution_bitcast_fusion.5
  37.3 0.3 fusion.6
  37.6 0.4 fusion.39
  39.6 0.3 convolution_bitcast_fusion.2
  39.9 0.3 fusion.10
  40.7 11.9 %all_to_all.10 = f32[8,72,64]{1,2,0:T(8,128)S(1)} all-to-all(f32[8,72,64]{1,2,0:T(8,128)S(1)} %bitcast.201), channel_id=1, replica_groups=mesh['parts'=2,'pix'=4,'ang'=2,'sl'=2] {'pix','ang'}, dimensions={0} | all-to-all | bytes 294912 | tf_op jit(solution)/shard_map/all_to_all | solution.py:176
  52.8 0.7 %copy.53 = f32[1,8,512]{2,1,0:T(8,128)} copy(f32[1,8,512]{1,2,0:T(8,128)S(1)} %bitcast.202) | data formatting | bytes 32768
  53.5 0.8 %copy.52 = f32[64,512]{1,0:T(8,128)} copy(f32[64,512]{0,1:T(8,128)S(1)} %bitcast.199) | data formatting | bytes 262144
  (38 shorter events, 5.3 us)
Async XLA Ops:
  0.6 11.0 %copy-start.1 = (bf16[32,4096]{1,0:T(8,128)(2,1)S(1)}, bf16[32,4096]{1,0:T(8,128)(2,1)}, u32[]{:S(2)}) copy-start(bf16[32,4096]{1,0:T(8,128)(2,1)} %param.7) | copy-start | bytes 786436
  4.4 16.2 %all-to-all-start = ((f32[8,116,64]{1,2,0:T(8,128)}), f32[8,116,64]{1,2,0:T(8,128)S(1)}, u32[]{:S(2)}, u32[]{:S(2)}) async-start(f32[8,116,64]{1,2,0:T(8,128)} %pad_maximum_fusion), calls=%async_computation | async-start | bytes 524288 | tf_op jit(solution)/shard_map/all_to_all | solution.py:125
  32.4 1.0 %copy-start = (f32[2,32,32,64]{3,2,1,0:T(8,128)}, f32[2,32,32,64]{3,2,1,0:T(8,128)S(1)}, u32[]{:S(2)}) copy-start(f32[2,32,32,64]{3,2,1,0:T(8,128)S(1)} %fusion.41) | copy-start | bytes 1572868

commit v2 on v1

--- a/solution.py
+++ b/solution.py
@@ -129,16 +129,20 @@
     measured = recv[:, :, tiles_dev:tiles_dev + rays_dev].transpose(1, 0, 2, 3).reshape(n_ang, ray_total, width)
     got = recv[:, :, tiles_dev + rays_dev:].reshape(n_pix, n_ang, -1)[:, :, :2 * nbd]
     got = got.reshape(n_pix, n_ang, 2, nbd).transpose(2, 1, 0, 3).astype(jnp.int32)
-    ray_ids = got[0].reshape(n_ang, n_pix, KINDS, nbd // KINDS)
-    pix_ids = got[1].reshape(n_ang, n_pix, KINDS, nbd // KINDS)
+    per_kind = nbd // KINDS
+    offsets = (jnp.arange(n_pix, dtype=jnp.int32) * tiles_dev)[None, :, None, None]
+    ray_ids = got[0].reshape(n_ang, n_pix, KINDS, per_kind)
+    pix_ids = got[1].reshape(n_ang, n_pix, KINDS, per_kind) + offsets
+    ray_ids = ray_ids.transpose(0, 2, 1, 3).reshape(n_ang, KINDS, n_pix * per_kind)
+    pix_ids = pix_ids.transpose(0, 2, 1, 3).reshape(n_ang, KINDS, n_pix * per_kind)
 
     one_ray = (ray_ids[..., None] == jnp.arange(ray_total, dtype=jnp.int32)).astype(jnp.bfloat16)
-    one_pix = (pix_ids[..., None] == jnp.arange(tiles_dev, dtype=jnp.int32)).astype(jnp.bfloat16)
-    counts = jnp.einsum("gpkbv,gpkbu->gkvpu", one_ray, one_pix, preferred_element_type=jnp.float32)
-    counts = counts.reshape(n_ang, KINDS, ray_total, pix_total)
-    count_low = counts.astype(jnp.bfloat16)
-    ray_count = jnp.sum(counts, axis=3)
-    pix_count = jnp.sum(counts, axis=2)
+    one_pix = (pix_ids[..., None] == jnp.arange(pix_total, dtype=jnp.int32)).astype(jnp.bfloat16)
+    count_low = jnp.einsum(
+        "gkbv,gkbu->gkvu", one_ray, one_pix, preferred_element_type=jnp.float32
+    ).astype(jnp.bfloat16)
+    ray_count = jnp.sum(one_ray.astype(jnp.float32), axis=2)
+    pix_count = jnp.sum(one_pix.astype(jnp.float32), axis=2)
 
     pattern = table.reshape(KINDS, TILE, TILE)
     pattern_wide = pattern.astype(jnp.float32)

time: 54.7 us -> 50.6 us (0.925)
  local copies, waits for them, and re-layouts: 13.5 us -> 7.37 us
  other arithmetic: 2.28 us -> 4.83 us
  matrix products: 10.9 us -> 10.3 us
    convert_element_type x4 -> x0, local copies, waits for them, and re-layouts: 6.08 us -> none  [the longest x2 5.91 us: per_device_split(): count_low = counts.astype(jnp.bfloat16)]
    reduce_sum x0 -> x2, other arithmetic: none -> 2.5 us  [the longest x1 2.15 us: per_device_split(): jnp.einsum('gku,kj->uj', pix_count, jnp.sum(pattern_wide, axis=1), precis...]
where the time goes in v2:
time: 50.6 us; the launch traced here: 50.2 us
  blocking collectives  12 us (24%)
  matrix products  10.3 us (20%)
  waiting for transfers between devices  7.46 us (15%)
  local copies, waits for them, and re-layouts  7.37 us (15%)
  starting transfers between devices  7.25 us (14%)
  other arithmetic  4.83 us (10%)
  between operations  0.98 us (2%)
    all_to_all x1, blocking collectives, per_device_split(): got_back = lax.all_to_all(back, ('pix', 'ang'), 0, 0, tiled=False)  12 us
    all_to_all x1, waiting for transfers between devices, per_device_split(): recv = lax.all_to_all(send, ('pix', 'ang'), 0, 0, tiled=False)  7.46 us
    all_to_all x1, starting transfers between devices, per_device_split(): recv = lax.all_to_all(send, ('pix', 'ang'), 0, 0, tiled=False)  7.25 us
    unnamed x8, local copies, waits for them, and re-layouts  4.09 us
    dot_general x1, matrix products, per_device_split(): jnp.einsum('gkbv,gkbu->gkvu', one_ray, one_pix, preferred_element_type=jn...  3.53 us
    reduce_sum x1, other arithmetic, per_device_split(): jnp.einsum('gku,kj->uj', pix_count, jnp.sum(pattern_wide, axis=1), precis...  2.15 us
    dot_general x2, matrix products, per_device_split(): jnp.einsum('gvsi,kij->gkvsj', scaled_low, pattern, preferred_element_type...  2.05 us
    dot_general x6, matrix products, per_device_split(): jnp.einsum('gkvu,gkvsj->usj', count_low, part, preferred_element_type=jnp...  1.98 us
  transfers between devices with their start and end apart: 1, of which 1 were waited for; matrix products, arithmetic and copies ran while one was open for 3% of the time, Pallas kernels for 0%

profile of v2, /device:TPU:0, one launch (start us, length us, event | category | flops | bytes accessed | tf_op | source)
XLA Modules:
  0.0 50.2 jit_solution(18394242003228991955)
XLA Ops:
  0.6 0.7 %add_convert_fusion = f32[2,1408]{1,0:T(2,128)S(1)} fusion(s32[1,1408]{1,0:T(1,128)} %bitcast.200, s32[1,1408]{1,0:T(1,128)} %bitcast.201), kind=kLoop, calls=%fused_computation.86 | loop fusion | flops 5632 | bytes 22528 | tf_op jit(solution)/shard_map/convert_element_type | solution.py:120
  1.5 1.0 %copy.31 = f32[64,512]{0,1:T(8,128)S(1)} copy(f32[64,512]{1,0:T(8,128)} %param.5) | data formatting | bytes 262144 | tf_op args[0]
  2.6 0.9 %copy.32 = f32[1,8,512]{1,2,0:T(8,128)S(1)} copy(f32[1,8,512]{2,1,0:T(8,128)} %param.6) | data formatting | bytes 32768 | tf_op args[1]
  3.5 0.9 %pad_maximum_fusion = f32[8,116,64]{1,2,0:T(8,128)} fusion(f32[8,44,64]{1,2,0:T(8,128)S(1)} %broadcast_in_dim.6, f32[8,8,64]{1,2,0:T(8,128)S(1)} %bitcast.196, f32[8,64,64]{1,2,0:T(8,128)S(1)} %bitcast.195), kind=kLoop, calls=%fused_computation.72 | loop fusion | flops 118784 | bytes 475136 | tf_op jit(solution)/shard_map/concatenate | solution.py:124
  4.4 7.3 %all-to-all-start = ((f32[8,116,64]{1,2,0:T(8,128)}), f32[8,116,64]{1,2,0:T(8,128)S(1)}, u32[]{:S(2)}, u32[]{:S(2)}) async-start(f32[8,116,64]{1,2,0:T(8,128)} %pad_maximum_fusion), calls=%async_computation | async-start | bytes 524288 | tf_op jit(solution)/shard_map/all_to_all | solution.py:125
  11.7 0.5 %reshape.150 = bf16[32,64,64,1]{2,1,0,3:T(8,128)(2,1)S(1)} reshape(bf16[32,4096]{1,0:T(8,128)(2,1)S(1)} %copy-done.1) | data formatting | bytes 524288 | tf_op jit(solution)/shard_map/reshape | solution.py:147
  12.2 0.5 %reshape.138 = bf16[32,64,64]{2,1,0:T(8,128)(2,1)S(1)} reshape(bf16[32,4096]{1,0:T(8,128)(2,1)S(1)} %copy-done.1) | data formatting | bytes 524288 | tf_op jit(solution)/shard_map/reshape | solution.py:147
  12.8 0.3 convert_reduce_fusion.2
  13.1 7.5 %all-to-all-done = f32[8,116,64]{1,2,0:T(8,128)S(1)} async-done(((f32[8,116,64]{1,2,0:T(8,128)}), f32[8,116,64]{1,2,0:T(8,128)S(1)}, u32[]{:S(2)}, u32[]{:S(2)}) %all-to-all-start) | async-done | bytes 237600 | tf_op jit(solution)/shard_map/all_to_all | solution.py:125
  21.7 0.3 convert_reduce_fusion.1
  22.5 2.2 %convert_reduce_fusion = f32[32,256]{1,0:T(8,128)S(1)} fusion(s32[2,32,176]{2,1,0:T(8,128)S(1)} %eq.34), kind=kLoop, calls=%fused_computation | loop fusion | flops 11526144 | bytes 77824 | tf_op jit(solution)/shard_map/gku,kj->uj/reduce_sum | solution.py:151
  24.7 3.5 %fusion.4 = bf16[2,32,32,256]{3,2,1,0:T(8,128)(2,1)S(1)} fusion(s32[2,32,176]{2,1,0:T(8,128)S(1)} %eq.34, s32[2,32,176]{2,1,0:T(8,128)S(1)} %eq.30), kind=kOutput, calls=%fused_computation.24 | convolution fusion | flops 188317696 | bytes 1138688 | tf_op jit(solution)/shard_map/gkbv,gkbu->gkvu/dot_general | solution.py:141
  28.5 0.4 fusion.44
  29.2 0.7 %copy-done = f32[2,32,32,64]{3,2,1,0:T(8,128)} copy-done((f32[2,32,32,64]{3,2,1,0:T(8,128)}, f32[2,32,32,64]{3,2,1,0:T(8,128)S(1)}, u32[]{:S(2)}) %copy-start) | copy-done | bytes 524312
  30.5 1.8 %convolution_bitcast_fusion.1 = f32[2,32,32,1,64]{4,2,1,0,3:T(8,128)S(1)} fusion(bf16[32,64,64,1]{2,1,0,3:T(8,128)(2,1)S(1)} %reshape.150, f32[2,32,64]{2,1,0:T(8,128)S(1)} %fusion.50, f32[2,32,64]{2,1,0:T(8,128)S(1)} %convolution_bitcast_fusion.11, f32[2,32,64]{2,1,0:T(8,128)S(1)} %convolution_bitcast_fusion.12, f32[2,32,32,64]{3,2,1,0:T(8,128)} %copy-done, ...), kind=kOutput, calls=%fused_computation.26 | convolution fusion | flops 33837056 | bytes 1376256 | tf_op jit(solution)/shard_map/gvsi,kij->gkvsj/dot_general | solution.py:169
  32.3 0.3 convolution_bitcast_fusion.5
  33.2 0.3 fusion.8
  33.6 0.4 fusion.42
  35.2 0.3 convolution_bitcast_fusion.2
  35.5 0.3 convolution_bitcast_fusion.3
  36.0 0.3 fusion.12
  36.6 12.0 %all_to_all.10 = f32[8,72,64]{1,2,0:T(8,128)S(1)} all-to-all(f32[8,72,64]{1,2,0:T(8,128)S(1)} %bitcast.193), channel_id=1, replica_groups=mesh['parts'=2,'pix'=4,'ang'=2,'sl'=2] {'pix','ang'}, dimensions={0} | all-to-all | bytes 294912 | tf_op jit(solution)/shard_map/all_to_all | solution.py:180
  48.6 0.8 %copy.44 = f32[64,512]{1,0:T(8,128)} copy(f32[64,512]{0,1:T(8,128)S(1)} %bitcast.192) | data formatting | bytes 262144
  49.5 0.7 %copy.45 = f32[1,8,512]{2,1,0:T(8,128)} copy(f32[1,8,512]{1,2,0:T(8,128)S(1)} %bitcast.194) | data formatting | bytes 32768
  (40 shorter events, 5.1 us)
Async XLA Ops:
  2.6 9.1 %copy-start.1 = (bf16[32,4096]{1,0:T(8,128)(2,1)S(1)}, bf16[32,4096]{1,0:T(8,128)(2,1)}, u32[]{:S(2)}) copy-start(bf16[32,4096]{1,0:T(8,128)(2,1)} %param.7) | copy-start | bytes 786436
  4.4 16.2 %all-to-all-start = ((f32[8,116,64]{1,2,0:T(8,128)}), f32[8,116,64]{1,2,0:T(8,128)S(1)}, u32[]{:S(2)}, u32[]{:S(2)}) async-start(f32[8,116,64]{1,2,0:T(8,128)} %pad_maximum_fusion), calls=%async_computation | async-start | bytes 524288 | tf_op jit(solution)/shard_map/all_to_all | solution.py:125
  28.9 1.0 %copy-start = (f32[2,32,32,64]{3,2,1,0:T(8,128)}, f32[2,32,32,64]{3,2,1,0:T(8,128)S(1)}, u32[]{:S(2)}) copy-start(f32[2,32,32,64]{3,2,1,0:T(8,128)S(1)} %fusion.44) | copy-start | bytes 1572868

commit v3 on v2

--- a/solution.py
+++ b/solution.py
@@ -100,8 +100,7 @@
     hi = lax.reduce_precision(x, exponent_bits=8, mantissa_bits=7)
     rest = x - hi
     mid = lax.reduce_precision(rest, exponent_bits=8, mantissa_bits=7)
-    low = rest - mid
-    return (hi.astype(jnp.bfloat16), mid.astype(jnp.bfloat16), low.astype(jnp.bfloat16))
+    return jnp.stack([hi, mid, rest - mid]).astype(jnp.bfloat16)
 
 
 def per_device_split(volume, sinogram, table, blk_ray, blk_pix, n_pix, n_ang):
@@ -114,72 +113,79 @@
     ray_total = rays_dev * n_pix
     pix_total = tiles_dev * n_pix
     width = per_dev * TILE
-
-    vol_send = volume.reshape(tiles_dev, n_grp, width).transpose(1, 0, 2)
-    sino_send = sinogram[0].reshape(rays_dev, n_grp, width).transpose(1, 0, 2)
+    per_kind = nbd // KINDS
+
     lists = jnp.stack([blk_ray.reshape(-1), blk_pix.reshape(-1)]).astype(jnp.float32)
     list_rows = (2 * nbd + width - 1) // width
-    lists = jnp.pad(lists.reshape(-1), (0, list_rows * width - 2 * nbd)).reshape(list_rows, width)
-    list_send = jnp.broadcast_to(lists[None], (n_grp, list_rows, width))
-    send = jnp.concatenate([vol_send, sino_send, list_send], axis=1)
-    recv = lax.all_to_all(send, ("pix", "ang"), 0, 0, tiled=False)
-    recv = recv.reshape(n_pix, n_ang, tiles_dev + rays_dev + list_rows, width)
-
-    current = recv[:, 0, :tiles_dev].reshape(pix_total, width)
-    measured = recv[:, :, tiles_dev:tiles_dev + rays_dev].transpose(1, 0, 2, 3).reshape(n_ang, ray_total, width)
-    got = recv[:, :, tiles_dev + rays_dev:].reshape(n_pix, n_ang, -1)[:, :, :2 * nbd]
-    got = got.reshape(n_pix, n_ang, 2, nbd).transpose(2, 1, 0, 3).astype(jnp.int32)
-    per_kind = nbd // KINDS
+    lists = jnp.pad(lists.reshape(-1), (0, list_rows * width - 2 * nbd)).reshape(list_rows, 1, width)
+    send = jnp.concatenate(
+        [
+            volume.reshape(tiles_dev, n_grp, width),
+            sinogram[0].reshape(rays_dev, n_grp, width),
+            jnp.broadcast_to(lists, (list_rows, n_grp, width)),
+        ],
+        axis=0,
+    )
+    recv = lax.all_to_all(send, ("pix", "ang"), 1, 1, tiled=False)
+    recv = recv.reshape(tiles_dev + rays_dev + list_rows, n_pix, n_ang, width)
+
+    current = recv[:tiles_dev, :, 0].transpose(1, 0, 2).reshape(pix_total, width)
+    measured = recv[tiles_dev:tiles_dev + rays_dev].transpose(2, 1, 0, 3).reshape(n_ang * ray_total, width)
+    got = recv[tiles_dev + rays_dev:].transpose(2, 1, 0, 3).reshape(n_ang, n_pix, list_rows * width)
+    got = got[:, :, :2 * nbd].reshape(n_ang, n_pix, 2, KINDS, per_kind).astype(jnp.int32)
     offsets = (jnp.arange(n_pix, dtype=jnp.int32) * tiles_dev)[None, :, None, None]
-    ray_ids = got[0].reshape(n_ang, n_pix, KINDS, per_kind)
-    pix_ids = got[1].reshape(n_ang, n_pix, KINDS, per_kind) + offsets
-    ray_ids = ray_ids.transpose(0, 2, 1, 3).reshape(n_ang, KINDS, n_pix * per_kind)
-    pix_ids = pix_ids.transpose(0, 2, 1, 3).reshape(n_ang, KINDS, n_pix * per_kind)
+    ray_ids = got[:, :, 0].transpose(0, 2, 1, 3).reshape(n_ang, KINDS, n_pix * per_kind)
+    pix_ids = (got[:, :, 1] + offsets).transpose(0, 2, 1, 3).reshape(n_ang, KINDS, n_pix * per_kind)
 
     one_ray = (ray_ids[..., None] == jnp.arange(ray_total, dtype=jnp.int32)).astype(jnp.bfloat16)
     one_pix = (pix_ids[..., None] == jnp.arange(pix_total, dtype=jnp.int32)).astype(jnp.bfloat16)
     count_low = jnp.einsum(
         "gkbv,gkbu->gkvu", one_ray, one_pix, preferred_element_type=jnp.float32
     ).astype(jnp.bfloat16)
-    ray_count = jnp.sum(one_ray.astype(jnp.float32), axis=2)
-    pix_count = jnp.sum(one_pix.astype(jnp.float32), axis=2)
+    counts = count_low.astype(jnp.float32)
+    ray_count = jnp.sum(counts, axis=3)
+    pix_count = jnp.sum(counts, axis=2)
+    count_rows = count_low.reshape(n_ang * KINDS * ray_total, pix_total)
 
     pattern = table.reshape(KINDS, TILE, TILE)
     pattern_wide = pattern.astype(jnp.float32)
     hi = lax.Precision.HIGHEST
     ray_weight = jnp.einsum("gkv,ki->gvi", ray_count, jnp.sum(pattern_wide, axis=2), precision=hi)
     pixel_weight = jnp.einsum("gku,kj->uj", pix_count, jnp.sum(pattern_wide, axis=1), precision=hi)
-    ray_weight = jnp.tile(ray_weight, (1, 1, per_dev))
+    ray_weight = jnp.tile(ray_weight.reshape(n_ang * ray_total, TILE), (1, per_dev))
     pixel_weight = jnp.tile(pixel_weight, (1, per_dev))
-
+    pattern_kj_i = pattern.transpose(0, 2, 1).reshape(KINDS * TILE, TILE)
+    pattern_i_kj = pattern.transpose(1, 0, 2).reshape(TILE, KINDS * TILE)
+
+    rows = n_ang * ray_total * per_dev
     cur = current.reshape(pix_total, per_dev, TILE)
-    meas = measured.reshape(n_ang, ray_total, per_dev, TILE)
-    rw = ray_weight.reshape(n_ang, ray_total, per_dev, TILE)
+    meas = measured.reshape(rows, TILE)
+    rw = ray_weight.reshape(rows, TILE)
     pw = pixel_weight.reshape(pix_total, per_dev, TILE)
     scaled = meas
     for iteration in range(ITERS):
-        low = cur.astype(jnp.bfloat16)
-        gathered = jnp.einsum("gkvu,usj->gkvsj", count_low, low, preferred_element_type=jnp.float32)
-        proj = sum(
-            jnp.einsum("gkvsj,kij->gvsi", part, pattern, preferred_element_type=jnp.float32)
-            for part in split3(gathered)
-        )
+        low = cur.astype(jnp.bfloat16).reshape(pix_total, width)
+        gathered = jnp.dot(count_rows, low, preferred_element_type=jnp.float32)
+        gathered = gathered.reshape(n_ang, KINDS, ray_total, per_dev, TILE)
+        parts = split3(gathered).transpose(0, 1, 3, 4, 2, 5).reshape(3 * rows, KINDS * TILE)
+        proj = jnp.dot(parts, pattern_kj_i, preferred_element_type=jnp.float32)
+        proj = jnp.sum(proj.reshape(3, rows, TILE), axis=0)
         scaled = (meas - proj) / rw
         scaled_low = scaled.astype(jnp.bfloat16)
-        spread = jnp.einsum("gvsi,kij->gkvsj", scaled_low, pattern, preferred_element_type=jnp.float32)
-        update = sum(
-            jnp.einsum("gkvu,gkvsj->usj", count_low, part, preferred_element_type=jnp.float32)
-            for part in split3(spread)
-        )
+        spread = jnp.dot(scaled_low, pattern_i_kj, preferred_element_type=jnp.float32)
+        spread = spread.reshape(n_ang, ray_total, per_dev, KINDS, TILE)
+        parts = split3(spread).transpose(1, 4, 2, 3, 0, 5).reshape(n_ang * KINDS * ray_total, per_dev * 3 * TILE)
+        update = lax.dot_general(count_rows, parts, (((0,), (0,)), ((), ())), preferred_element_type=jnp.float32)
+        update = jnp.sum(update.reshape(pix_total, per_dev, 3, TILE), axis=2)
         cur = cur + update / pw
 
-    vol_back = cur.reshape(n_pix, tiles_dev, width)
-    vol_back = jnp.broadcast_to(vol_back[:, None], (n_pix, n_ang, tiles_dev, width))
+    vol_back = jnp.broadcast_to(cur.reshape(n_pix, 1, tiles_dev, width), (n_pix, n_ang, tiles_dev, width))
     res_back = scaled.reshape(n_ang, n_pix, rays_dev, width).transpose(1, 0, 2, 3)
     back = jnp.concatenate([vol_back, res_back], axis=2).reshape(n_grp, tiles_dev + rays_dev, width)
-    got_back = lax.all_to_all(back, ("pix", "ang"), 0, 0, tiled=False)
-    vol_out = got_back[:, :tiles_dev].transpose(1, 0, 2).reshape(tiles_dev, slices * TILE)
-    res_out = got_back[:, tiles_dev:].transpose(1, 0, 2).reshape(1, rays_dev, slices * TILE)
+    back = back.transpose(1, 0, 2)
+    got_back = lax.all_to_all(back, ("pix", "ang"), 1, 1, tiled=False)
+    vol_out = got_back[:tiles_dev].reshape(tiles_dev, slices * TILE)
+    res_out = got_back[tiles_dev:].reshape(1, rays_dev, slices * TILE)
     return (vol_out, res_out)
 
 

time: 50.6 us -> 69.1 us (1.37)
  local copies, waits for them, and re-layouts: 7.37 us -> 24.4 us
  waiting for transfers between devices: 7.46 us -> 5.79 us
  other arithmetic: 4.83 us -> 6.42 us
  matrix products: 10.3 us -> 11.5 us
    dot_general x0 -> x6, local copies, waits for them, and re-layouts: none -> 7.32 us  [the longest x2 3.49 us: per_device_split(): proj = jnp.dot(parts, pattern_kj_i, preferred_element_type=jnp.float32)]
    reshape x0 -> x6, local copies, waits for them, and re-layouts: none -> 6.5 us  [the longest x2 4.77 us: per_device_split(): split3(spread).transpose(1, 4, 2, 3, 0, 5)]
    transpose x4 -> x11, local copies, waits for them, and re-layouts: 0.41 us -> 4.67 us  [the longest x2 2.7 us: per_device_split(): split3(spread).transpose(1, 4, 2, 3, 0, 5)]
    reduce_sum x2 -> x0, other arithmetic: 2.5 us -> none  [the longest x1 2.15 us: per_device_split(): jnp.einsum('gku,kj->uj', pix_count, jnp.sum(pattern_wide, axis=1), precis...]
    all_to_all x1, waiting for transfers between devices: 7.46 us -> 5.79 us  [per_device_split(): recv = lax.all_to_all(send, ('pix', 'ang'), 1, 1, tiled=False)]
    transpose x1 -> x5, other arithmetic: 0.08 us -> 1.61 us  [the longest x2 0.76 us: per_device_split(): split3(spread).transpose(1, 4, 2, 3, 0, 5)]
    dot_general x1, matrix products: 3.53 us -> 4.73 us  [per_device_split(): jnp.einsum('gkbv,gkbu->gkvu', one_ray, one_pix, preferred_element_type=jn...]
    another operation x0 -> x4, other arithmetic: none -> 1.11 us  [split3(): return jnp.stack([hi, mid, rest - mid]).astype(jnp.bfloat16)]
  transfers between devices with their start and end apart: 1 -> 1, of which waited for: 1 -> 1; matrix products, arithmetic and copies ran while one was open for 3% -> 5% of each run, Pallas kernels for 0% -> 0%
where the time goes in v3:
time: 69.1 us; the launch traced here: 68.4 us
  local copies, waits for them, and re-layouts  24.4 us (35%)
  blocking collectives  11.9 us (17%)
  matrix products  11.5 us (17%)
  starting transfers between devices  7.25 us (10%)
  other arithmetic  6.42 us (9%)
  waiting for transfers between devices  5.79 us (8%)
  between operations  1.08 us (2%)
    all_to_all x1, blocking collectives, per_device_split(): got_back = lax.all_to_all(back, ('pix', 'ang'), 1, 1, tiled=False)  11.9 us
    all_to_all x1, starting transfers between devices, per_device_split(): recv = lax.all_to_all(send, ('pix', 'ang'), 1, 1, tiled=False)  7.25 us
    all_to_all x1, waiting for transfers between devices, per_device_split(): recv = lax.all_to_all(send, ('pix', 'ang'), 1, 1, tiled=False)  5.79 us
    reshape x2, local copies, waits for them, and re-layouts, per_device_split(): split3(spread).transpose(1, 4, 2, 3, 0, 5)  4.77 us
    dot_general x1, matrix products, per_device_split(): jnp.einsum('gkbv,gkbu->gkvu', one_ray, one_pix, preferred_element_type=jn...  4.73 us
    dot_general x2, local copies, waits for them, and re-layouts, per_device_split(): proj = jnp.dot(parts, pattern_kj_i, preferred_element_type=jnp.float32)  3.49 us
    unnamed x20, local copies, waits for them, and re-layouts  3.39 us
    dot_general x2, local copies, waits for them, and re-layouts, per_device_split(): lax.dot_general(count_rows, parts, (((0,), (0,)), ((), ())), preferred_el...  2.94 us
  transfers between devices with their start and end apart: 1, of which 1 were waited for; matrix products, arithmetic and copies ran while one was open for 5% of the time, Pallas kernels for 0%

profile of v3, /device:TPU:0, one launch (start us, length us, event | category | flops | bytes accessed | tf_op | source)
XLA Modules:
  0.0 68.4 jit_solution(4797468310405811526)
XLA Ops:
  0.6 0.8 %add_convert_fusion = f32[2,1408]{1,0:T(2,128)S(1)} fusion(s32[1,1408]{1,0:T(1,128)} %bitcast.156, s32[1,1408]{1,0:T(1,128)} %bitcast.157), kind=kLoop, calls=%fused_computation.70 | loop fusion | flops 5632 | bytes 22528 | tf_op jit(solution)/shard_map/convert_element_type | solution.py:118
  1.6 0.8 %copy.58 = f32[1,8,512]{1,2,0:T(8,128)S(1)} copy(f32[1,8,512]{2,1,0:T(8,128)} %param.6) | data formatting | bytes 32768 | tf_op args[1]
  2.4 1.0 %copy.57 = f32[64,512]{0,1:T(8,128)S(1)} copy(f32[64,512]{1,0:T(8,128)} %param.5) | data formatting | bytes 262144 | tf_op args[0]
  3.5 0.9 %pad_maximum_fusion = f32[116,8,64]{0,2,1:T(8,128)} fusion(f32[44,8,64]{0,2,1:T(8,128)S(1)} %broadcast_in_dim.6, f32[8,8,64]{0,2,1:T(8,128)S(1)} %bitcast.151, f32[64,8,64]{0,2,1:T(8,128)S(1)} %bitcast.152), kind=kLoop, calls=%fused_computation.52 | loop fusion | flops 118784 | bytes 475136 | tf_op jit(solution)/shard_map/concatenate | solution.py:121
  4.4 7.3 %all-to-all-start = ((f32[116,8,64]{0,2,1:T(8,128)}), f32[116,8,64]{0,2,1:T(8,128)S(1)}, u32[]{:S(2)}, u32[]{:S(2)}) async-start(f32[116,8,64]{0,2,1:T(8,128)} %pad_maximum_fusion), calls=%async_computation | async-start | bytes 524288 | tf_op jit(solution)/shard_map/all_to_all | solution.py:129
  13.8 1.0 %convert_reduce_fusion.2 = (f32[32,64]{1,0:T(8,128)S(1)}, f32[32,64]{1,0:T(8,128)}) fusion(bf16[32,64,64]{2,1,0:T(8,128)(2,1)S(1)} %reshape.585), kind=kLoop, calls=%fused_computation.27 | loop fusion | flops 389120 | bytes 278528 | tf_op jit(solution)/shard_map/reduce_sum | solution.py:154
  14.8 5.8 %all-to-all-done = f32[116,8,64]{0,2,1:T(8,128)S(1)} async-done(((f32[116,8,64]{0,2,1:T(8,128)}), f32[116,8,64]{0,2,1:T(8,128)S(1)}, u32[]{:S(2)}, u32[]{:S(2)}) %all-to-all-start) | async-done | bytes 237600 | tf_op jit(solution)/shard_map/all_to_all | solution.py:129
  21.8 4.7 %convert_reduce_fusion = (f32[32,256]{1,0:T(8,128)}, f32[2,32,32]{2,1,0:T(8,128)}, bf16[2,32,32,256]{3,2,1,0:T(8,128)(2,1)S(1)}) fusion(s32[2,32,176]{2,1,0:T(8,128)S(1)} %eq.34, s32[2,32,176]{2,1,0:T(8,128)S(1)} %eq.30), kind=kOutput, calls=%fused_computation.3 | convolution fusion | flops 189880320 | bytes 1179648 | tf_op jit(solution)/shard_map/gkbv,gkbu->gkvu/dot_general | solution.py:142
  28.3 2.0 %dot_general.47 = bf16[3,64,2048]{2,1,0:T(8,128)(2,1)} reshape(bf16[3,2,32,1,32,64]{5,4,2,1,0,3:T(8,128)(2,1)S(1)} %copy.68) | data formatting | bytes 1572864 | tf_op jit(solution)/shard_map/dot_general | solution.py:171
  30.5 0.8 %copy.70 = f32[2,32,32]{1,0,2:T(2,128)S(1)} copy(f32[2,32,32]{1,2,0:T(8,128)} %bitcast.155) | data formatting | bytes 16384 | tf_op jit(solution)/shard_map/gkv,ki->gvi/dot_general | solution.py:153
  31.7 1.5 %convolution_reduce_fusion.3 = f32[64,64]{1,0:T(8,128)S(1)} fusion(bf16[3,64,2048]{2,1,0:T(8,128)(2,1)} %dot_general.47, bf16[2048,64,1]{0,1,2:T(8,128)(2,1)S(1)} %reshape.599), kind=kOutput, calls=%fused_computation.32 | convolution fusion | flops 50339840 | bytes 1064960 | tf_op jit(solution)/shard_map/dot_general | solution.py:171
  33.2 0.8 %fusion.23 = (bf16[64,64]{1,0:T(8,128)(2,1)S(1)}, f32[64,64]{1,0:T(8,128)}) fusion(f32[64,64]{1,0:T(8,128)S(1)} %convolution_reduce_fusion.3, f32[2,4,8,64]{3,2,1,0:T(8,128)S(1)} %copy.65, f32[64,32]{0,1:T(8,128)S(1)} %dot_general.50, f32[32,64]{1,0:T(8,128)S(1)} %copy-done.6), kind=kOutput, calls=%fused_computation.64 | convolution fusion | flops 1585152 | bytes 73728 | tf_op jit(solution)/shard_map/gkv,ki->gvi/dot_general | solution.py:153
  35.3 1.4 %copy.72 = bf16[2,32,32,1,3,64]{5,4,2,1,0,3:T(4,128)(2,1)S(1)} copy(bf16[2,32,32,1,3,64]{5,1,2,0,3,4:T(8,128)(2,1)S(1)} %maximum_bitcast_fusion.1) | data formatting | bytes 1572864 | tf_op jit(solution)/shard_map/transpose | solution.py:177
  36.7 2.4 %reshape.589 = bf16[2048,192]{1,0:T(8,128)(2,1)} reshape(bf16[2,32,32,1,3,64]{5,4,2,1,0,3:T(4,128)(2,1)S(1)} %copy.72) | data formatting | bytes 1572864 | tf_op jit(solution)/shard_map/reshape | solution.py:177
  39.1 1.5 %copy.73 = bf16[192,2048]{1,0:T(8,128)(2,1)S(1)} copy(bf16[192,2048]{0,1:T(8,128)(2,1)} %bitcast.137) | data formatting | bytes 1572864 | tf_op jit(solution)/shard_map/dot_general | solution.py:178
  42.9 1.5 %dot_general.57 = bf16[3,64,2048]{2,1,0:T(8,128)(2,1)S(1)} reshape(bf16[3,2,32,1,32,64]{5,4,2,1,0,3:T(8,128)(2,1)S(1)} %copy.75) | data formatting | bytes 1572864 | tf_op jit(solution)/shard_map/dot_general | solution.py:171
  44.4 1.3 %convolution_reduce_fusion.2 = f32[64,64]{1,0:T(8,128)S(1)} fusion(bf16[3,64,2048]{2,1,0:T(8,128)(2,1)S(1)} %dot_general.57, bf16[2048,64,1]{0,1,2:T(8,128)(2,1)} %copy-done.1), kind=kOutput, calls=%fused_computation.31 | convolution fusion | flops 50339840 | bytes 1064960 | tf_op jit(solution)/shard_map/dot_general | solution.py:171
  45.7 0.8 %fusion.24 = f32[64,64]{1,0:T(8,128)S(1)} fusion(f32[64,64]{1,0:T(8,128)} %get-tuple-element.22, f32[64,64]{1,0:T(8,128)S(1)} %convolution_reduce_fusion.2, f32[2,4,8,64]{3,2,1,0:T(8,128)} %copy-done.4), kind=kLoop, calls=%fused_computation.65 | loop fusion | flops 8192 | bytes 65536 | tf_op jit(solution)/shard_map/div | solution.py:173
  46.5 1.2 %fusion.27 = f32[64,2048]{1,0:T(8,128)S(1)} fusion(bf16[64,2048]{1,0:T(8,128)(2,1)} %copy-done, f32[64,64]{1,0:T(8,128)S(1)} %fusion.24), kind=kOutput, calls=%fused_computation.68 | convolution fusion | flops 16781312 | bytes 802816 | tf_op jit(solution)/shard_map/dot_general | solution.py:175
  48.9 1.4 %copy.76 = bf16[2,32,32,1,3,64]{5,4,2,1,0,3:T(4,128)(2,1)S(1)} copy(bf16[2,32,32,1,3,64]{5,1,2,0,3,4:T(8,128)(2,1)S(1)} %maximum_bitcast_fusion.3) | data formatting | bytes 1572864 | tf_op jit(solution)/shard_map/transpose | solution.py:177
  50.3 2.4 %reshape.593 = bf16[2048,192]{1,0:T(8,128)(2,1)} reshape(bf16[2,32,32,1,3,64]{5,4,2,1,0,3:T(4,128)(2,1)S(1)} %copy.76) | data formatting | bytes 1572864 | tf_op jit(solution)/shard_map/reshape | solution.py:177
  52.6 1.5 %copy.77 = bf16[192,2048]{1,0:T(8,128)(2,1)S(1)} copy(bf16[192,2048]{0,1:T(8,128)(2,1)} %bitcast.138) | data formatting | bytes 1572864 | tf_op jit(solution)/shard_map/dot_general | solution.py:178
  54.9 11.9 %all_to_all.10 = f32[72,8,64]{0,2,1:T(8,128)S(1)} all-to-all(f32[72,8,64]{0,2,1:T(8,128)S(1)} %bitcast.147), channel_id=1, replica_groups=mesh['parts'=2,'pix'=4,'ang'=2,'sl'=2] {'pix','ang'}, dimensions={1} | all-to-all | bytes 294912 | tf_op jit(solution)/shard_map/all_to_all | solution.py:186
  66.8 0.8 %copy.80 = f32[64,512]{1,0:T(8,128)} copy(f32[64,512]{0,1:T(8,128)S(1)} %bitcast.145) | data formatting | bytes 262144
  (69 shorter events, 12.1 us)
Async XLA Ops:
  0.6 11.0 %copy-start.5 = (bf16[32,4096]{1,0:T(8,128)(2,1)S(1)}, bf16[32,4096]{1,0:T(8,128)(2,1)}, u32[]{:S(2)}) copy-start(bf16[32,4096]{1,0:T(8,128)(2,1)} %param.7) | copy-start | bytes 786436
  4.4 16.2 %all-to-all-start = ((f32[116,8,64]{0,2,1:T(8,128)}), f32[116,8,64]{0,2,1:T(8,128)S(1)}, u32[]{:S(2)}, u32[]{:S(2)}) async-start(f32[116,8,64]{0,2,1:T(8,128)} %pad_maximum_fusion), calls=%async_computation | async-start | bytes 524288 | tf_op jit(solution)/shard_map/all_to_all | solution.py:129
  13.3 18.3 %copy-start.1 = (bf16[2048,64,1]{0,1,2:T(8,128)(2,1)}, bf16[2048,64,1]{0,1,2:T(8,128)(2,1)S(1)}, u32[]{:S(2)}) copy-start(bf16[2048,64,1]{0,1,2:T(8,128)(2,1)S(1)} %reshape.599) | copy-start | bytes 786436
  13.8 20.2 %copy-start = (bf16[64,2048]{1,0:T(8,128)(2,1)}, bf16[64,2048]{1,0:T(8,128)(2,1)S(1)}, u32[]{:S(2)}) copy-start(bf16[64,2048]{1,0:T(8,128)(2,1)S(1)} %reshape.587) | copy-start | bytes 786436
  30.3 2.9 %copy-start.6 = (f32[32,64]{1,0:T(8,128)S(1)}, f32[32,64]{1,0:T(8,128)}, u32[]{:S(2)}) copy-start(f32[32,64]{1,0:T(8,128)} %get-tuple-element.7) | copy-start | bytes 24580
  30.5 3.5 %copy-start.4 = (f32[2,4,8,64]{3,2,1,0:T(8,128)}, f32[2,4,8,64]{3,2,1,0:T(8,128)S(1)}, u32[]{:S(2)}) copy-start(f32[2,4,8,64]{3,2,1,0:T(8,128)S(1)} %copy.65) | copy-start | bytes 49156
  39.1 1.9 %copy-start.7 = (f32[32,256]{1,0:T(8,128)S(1)}, f32[32,256]{1,0:T(8,128)}, u32[]{:S(2)}) copy-start(f32[32,256]{1,0:T(8,128)} %get-tuple-element.4) | copy-start | bytes 98308
  40.9 1.0 %copy-start.2 = (f32[256,64]{0,1:T(8,128)}, f32[256,64]{0,1:T(8,128)S(1)}, u32[]{:S(2)}) copy-start(f32[256,64]{0,1:T(8,128)S(1)} %convolution_reduce_fusion.1) | copy-start | bytes 196612
  52.6 1.9 %copy-start.3 = (f32[256,64]{0,1:T(8,128)S(1)}, f32[256,64]{0,1:T(8,128)}, u32[]{:S(2)}) copy-start(f32[256,64]{0,1:T(8,128)} %copy-done.2) | copy-start | bytes 196612

commit v4 on v2

--- a/solution.py
+++ b/solution.py
@@ -96,12 +96,9 @@
     return (current, scaled[None])
 
 
-def split3(x):
+def split2(x):
     hi = lax.reduce_precision(x, exponent_bits=8, mantissa_bits=7)
-    rest = x - hi
-    mid = lax.reduce_precision(rest, exponent_bits=8, mantissa_bits=7)
-    low = rest - mid
-    return (hi.astype(jnp.bfloat16), mid.astype(jnp.bfloat16), low.astype(jnp.bfloat16))
+    return (hi.astype(jnp.bfloat16), (x - hi).astype(jnp.bfloat16))
 
 
 def per_device_split(volume, sinogram, table, blk_ray, blk_pix, n_pix, n_ang):
@@ -141,8 +138,9 @@
     count_low = jnp.einsum(
         "gkbv,gkbu->gkvu", one_ray, one_pix, preferred_element_type=jnp.float32
     ).astype(jnp.bfloat16)
-    ray_count = jnp.sum(one_ray.astype(jnp.float32), axis=2)
-    pix_count = jnp.sum(one_pix.astype(jnp.float32), axis=2)
+    count_low = lax.optimization_barrier(count_low)
+    ray_count = jnp.sum(count_low.astype(jnp.float32), axis=3)
+    pix_count = jnp.sum(count_low.astype(jnp.float32), axis=2)
 
     pattern = table.reshape(KINDS, TILE, TILE)
     pattern_wide = pattern.astype(jnp.float32)
@@ -162,14 +160,14 @@
         gathered = jnp.einsum("gkvu,usj->gkvsj", count_low, low, preferred_element_type=jnp.float32)
         proj = sum(
             jnp.einsum("gkvsj,kij->gvsi", part, pattern, preferred_element_type=jnp.float32)
-            for part in split3(gathered)
+            for part in split2(gathered)
         )
         scaled = (meas - proj) / rw
         scaled_low = scaled.astype(jnp.bfloat16)
         spread = jnp.einsum("gvsi,kij->gkvsj", scaled_low, pattern, preferred_element_type=jnp.float32)
         update = sum(
             jnp.einsum("gkvu,gkvsj->usj", count_low, part, preferred_element_type=jnp.float32)
-            for part in split3(spread)
+            for part in split2(spread)
         )
         cur = cur + update / pw
 

time: 50.6 us -> 47.1 us (0.931)
  other arithmetic: 4.83 us -> 2.75 us
  matrix products: 10.3 us -> 9.1 us
    reduce_sum x1, other arithmetic: 2.15 us -> 0.43 us  [per_device_split(): jnp.einsum('gku,kj->uj', pix_count, jnp.sum(pattern_wide, axis=1), precis...]
    dot_general x6 -> x4, matrix products: 1.98 us -> 1.31 us  [per_device_split(): jnp.einsum('gkvu,gkvsj->usj', count_low, part, preferred_element_type=jnp...]
    dot_general x5 -> x3, matrix products: 1.48 us -> 0.9 us  [per_device_split(): jnp.einsum('gkvsj,kij->gvsi', part, pattern, preferred_element_type=jnp.f...]
where the time goes in v4:
time: 47.1 us; the launch traced here: 46.7 us
  blocking collectives  11.9 us (25%)
  matrix products  9.1 us (19%)
  waiting for transfers between devices  7.46 us (16%)
  local copies, waits for them, and re-layouts  7.26 us (15%)
  starting transfers between devices  7.25 us (15%)
  other arithmetic  2.75 us (6%)
  between operations  0.93 us (2%)
    all_to_all x1, blocking collectives, per_device_split(): got_back = lax.all_to_all(back, ('pix', 'ang'), 0, 0, tiled=False)  11.9 us
    all_to_all x1, waiting for transfers between devices, per_device_split(): recv = lax.all_to_all(send, ('pix', 'ang'), 0, 0, tiled=False)  7.46 us
    all_to_all x1, starting transfers between devices, per_device_split(): recv = lax.all_to_all(send, ('pix', 'ang'), 0, 0, tiled=False)  7.25 us
    unnamed x8, local copies, waits for them, and re-layouts  3.97 us
    dot_general x1, matrix products, per_device_split(): jnp.einsum('gkbv,gkbu->gkvu', one_ray, one_pix, preferred_element_type=jn...  3.53 us
    dot_general x2, matrix products, per_device_split(): jnp.einsum('gvsi,kij->gkvsj', scaled_low, pattern, preferred_element_type...  2.05 us
    dot_general x4, matrix products, per_device_split(): jnp.einsum('gkvu,gkvsj->usj', count_low, part, preferred_element_type=jnp...  1.31 us
    reshape x2, local copies, waits for them, and re-layouts, per_device_split(): pattern = table.reshape(KINDS, TILE, TILE)  1.07 us
  transfers between devices with their start and end apart: 1, of which 1 were waited for; matrix products, arithmetic and copies ran while one was open for 3% of the time, Pallas kernels for 0%

profile of v4, /device:TPU:0, one launch (start us, length us, event | category | flops | bytes accessed | tf_op | source)
XLA Modules:
  0.0 46.7 jit_solution(8695967747133028857)
XLA Ops:
  0.6 0.7 %add_convert_fusion = f32[2,1408]{1,0:T(2,128)S(1)} fusion(s32[1,1408]{1,0:T(1,128)} %bitcast.168, s32[1,1408]{1,0:T(1,128)} %bitcast.169), kind=kLoop, calls=%fused_computation.66 | loop fusion | flops 5632 | bytes 22528 | tf_op jit(solution)/shard_map/convert_element_type | solution.py:117
  1.5 1.0 %copy.31 = f32[64,512]{0,1:T(8,128)S(1)} copy(f32[64,512]{1,0:T(8,128)} %param.5) | data formatting | bytes 262144 | tf_op args[0]
  2.6 0.9 %copy.32 = f32[1,8,512]{1,2,0:T(8,128)S(1)} copy(f32[1,8,512]{2,1,0:T(8,128)} %param.6) | data formatting | bytes 32768 | tf_op args[1]
  3.5 0.9 %pad_maximum_fusion = f32[8,116,64]{1,2,0:T(8,128)} fusion(f32[8,44,64]{1,2,0:T(8,128)S(1)} %broadcast_in_dim.6, f32[8,8,64]{1,2,0:T(8,128)S(1)} %bitcast.164, f32[8,64,64]{1,2,0:T(8,128)S(1)} %bitcast.163), kind=kLoop, calls=%fused_computation.52 | loop fusion | flops 118784 | bytes 475136 | tf_op jit(solution)/shard_map/concatenate | solution.py:121
  4.4 7.3 %all-to-all-start = ((f32[8,116,64]{1,2,0:T(8,128)}), f32[8,116,64]{1,2,0:T(8,128)S(1)}, u32[]{:S(2)}, u32[]{:S(2)}) async-start(f32[8,116,64]{1,2,0:T(8,128)} %pad_maximum_fusion), calls=%async_computation | async-start | bytes 524288 | tf_op jit(solution)/shard_map/all_to_all | solution.py:122
  11.7 0.5 %reshape.124 = bf16[32,64,64,1]{2,1,0,3:T(8,128)(2,1)S(1)} reshape(bf16[32,4096]{1,0:T(8,128)(2,1)S(1)} %copy-done.1) | data formatting | bytes 524288 | tf_op jit(solution)/shard_map/reshape | solution.py:145
  12.2 0.5 %reshape.114 = bf16[32,64,64]{2,1,0:T(8,128)(2,1)S(1)} reshape(bf16[32,4096]{1,0:T(8,128)(2,1)S(1)} %copy-done.1) | data formatting | bytes 524288 | tf_op jit(solution)/shard_map/reshape | solution.py:145
  12.8 0.3 convert_reduce_fusion.2
  13.1 7.5 %all-to-all-done = f32[8,116,64]{1,2,0:T(8,128)S(1)} async-done(((f32[8,116,64]{1,2,0:T(8,128)}), f32[8,116,64]{1,2,0:T(8,128)S(1)}, u32[]{:S(2)}, u32[]{:S(2)}) %all-to-all-start) | async-done | bytes 237600 | tf_op jit(solution)/shard_map/all_to_all | solution.py:122
  22.2 3.5 %fusion.2 = bf16[2,32,32,256]{3,2,1,0:T(8,128)(2,1)S(1)} fusion(s32[2,32,176]{2,1,0:T(8,128)S(1)} %eq.34, s32[2,32,176]{2,1,0:T(8,128)S(1)} %eq.30), kind=kOutput, calls=%fused_computation.14 | convolution fusion | flops 188317696 | bytes 1138688 | tf_op jit(solution)/shard_map/gkbv,gkbu->gkvu/dot_general | solution.py:138
  25.9 0.4 convert_reduce_fusion
  26.4 0.4 fusion.34
  26.9 0.3 convolution_bitcast_fusion.8
  27.2 0.6 %copy-done = f32[2,32,32,64]{3,2,1,0:T(8,128)} copy-done((f32[2,32,32,64]{3,2,1,0:T(8,128)}, f32[2,32,32,64]{3,2,1,0:T(8,128)S(1)}, u32[]{:S(2)}) %copy-start) | copy-done | bytes 524312
  28.0 1.8 %convolution_bitcast_fusion.1 = f32[2,32,32,1,64]{4,2,1,0,3:T(8,128)S(1)} fusion(bf16[32,64,64,1]{2,1,0,3:T(8,128)(2,1)S(1)} %reshape.124, f32[2,32,64]{2,1,0:T(8,128)S(1)} %fusion.40, f32[2,32,64]{2,1,0:T(8,128)S(1)} %convolution_bitcast_fusion.8, f32[2,32,32,64]{3,2,1,0:T(8,128)} %copy-done, f32[2,4,8,64]{3,2,1,0:T(8,128)S(1)} %copy.40), kind=kOutput, calls=%fused_computation.16 | convolution fusion | flops 33832960 | bytes 1359872 | tf_op jit(solution)/shard_map/gvsi,kij->gkvsj/dot_general | solution.py:167
  29.8 0.3 convolution_bitcast_fusion.4
  30.4 0.3 fusion.5
  30.7 0.4 fusion.32
  31.2 0.3 convolution_bitcast_fusion.6
  32.0 0.3 convolution_bitcast_fusion.2
  32.4 0.3 fusion.8
  33.1 11.9 %all_to_all.10 = f32[8,72,64]{1,2,0:T(8,128)S(1)} all-to-all(f32[8,72,64]{1,2,0:T(8,128)S(1)} %bitcast.161), channel_id=1, replica_groups=mesh['parts'=2,'pix'=4,'ang'=2,'sl'=2] {'pix','ang'}, dimensions={0} | all-to-all | bytes 294912 | tf_op jit(solution)/shard_map/all_to_all | solution.py:178
  45.2 0.7 %copy.45 = f32[1,8,512]{2,1,0:T(8,128)} copy(f32[1,8,512]{1,2,0:T(8,128)S(1)} %bitcast.162) | data formatting | bytes 32768
  45.9 0.8 %copy.44 = f32[64,512]{1,0:T(8,128)} copy(f32[64,512]{0,1:T(8,128)S(1)} %bitcast.160) | data formatting | bytes 262144
  (35 shorter events, 3.6 us)
Async XLA Ops:
  2.6 9.1 %copy-start.1 = (bf16[32,4096]{1,0:T(8,128)(2,1)S(1)}, bf16[32,4096]{1,0:T(8,128)(2,1)}, u32[]{:S(2)}) copy-start(bf16[32,4096]{1,0:T(8,128)(2,1)} %param.7) | copy-start | bytes 786436
  4.4 16.2 %all-to-all-start = ((f32[8,116,64]{1,2,0:T(8,128)}), f32[8,116,64]{1,2,0:T(8,128)S(1)}, u32[]{:S(2)}, u32[]{:S(2)}) async-start(f32[8,116,64]{1,2,0:T(8,128)} %pad_maximum_fusion), calls=%async_computation | async-start | bytes 524288 | tf_op jit(solution)/shard_map/all_to_all | solution.py:122
  26.8 1.0 %copy-start = (f32[2,32,32,64]{3,2,1,0:T(8,128)}, f32[2,32,32,64]{3,2,1,0:T(8,128)S(1)}, u32[]{:S(2)}) copy-start(f32[2,32,32,64]{3,2,1,0:T(8,128)S(1)} %fusion.34) | copy-start | bytes 1572868

commit v5 on v4

--- a/solution.py
+++ b/solution.py
@@ -139,8 +139,9 @@
         "gkbv,gkbu->gkvu", one_ray, one_pix, preferred_element_type=jnp.float32
     ).astype(jnp.bfloat16)
     count_low = lax.optimization_barrier(count_low)
-    ray_count = jnp.sum(count_low.astype(jnp.float32), axis=3)
-    pix_count = jnp.sum(count_low.astype(jnp.float32), axis=2)
+    counts = count_low.astype(jnp.float32)
+    ray_count = jnp.sum(counts, axis=3)
+    pix_count = jnp.sum(counts, axis=2)
 
     pattern = table.reshape(KINDS, TILE, TILE)
     pattern_wide = pattern.astype(jnp.float32)
@@ -158,16 +159,16 @@
     for iteration in range(ITERS):
         low = cur.astype(jnp.bfloat16)
         gathered = jnp.einsum("gkvu,usj->gkvsj", count_low, low, preferred_element_type=jnp.float32)
-        proj = sum(
-            jnp.einsum("gkvsj,kij->gvsi", part, pattern, preferred_element_type=jnp.float32)
-            for part in split2(gathered)
+        proj = jnp.einsum(
+            "gkvsj,kij->gvsi", gathered, pattern_wide, precision=lax.Precision.HIGH,
+            preferred_element_type=jnp.float32,
         )
         scaled = (meas - proj) / rw
         scaled_low = scaled.astype(jnp.bfloat16)
         spread = jnp.einsum("gvsi,kij->gkvsj", scaled_low, pattern, preferred_element_type=jnp.float32)
-        update = sum(
-            jnp.einsum("gkvu,gkvsj->usj", count_low, part, preferred_element_type=jnp.float32)
-            for part in split2(spread)
+        update = jnp.einsum(
+            "gkvu,gkvsj->usj", counts, spread, precision=lax.Precision.HIGH,
+            preferred_element_type=jnp.float32,
         )
         cur = cur + update / pw
 

time: 47.1 us -> 45.2 us (0.960)
  matrix products: 9.1 us -> 7.69 us
  local copies, waits for them, and re-layouts: 7.26 us -> 6.77 us
    dot_general x2, matrix products: 2.05 us -> 0.54 us  [per_device_split(): jnp.einsum('gvsi,kij->gkvsj', scaled_low, pattern, preferred_element_type...]
    unnamed x8 -> x6, local copies, waits for them, and re-layouts: 3.97 us -> 3.4 us
    dot_general x7 -> x4, matrix products: 2.22 us -> 2.32 us  [the longest x2 1.44 us: per_device_split(): jnp.einsum('gkvu,gkvsj->usj', counts, spread, precision=lax.Precision.HIG...]
where the time goes in v5:
time: 45.2 us; the launch traced here: 44.8 us
  blocking collectives  11.9 us (26%)
  matrix products  7.69 us (17%)
  waiting for transfers between devices  7.46 us (17%)
  starting transfers between devices  7.25 us (16%)
  local copies, waits for them, and re-layouts  6.77 us (15%)
  other arithmetic  2.75 us (6%)
  between operations  0.9 us (2%)
    all_to_all x1, blocking collectives, per_device_split(): got_back = lax.all_to_all(back, ('pix', 'ang'), 0, 0, tiled=False)  11.9 us
    all_to_all x1, waiting for transfers between devices, per_device_split(): recv = lax.all_to_all(send, ('pix', 'ang'), 0, 0, tiled=False)  7.46 us
    all_to_all x1, starting transfers between devices, per_device_split(): recv = lax.all_to_all(send, ('pix', 'ang'), 0, 0, tiled=False)  7.25 us
    dot_general x1, matrix products, per_device_split(): jnp.einsum('gkbv,gkbu->gkvu', one_ray, one_pix, preferred_element_type=jn...  3.53 us
    unnamed x6, local copies, waits for them, and re-layouts  3.4 us
    dot_general x2, matrix products, per_device_split(): jnp.einsum('gkvu,gkvsj->usj', counts, spread, precision=lax.Precision.HIG...  1.44 us
    reshape x2, local copies, waits for them, and re-layouts, per_device_split(): pattern = table.reshape(KINDS, TILE, TILE)  1.07 us
  transfers between devices with their start and end apart: 1, of which 1 were waited for; matrix products, arithmetic and copies ran while one was open for 3% of the time, Pallas kernels for 0%

profile of v5, /device:TPU:0, one launch (start us, length us, event | category | flops | bytes accessed | tf_op | source)
XLA Modules:
  0.0 44.8 jit_solution(15547388474167661272)
XLA Ops:
  0.6 0.7 %add_convert_fusion = f32[2,1408]{1,0:T(2,128)S(1)} fusion(s32[1,1408]{1,0:T(1,128)} %bitcast.136, s32[1,1408]{1,0:T(1,128)} %bitcast.137), kind=kLoop, calls=%fused_computation.43 | loop fusion | flops 5632 | bytes 22528 | tf_op jit(solution)/shard_map/convert_element_type | solution.py:117
  1.5 1.0 %copy.42 = f32[64,512]{0,1:T(8,128)S(1)} copy(f32[64,512]{1,0:T(8,128)} %param.5) | data formatting | bytes 262144 | tf_op args[0]
  2.6 0.9 %copy.43 = f32[1,8,512]{1,2,0:T(8,128)S(1)} copy(f32[1,8,512]{2,1,0:T(8,128)} %param.6) | data formatting | bytes 32768 | tf_op args[1]
  3.5 0.9 %pad_maximum_fusion = f32[8,116,64]{1,2,0:T(8,128)} fusion(f32[8,44,64]{1,2,0:T(8,128)S(1)} %broadcast_in_dim.6, f32[8,8,64]{1,2,0:T(8,128)S(1)} %bitcast.132, f32[8,64,64]{1,2,0:T(8,128)S(1)} %bitcast.131), kind=kLoop, calls=%fused_computation.28 | loop fusion | flops 118784 | bytes 475136 | tf_op jit(solution)/shard_map/concatenate | solution.py:121
  4.4 7.3 %all-to-all-start = ((f32[8,116,64]{1,2,0:T(8,128)}), f32[8,116,64]{1,2,0:T(8,128)S(1)}, u32[]{:S(2)}, u32[]{:S(2)}) async-start(f32[8,116,64]{1,2,0:T(8,128)} %pad_maximum_fusion), calls=%async_computation | async-start | bytes 524288 | tf_op jit(solution)/shard_map/all_to_all | solution.py:122
  11.7 0.5 %reshape.96 = bf16[32,64,64,1]{2,1,0,3:T(8,128)(2,1)S(1)} reshape(bf16[32,4096]{1,0:T(8,128)(2,1)S(1)} %copy-done) | data formatting | bytes 524288 | tf_op jit(solution)/shard_map/reshape | solution.py:146
  12.2 0.5 %reshape.88 = bf16[32,64,64]{2,1,0:T(8,128)(2,1)S(1)} reshape(bf16[32,4096]{1,0:T(8,128)(2,1)S(1)} %copy-done) | data formatting | bytes 524288 | tf_op jit(solution)/shard_map/reshape | solution.py:146
  12.8 0.3 convert_reduce_fusion.2
  13.1 7.5 %all-to-all-done = f32[8,116,64]{1,2,0:T(8,128)S(1)} async-done(((f32[8,116,64]{1,2,0:T(8,128)}), f32[8,116,64]{1,2,0:T(8,128)S(1)}, u32[]{:S(2)}, u32[]{:S(2)}) %all-to-all-start) | async-done | bytes 237600 | tf_op jit(solution)/shard_map/all_to_all | solution.py:122
  22.6 3.5 %fusion.2 = bf16[2,32,32,256]{3,2,1,0:T(8,128)(2,1)S(1)} fusion(s32[2,32,176]{2,1,0:T(8,128)S(1)} %eq.34, s32[2,32,176]{2,1,0:T(8,128)S(1)} %eq.30), kind=kOutput, calls=%fused_computation.6 | convolution fusion | flops 188317696 | bytes 1138688 | tf_op jit(solution)/shard_map/gkbv,gkbu->gkvu/dot_general | solution.py:138
  26.1 0.4 convert_reduce_fusion
  26.6 0.4 fusion.16
  27.0 0.2 fusion.21
  27.2 0.4 fusion.12
  27.7 0.3 convolution_bitcast_fusion.1
  27.9 0.3 fusion.24
  28.2 0.7 %fusion.4 = f32[256,64]{0,1:T(8,128)S(1)} fusion(f32[256,64]{0,1:T(8,128)S(1)} %reshape_reshape_squeeze.3, f32[256,64]{0,1:T(8,128)S(1)} %fusion.24, bf16[2,32,32,256]{3,2,1,0:T(8,128)(2,1)S(1)} %fusion.2, f32[2,32,32,64]{3,2,1,0:T(8,128)S(1)} %convolution_bitcast_fusion.1), kind=kOutput, calls=%fused_computation.16 | convolution fusion | flops 201359360 | bytes 1769472 | tf_op jit(solution)/shard_map/gkvu,gkvsj->usj/dot_general | solution.py:169
  28.9 0.4 fusion.14
  29.3 0.4 fusion.10
  29.8 0.3 convolution_bitcast_fusion
  30.2 0.7 %fusion.6 = f32[256,64]{0,1:T(8,128)S(1)} fusion(f32[256,64]{0,1:T(8,128)S(1)} %fusion.4, f32[256,64]{0,1:T(8,128)S(1)} %fusion.24, bf16[2,32,32,256]{3,2,1,0:T(8,128)(2,1)S(1)} %fusion.2, f32[2,32,32,64]{3,2,1,0:T(8,128)S(1)} %convolution_bitcast_fusion), kind=kOutput, calls=%fused_computation.18 | convolution fusion | flops 201359360 | bytes 1769472 | tf_op jit(solution)/shard_map/gkvu,gkvsj->usj/dot_general | solution.py:169
  31.2 11.9 %all_to_all.10 = f32[8,72,64]{1,2,0:T(8,128)S(1)} all-to-all(f32[8,72,64]{1,2,0:T(8,128)S(1)} %bitcast.129), channel_id=1, replica_groups=mesh['parts'=2,'pix'=4,'ang'=2,'sl'=2] {'pix','ang'}, dimensions={0} | all-to-all | bytes 294912 | tf_op jit(solution)/shard_map/all_to_all | solution.py:179
  43.2 0.8 %copy.54 = f32[64,512]{1,0:T(8,128)} copy(f32[64,512]{0,1:T(8,128)S(1)} %bitcast.128) | data formatting | bytes 262144
  44.1 0.7 %copy.55 = f32[1,8,512]{2,1,0:T(8,128)} copy(f32[1,8,512]{1,2,0:T(8,128)S(1)} %bitcast.130) | data formatting | bytes 32768
  (29 shorter events, 2.7 us)
Async XLA Ops:
  2.6 9.1 %copy-start = (bf16[32,4096]{1,0:T(8,128)(2,1)S(1)}, bf16[32,4096]{1,0:T(8,128)(2,1)}, u32[]{:S(2)}) copy-start(bf16[32,4096]{1,0:T(8,128)(2,1)} %param.7) | copy-start | bytes 786436
  4.4 16.2 %all-to-all-start = ((f32[8,116,64]{1,2,0:T(8,128)}), f32[8,116,64]{1,2,0:T(8,128)S(1)}, u32[]{:S(2)}, u32[]{:S(2)}) async-start(f32[8,116,64]{1,2,0:T(8,128)} %pad_maximum_fusion), calls=%async_computation | async-start | bytes 524288 | tf_op jit(solution)/shard_map/all_to_all | solution.py:122

commit v6 on v5

--- a/solution.py
+++ b/solution.py
@@ -2,6 +2,8 @@
 import jax.numpy as jnp
 from jax import lax
 from jax.sharding import PartitionSpec as P
+from jax.experimental import pallas as pl
+from jax.experimental.pallas import tpu as pltpu
 
 TILE = 64
 KINDS = 32
@@ -96,6 +98,27 @@
     return (current, scaled[None])
 
 
+def pack_kernel(vol_ref, sino_ref, list_ref, out_ref):
+    n_dest = out_ref.shape[0]
+    tiles = vol_ref.shape[0]
+    rays = sino_ref.shape[0]
+    width = out_ref.shape[2]
+    lists = list_ref[...]
+    for q in range(n_dest):
+        out_ref[q, 0:tiles, :] = vol_ref[:, q * width:(q + 1) * width]
+        out_ref[q, tiles:tiles + rays, :] = sino_ref[:, q * width:(q + 1) * width]
+        out_ref[q, tiles + rays:, :] = lists
+
+
+def pack_send(volume, sino, lists, n_dest):
+    tiles, total = volume.shape
+    rows = tiles + sino.shape[0] + lists.shape[0]
+    return pl.pallas_call(
+        pack_kernel,
+        out_shape=jax.ShapeDtypeStruct((n_dest, rows, total // n_dest), jnp.float32),
+    )(volume, sino, lists)
+
+
 def split2(x):
     hi = lax.reduce_precision(x, exponent_bits=8, mantissa_bits=7)
     return (hi.astype(jnp.bfloat16), (x - hi).astype(jnp.bfloat16))
@@ -112,13 +135,10 @@
     pix_total = tiles_dev * n_pix
     width = per_dev * TILE
 
-    vol_send = volume.reshape(tiles_dev, n_grp, width).transpose(1, 0, 2)
-    sino_send = sinogram[0].reshape(rays_dev, n_grp, width).transpose(1, 0, 2)
     lists = jnp.stack([blk_ray.reshape(-1), blk_pix.reshape(-1)]).astype(jnp.float32)
     list_rows = (2 * nbd + width - 1) // width
     lists = jnp.pad(lists.reshape(-1), (0, list_rows * width - 2 * nbd)).reshape(list_rows, width)
-    list_send = jnp.broadcast_to(lists[None], (n_grp, list_rows, width))
-    send = jnp.concatenate([vol_send, sino_send, list_send], axis=1)
+    send = pack_send(volume, sinogram[0], lists, n_grp)
     recv = lax.all_to_all(send, ("pix", "ang"), 0, 0, tiled=False)
     recv = recv.reshape(n_pix, n_ang, tiles_dev + rays_dev + list_rows, width)
 

time: 45.2 us -> 46.6 us (1.031)
  Pallas kernels: 0 us -> 1.8 us
  other arithmetic: 2.75 us -> 1.78 us
  local copies, waits for them, and re-layouts: 6.77 us -> 7.4 us
    pallas_call x0 -> x1, local copies, waits for them, and re-layouts: none -> 1.92 us  [pack_send(): pl.pallas_call(pack_kernel, out_shape=jax.ShapeDtypeStruct((n_dest, rows,...]
    pallas_call x0 -> x1, Pallas kernels: none -> 1.8 us  [pack_send(): pl.pallas_call(pack_kernel, out_shape=jax.ShapeDtypeStruct((n_dest, rows,...]
    unnamed x6 -> x7, local copies, waits for them, and re-layouts: 3.4 us -> 1.85 us
    concatenate x1 -> x0, other arithmetic: 0.9 us -> none  [per_device_split(): send = jnp.concatenate([vol_send, sino_send, list_send], axis=1)]
    convert_element_type x2 -> x1, local copies, waits for them, and re-layouts: 0.17 us -> 0.69 us  [per_device_split(): jnp.stack([blk_ray.reshape(-1), blk_pix.reshape(-1)]).astype(jnp.float32)]
where the time goes in v6:
time: 46.6 us; the launch traced here: 46.2 us
  blocking collectives  11.9 us (26%)
  matrix products  7.69 us (17%)
  waiting for transfers between devices  7.46 us (16%)
  local copies, waits for them, and re-layouts  7.4 us (16%)
  starting transfers between devices  7.25 us (16%)
  Pallas kernels  1.8 us (4%)
  other arithmetic  1.78 us (4%)
  between operations  0.89 us (2%)
    all_to_all x1, blocking collectives, per_device_split(): got_back = lax.all_to_all(back, ('pix', 'ang'), 0, 0, tiled=False)  11.9 us
    all_to_all x1, waiting for transfers between devices, per_device_split(): recv = lax.all_to_all(send, ('pix', 'ang'), 0, 0, tiled=False)  7.46 us
    all_to_all x1, starting transfers between devices, per_device_split(): recv = lax.all_to_all(send, ('pix', 'ang'), 0, 0, tiled=False)  7.25 us
    dot_general x1, matrix products, per_device_split(): jnp.einsum('gkbv,gkbu->gkvu', one_ray, one_pix, preferred_element_type=jn...  3.53 us
    pallas_call x1, local copies, waits for them, and re-layouts, pack_send(): pl.pallas_call(pack_kernel, out_shape=jax.ShapeDtypeStruct((n_dest, rows,...  1.92 us
    unnamed x7, local copies, waits for them, and re-layouts  1.85 us
    pallas_call x1, Pallas kernels, pack_send(): pl.pallas_call(pack_kernel, out_shape=jax.ShapeDtypeStruct((n_dest, rows,...  1.8 us
    dot_general x2, matrix products, per_device_split(): jnp.einsum('gkvu,gkvsj->usj', counts, spread, precision=lax.Precision.HIG...  1.44 us
  transfers between devices with their start and end apart: 1, of which 1 were waited for; matrix products, arithmetic and copies ran while one was open for 3% of the time, Pallas kernels for 0%

profile of v6, /device:TPU:0, one launch (start us, length us, event | category | flops | bytes accessed | tf_op | source)
XLA Modules:
  0.0 46.2 jit_solution(7035390875281682567)
XLA Ops:
  0.6 0.8 %add_convert_fusion = f32[2,1408]{1,0:T(2,128)S(1)} fusion(s32[1,1408]{1,0:T(1,128)} %bitcast.130, s32[1,1408]{1,0:T(1,128)} %bitcast.131), kind=kLoop, calls=%fused_computation.40 | loop fusion | flops 5632 | bytes 22528 | tf_op jit(solution)/shard_map/convert_element_type | solution.py:138
  1.4 0.7 %convert_element_type.46.list_ref = f32[44,64]{1,0:T(8,128)} reshape(f32[2,1408]{1,0:T(2,128)S(1)} %add_convert_fusion) | data formatting | bytes 22528 | tf_op jit(solution)/shard_map/convert_element_type | solution.py:138
  2.1 1.8 %shard_map.68 = f32[8,116,64]{2,1,0:T(8,128)} custom-call(f32[64,512]{1,0:T(8,128)} %vol_ref.1, f32[8,512]{1,0:T(8,128)} %bitcast.129, f32[44,64]{1,0:T(8,128)} %convert_element_type.46.list_ref), custom_call_target="tpu_custom_call" | custom-call | tf_op jit(solution)/shard_map/pallas_call | solution.py:116
  3.9 1.9 %copy.34 = f32[8,116,64]{1,2,0:T(8,128)} copy(f32[8,116,64]{2,1,0:T(8,128)} %shard_map.68) | data formatting | bytes 475136 | tf_op jit(solution)/shard_map/pallas_call | solution.py:116
  5.8 7.3 %all-to-all-start = ((f32[8,116,64]{1,2,0:T(8,128)}), f32[8,116,64]{1,2,0:T(8,128)S(1)}, u32[]{:S(2)}, u32[]{:S(2)}) async-start(f32[8,116,64]{1,2,0:T(8,128)} %copy.34), calls=%async_computation | async-start | bytes 524288 | tf_op jit(solution)/shard_map/all_to_all | solution.py:142
  13.1 0.5 %reshape.89 = bf16[32,64,64,1]{2,1,0,3:T(8,128)(2,1)S(1)} reshape(bf16[32,4096]{1,0:T(8,128)(2,1)S(1)} %copy-done) | data formatting | bytes 524288 | tf_op jit(solution)/shard_map/reshape | solution.py:166
  13.6 0.5 %reshape.81 = bf16[32,64,64]{2,1,0:T(8,128)(2,1)S(1)} reshape(bf16[32,4096]{1,0:T(8,128)(2,1)S(1)} %copy-done) | data formatting | bytes 524288 | tf_op jit(solution)/shard_map/reshape | solution.py:166
  14.2 0.3 convert_reduce_fusion.2
  14.5 7.5 %all-to-all-done = f32[8,116,64]{1,2,0:T(8,128)S(1)} async-done(((f32[8,116,64]{1,2,0:T(8,128)}), f32[8,116,64]{1,2,0:T(8,128)S(1)}, u32[]{:S(2)}, u32[]{:S(2)}) %all-to-all-start) | async-done | bytes 237600 | tf_op jit(solution)/shard_map/all_to_all | solution.py:142
  24.0 3.5 %fusion.2 = bf16[2,32,32,256]{3,2,1,0:T(8,128)(2,1)S(1)} fusion(s32[2,32,176]{2,1,0:T(8,128)S(1)} %eq.34, s32[2,32,176]{2,1,0:T(8,128)S(1)} %eq.30), kind=kOutput, calls=%fused_computation.6 | convolution fusion | flops 188317696 | bytes 1138688 | tf_op jit(solution)/shard_map/gkbv,gkbu->gkvu/dot_general | solution.py:158
  27.6 0.4 convert_reduce_fusion
  28.0 0.4 fusion.16
  28.4 0.2 fusion.21
  28.6 0.4 fusion.12
  29.1 0.3 convolution_bitcast_fusion.1
  29.4 0.3 fusion.24
  29.6 0.7 %fusion.4 = f32[256,64]{0,1:T(8,128)S(1)} fusion(f32[256,64]{0,1:T(8,128)S(1)} %reshape_reshape_squeeze.3, f32[256,64]{0,1:T(8,128)S(1)} %fusion.24, bf16[2,32,32,256]{3,2,1,0:T(8,128)(2,1)S(1)} %fusion.2, f32[2,32,32,64]{3,2,1,0:T(8,128)S(1)} %convolution_bitcast_fusion.1), kind=kOutput, calls=%fused_computation.16 | convolution fusion | flops 201359360 | bytes 1769472 | tf_op jit(solution)/shard_map/gkvu,gkvsj->usj/dot_general | solution.py:189
  30.4 0.4 fusion.14
  30.8 0.4 fusion.10
  31.2 0.3 convolution_bitcast_fusion
  31.6 0.7 %fusion.6 = f32[256,64]{0,1:T(8,128)S(1)} fusion(f32[256,64]{0,1:T(8,128)S(1)} %fusion.4, f32[256,64]{0,1:T(8,128)S(1)} %fusion.24, bf16[2,32,32,256]{3,2,1,0:T(8,128)(2,1)S(1)} %fusion.2, f32[2,32,32,64]{3,2,1,0:T(8,128)S(1)} %convolution_bitcast_fusion), kind=kOutput, calls=%fused_computation.18 | convolution fusion | flops 201359360 | bytes 1769472 | tf_op jit(solution)/shard_map/gkvu,gkvsj->usj/dot_general | solution.py:189
  32.7 11.9 %all_to_all.10 = f32[8,72,64]{1,2,0:T(8,128)S(1)} all-to-all(f32[8,72,64]{1,2,0:T(8,128)S(1)} %bitcast.124), channel_id=1, replica_groups=mesh['parts'=2,'pix'=4,'ang'=2,'sl'=2] {'pix','ang'}, dimensions={0} | all-to-all | bytes 294912 | tf_op jit(solution)/shard_map/all_to_all | solution.py:199
  44.6 0.8 %copy.44 = f32[64,512]{1,0:T(8,128)} copy(f32[64,512]{0,1:T(8,128)S(1)} %bitcast.123) | data formatting | bytes 262144
  45.5 0.7 %copy.45 = f32[1,8,512]{2,1,0:T(8,128)} copy(f32[1,8,512]{1,2,0:T(8,128)S(1)} %bitcast.125) | data formatting | bytes 32768
  (27 shorter events, 2.5 us)
Async XLA Ops:
  0.6 12.4 %copy-start = (bf16[32,4096]{1,0:T(8,128)(2,1)S(1)}, bf16[32,4096]{1,0:T(8,128)(2,1)}, u32[]{:S(2)}) copy-start(bf16[32,4096]{1,0:T(8,128)(2,1)} %param.7) | copy-start | bytes 786436
  5.8 16.2 %all-to-all-start = ((f32[8,116,64]{1,2,0:T(8,128)}), f32[8,116,64]{1,2,0:T(8,128)S(1)}, u32[]{:S(2)}, u32[]{:S(2)}) async-start(f32[8,116,64]{1,2,0:T(8,128)} %copy.34), calls=%async_computation | async-start | bytes 524288 | tf_op jit(solution)/shard_map/all_to_all | solution.py:142

commit v7 on v5

--- a/solution.py
+++ b/solution.py
@@ -112,20 +112,19 @@
     pix_total = tiles_dev * n_pix
     width = per_dev * TILE
 
+    lists = jnp.stack([blk_ray.reshape(-1), blk_pix.reshape(-1)])
+    list_send = jnp.broadcast_to(lists[None], (n_grp, 2, nbd))
+    got = lax.all_to_all(list_send, ("pix", "ang"), 0, 0, tiled=False)
+    got = got.reshape(n_pix, n_ang, 2, nbd).transpose(2, 1, 0, 3)
+
     vol_send = volume.reshape(tiles_dev, n_grp, width).transpose(1, 0, 2)
     sino_send = sinogram[0].reshape(rays_dev, n_grp, width).transpose(1, 0, 2)
-    lists = jnp.stack([blk_ray.reshape(-1), blk_pix.reshape(-1)]).astype(jnp.float32)
-    list_rows = (2 * nbd + width - 1) // width
-    lists = jnp.pad(lists.reshape(-1), (0, list_rows * width - 2 * nbd)).reshape(list_rows, width)
-    list_send = jnp.broadcast_to(lists[None], (n_grp, list_rows, width))
-    send = jnp.concatenate([vol_send, sino_send, list_send], axis=1)
+    send = jnp.concatenate([vol_send, sino_send], axis=1)
     recv = lax.all_to_all(send, ("pix", "ang"), 0, 0, tiled=False)
-    recv = recv.reshape(n_pix, n_ang, tiles_dev + rays_dev + list_rows, width)
+    recv = recv.reshape(n_pix, n_ang, tiles_dev + rays_dev, width)
 
     current = recv[:, 0, :tiles_dev].reshape(pix_total, width)
-    measured = recv[:, :, tiles_dev:tiles_dev + rays_dev].transpose(1, 0, 2, 3).reshape(n_ang, ray_total, width)
-    got = recv[:, :, tiles_dev + rays_dev:].reshape(n_pix, n_ang, -1)[:, :, :2 * nbd]
-    got = got.reshape(n_pix, n_ang, 2, nbd).transpose(2, 1, 0, 3).astype(jnp.int32)
+    measured = recv[:, :, tiles_dev:].transpose(1, 0, 2, 3).reshape(n_ang, ray_total, width)
     per_kind = nbd // KINDS
     offsets = (jnp.arange(n_pix, dtype=jnp.int32) * tiles_dev)[None, :, None, None]
     ray_ids = got[0].reshape(n_ang, n_pix, KINDS, per_kind)

time: 45.2 us -> 46.5 us (1.029)
  starting transfers between devices: 7.25 us -> 10.7 us
  waiting for transfers between devices: 7.46 us -> 5.62 us
    all_to_all x0 -> x1, starting transfers between devices: none -> 7.25 us  [per_device_split(): got = lax.all_to_all(list_send, ('pix', 'ang'), 0, 0, tiled=False)]
    all_to_all x1, waiting for transfers between devices: 7.46 us -> 2.71 us  [per_device_split(): recv = lax.all_to_all(send, ('pix', 'ang'), 0, 0, tiled=False)]
    all_to_all x1, starting transfers between devices: 7.25 us -> 3.41 us  [per_device_split(): recv = lax.all_to_all(send, ('pix', 'ang'), 0, 0, tiled=False)]
    all_to_all x0 -> x1, waiting for transfers between devices: none -> 2.9 us  [per_device_split(): got = lax.all_to_all(list_send, ('pix', 'ang'), 0, 0, tiled=False)]
    convert_element_type x2 -> x0, other arithmetic: 0.86 us -> none  [the longest x1 0.72 us: per_device_split(): jnp.stack([blk_ray.reshape(-1), blk_pix.reshape(-1)]).astype(jnp.float32)]
    another operation x0 -> x1, other arithmetic: none -> 0.76 us  [per_device_split(): lists = jnp.stack([blk_ray.reshape(-1), blk_pix.reshape(-1)])]
    broadcast_in_dim x1, local copies, waits for them, and re-layouts: 0.02 us -> 0.66 us  [per_device_split(): list_send = jnp.broadcast_to(lists[None], (n_grp, 2, nbd))]
    convert_element_type x4 -> x0, local copies, waits for them, and re-layouts: 0.48 us -> none  [the longest x2 0.3 us: per_device_split(): got.reshape(n_pix, n_ang, 2, nbd).transpose(2, 1, 0, 3).astype(jnp.int32)]
  transfers between devices with their start and end apart: 1 -> 2, of which waited for: 1 -> 2; matrix products, arithmetic and copies ran while one was open for 3% -> 21% of each run, Pallas kernels for 0% -> 0%
where the time goes in v7:
time: 46.5 us; the launch traced here: 46 us
  blocking collectives  11.7 us (25%)
  starting transfers between devices  10.7 us (23%)
  matrix products  7.71 us (17%)
  local copies, waits for them, and re-layouts  6.83 us (15%)
  waiting for transfers between devices  5.62 us (12%)
  other arithmetic  2.59 us (6%)
  between operations  0.9 us (2%)
    all_to_all x1, blocking collectives, per_device_split(): got_back = lax.all_to_all(back, ('pix', 'ang'), 0, 0, tiled=False)  11.7 us
    all_to_all x1, starting transfers between devices, per_device_split(): got = lax.all_to_all(list_send, ('pix', 'ang'), 0, 0, tiled=False)  7.25 us
    dot_general x1, matrix products, per_device_split(): jnp.einsum('gkbv,gkbu->gkvu', one_ray, one_pix, preferred_element_type=jn...  3.53 us
    all_to_all x1, starting transfers between devices, per_device_split(): recv = lax.all_to_all(send, ('pix', 'ang'), 0, 0, tiled=False)  3.41 us
    unnamed x6, local copies, waits for them, and re-layouts  3.36 us
    all_to_all x1, waiting for transfers between devices, per_device_split(): got = lax.all_to_all(list_send, ('pix', 'ang'), 0, 0, tiled=False)  2.9 us
    all_to_all x1, waiting for transfers between devices, per_device_split(): recv = lax.all_to_all(send, ('pix', 'ang'), 0, 0, tiled=False)  2.71 us
    dot_general x2, matrix products, per_device_split(): jnp.einsum('gkvu,gkvsj->usj', counts, spread, precision=lax.Precision.HIG...  1.44 us
  transfers between devices with their start and end apart: 2, of which 2 were waited for; matrix products, arithmetic and copies ran while one was open for 21% of the time, Pallas kernels for 0%

profile of v7, /device:TPU:0, one launch (start us, length us, event | category | flops | bytes accessed | tf_op | source)
XLA Modules:
  0.0 46.0 jit_solution(4225486866238944977)
XLA Ops:
  0.6 0.8 %pad_add_fusion = s32[2,1408]{1,0:T(2,128)S(1)} fusion(s32[1,1408]{1,0:T(1,128)} %bitcast.133, s32[1,1408]{1,0:T(1,128)} %bitcast.134), kind=kLoop, calls=%fused_computation.40 | loop fusion | flops 2816 | bytes 22528 | tf_op jit(solution)/shard_map/stack | solution.py:115
  1.4 0.7 %broadcast_in_dim.6 = s32[8,2,1408]{2,1,0:T(2,128)} broadcast(s32[2,1408]{1,0:T(2,128)S(1)} %pad_add_fusion), dimensions={1,2} | broadcast | bytes 101376 | tf_op jit(solution)/shard_map/broadcast_in_dim | solution.py:116
  2.1 7.3 %all-to-all-start.1 = ((s32[8,2,1408]{2,1,0:T(2,128)}), s32[8,2,1408]{2,1,0:T(2,128)S(1)}, u32[]{:S(2)}, u32[]{:S(2)}) async-start(s32[8,2,1408]{2,1,0:T(2,128)} %broadcast_in_dim.6), calls=%async_computation.1 | async-start | bytes 180224 | tf_op jit(solution)/shard_map/all_to_all | solution.py:117
  9.3 1.0 %copy.26 = f32[64,512]{0,1:T(8,128)S(1)} copy(f32[64,512]{1,0:T(8,128)} %param.5) | data formatting | bytes 262144 | tf_op args[0]
  10.4 0.8 %copy.27 = f32[1,8,512]{1,2,0:T(8,128)S(1)} copy(f32[1,8,512]{2,1,0:T(8,128)} %param.6) | data formatting | bytes 32768 | tf_op args[1]
  11.2 0.8 %pad_maximum_fusion = f32[8,72,64]{1,2,0:T(8,128)} fusion(f32[8,8,64]{1,2,0:T(8,128)S(1)} %bitcast.128, f32[8,64,64]{1,2,0:T(8,128)S(1)} %bitcast.127), kind=kLoop, calls=%fused_computation.27 | loop fusion | flops 36864 | bytes 294912 | tf_op jit(solution)/shard_map/concatenate | solution.py:122
  12.0 0.5 %reshape.92 = bf16[32,64,64,1]{2,1,0,3:T(8,128)(2,1)S(1)} reshape(bf16[32,4096]{1,0:T(8,128)(2,1)S(1)} %copy-done) | data formatting | bytes 524288 | tf_op jit(solution)/shard_map/reshape | solution.py:145
  12.6 0.5 %reshape.84 = bf16[32,64,64]{2,1,0:T(8,128)(2,1)S(1)} reshape(bf16[32,4096]{1,0:T(8,128)(2,1)S(1)} %copy-done) | data formatting | bytes 524288 | tf_op jit(solution)/shard_map/reshape | solution.py:145
  13.1 0.3 convert_reduce_fusion.2
  13.5 2.9 %all-to-all-done.1 = s32[8,2,1408]{2,1,0:T(2,128)S(1)} async-done(((s32[8,2,1408]{2,1,0:T(2,128)}), s32[8,2,1408]{2,1,0:T(2,128)S(1)}, u32[]{:S(2)}, u32[]{:S(2)}) %all-to-all-start.1) | async-done | bytes 90144 | tf_op jit(solution)/shard_map/all_to_all | solution.py:117
  16.4 3.4 %all-to-all-start = ((f32[8,72,64]{1,2,0:T(8,128)}), f32[8,72,64]{1,2,0:T(8,128)S(1)}, u32[]{:S(2)}, u32[]{:S(2)}) async-start(f32[8,72,64]{1,2,0:T(8,128)} %pad_maximum_fusion), calls=%async_computation | async-start | bytes 524288 | tf_op jit(solution)/shard_map/all_to_all | solution.py:123
  20.8 3.5 %fusion.2 = bf16[2,32,32,256]{3,2,1,0:T(8,128)(2,1)S(1)} fusion(s32[2,32,176]{2,1,0:T(8,128)S(1)} %eq.34, s32[2,32,176]{2,1,0:T(8,128)S(1)} %eq.30), kind=kOutput, calls=%fused_computation.6 | convolution fusion | flops 188317696 | bytes 1138688 | tf_op jit(solution)/shard_map/gkbv,gkbu->gkvu/dot_general | solution.py:137
  24.4 0.4 convert_reduce_fusion
  25.3 2.7 %all-to-all-done = f32[8,72,64]{1,2,0:T(8,128)S(1)} async-done(((f32[8,72,64]{1,2,0:T(8,128)}), f32[8,72,64]{1,2,0:T(8,128)S(1)}, u32[]{:S(2)}, u32[]{:S(2)}) %all-to-all-start) | async-done | bytes 147488 | tf_op jit(solution)/shard_map/all_to_all | solution.py:123
  28.5 0.4 fusion.16
  28.9 0.4 fusion.12
  29.4 0.3 convolution_bitcast_fusion.1
  29.7 0.7 %fusion.4 = f32[256,64]{0,1:T(8,128)S(1)} fusion(f32[256,64]{0,1:T(8,128)S(1)} %reshape_reshape_squeeze.3, f32[256,64]{0,1:T(8,128)S(1)} %fusion.25, bf16[2,32,32,256]{3,2,1,0:T(8,128)(2,1)S(1)} %fusion.2, f32[2,32,32,64]{3,2,1,0:T(8,128)S(1)} %convolution_bitcast_fusion.1), kind=kOutput, calls=%fused_computation.16 | convolution fusion | flops 201359360 | bytes 1769472 | tf_op jit(solution)/shard_map/gkvu,gkvsj->usj/dot_general | solution.py:168
  30.4 0.4 fusion.14
  30.8 0.4 fusion.10
  31.7 0.7 %fusion.6 = f32[256,64]{0,1:T(8,128)S(1)} fusion(f32[256,64]{0,1:T(8,128)S(1)} %fusion.4, f32[256,64]{0,1:T(8,128)S(1)} %fusion.25, bf16[2,32,32,256]{3,2,1,0:T(8,128)(2,1)S(1)} %fusion.2, f32[2,32,32,64]{3,2,1,0:T(8,128)S(1)} %convolution_bitcast_fusion), kind=kOutput, calls=%fused_computation.18 | convolution fusion | flops 201359360 | bytes 1769472 | tf_op jit(solution)/shard_map/gkvu,gkvsj->usj/dot_general | solution.py:168
  32.7 11.7 %all_to_all.15 = f32[8,72,64]{1,2,0:T(8,128)S(1)} all-to-all(f32[8,72,64]{1,2,0:T(8,128)S(1)} %bitcast.126), channel_id=1, replica_groups=mesh['parts'=2,'pix'=4,'ang'=2,'sl'=2] {'pix','ang'}, dimensions={0} | all-to-all | bytes 294912 | tf_op jit(solution)/shard_map/all_to_all | solution.py:178
  44.4 0.8 %copy.37 = f32[64,512]{1,0:T(8,128)} copy(f32[64,512]{0,1:T(8,128)S(1)} %bitcast.123) | data formatting | bytes 262144
  45.3 0.7 %copy.38 = f32[1,8,512]{2,1,0:T(8,128)} copy(f32[1,8,512]{1,2,0:T(8,128)S(1)} %bitcast.129) | data formatting | bytes 32768
  (27 shorter events, 2.7 us)
Async XLA Ops:
  0.6 11.4 %copy-start = (bf16[32,4096]{1,0:T(8,128)(2,1)S(1)}, bf16[32,4096]{1,0:T(8,128)(2,1)}, u32[]{:S(2)}) copy-start(bf16[32,4096]{1,0:T(8,128)(2,1)} %param.7) | copy-start | bytes 786436
  2.1 14.3 %all-to-all-start.1 = ((s32[8,2,1408]{2,1,0:T(2,128)}), s32[8,2,1408]{2,1,0:T(2,128)S(1)}, u32[]{:S(2)}, u32[]{:S(2)}) async-start(s32[8,2,1408]{2,1,0:T(2,128)} %broadcast_in_dim.6), calls=%async_computation.1 | async-start | bytes 180224 | tf_op jit(solution)/shard_map/all_to_all | solution.py:117
  16.4 11.6 %all-to-all-start = ((f32[8,72,64]{1,2,0:T(8,128)}), f32[8,72,64]{1,2,0:T(8,128)S(1)}, u32[]{:S(2)}, u32[]{:S(2)}) async-start(f32[8,72,64]{1,2,0:T(8,128)} %pad_maximum_fusion), calls=%async_computation | async-start | bytes 524288 | tf_op jit(solution)/shard_map/all_to_all | solution.py:123

commit v8 on v5

--- a/solution.py
+++ b/solution.py
@@ -105,20 +105,22 @@
     n_grp = n_pix * n_ang
     tiles_dev = volume.shape[0]
     slices = volume.shape[1] // TILE
-    per_dev = slices // n_grp
+    per_dev = slices // n_pix
     rays_dev = sinogram.shape[1]
     nbd = blk_ray.shape[-1]
     ray_total = rays_dev * n_pix
     pix_total = tiles_dev * n_pix
     width = per_dev * TILE
 
-    vol_send = volume.reshape(tiles_dev, n_grp, width).transpose(1, 0, 2)
-    sino_send = sinogram[0].reshape(rays_dev, n_grp, width).transpose(1, 0, 2)
+    vol_send = volume.reshape(tiles_dev, n_pix, width).transpose(1, 0, 2)
+    vol_send = jnp.broadcast_to(vol_send[:, None], (n_pix, n_ang, tiles_dev, width))
+    sino_send = sinogram[0].reshape(rays_dev, n_pix, width).transpose(1, 0, 2)
+    sino_send = jnp.broadcast_to(sino_send[:, None], (n_pix, n_ang, rays_dev, width))
     lists = jnp.stack([blk_ray.reshape(-1), blk_pix.reshape(-1)]).astype(jnp.float32)
     list_rows = (2 * nbd + width - 1) // width
     lists = jnp.pad(lists.reshape(-1), (0, list_rows * width - 2 * nbd)).reshape(list_rows, width)
-    list_send = jnp.broadcast_to(lists[None], (n_grp, list_rows, width))
-    send = jnp.concatenate([vol_send, sino_send, list_send], axis=1)
+    list_send = jnp.broadcast_to(lists, (n_pix, n_ang, list_rows, width))
+    send = jnp.concatenate([vol_send, sino_send, list_send], axis=2).reshape(n_grp, -1, width)
     recv = lax.all_to_all(send, ("pix", "ang"), 0, 0, tiled=False)
     recv = recv.reshape(n_pix, n_ang, tiles_dev + rays_dev + list_rows, width)
 
@@ -172,11 +174,12 @@
         )
         cur = cur + update / pw
 
+    own_group = lax.axis_index("ang")
     vol_back = cur.reshape(n_pix, tiles_dev, width)
-    vol_back = jnp.broadcast_to(vol_back[:, None], (n_pix, n_ang, tiles_dev, width))
-    res_back = scaled.reshape(n_ang, n_pix, rays_dev, width).transpose(1, 0, 2, 3)
-    back = jnp.concatenate([vol_back, res_back], axis=2).reshape(n_grp, tiles_dev + rays_dev, width)
-    got_back = lax.all_to_all(back, ("pix", "ang"), 0, 0, tiled=False)
+    res_back = lax.dynamic_index_in_dim(scaled, own_group, 0, keepdims=False)
+    res_back = res_back.reshape(n_pix, rays_dev, width)
+    back = jnp.concatenate([vol_back, res_back], axis=1)
+    got_back = lax.all_to_all(back, "pix", 0, 0, tiled=False)
     vol_out = got_back[:, :tiles_dev].transpose(1, 0, 2).reshape(tiles_dev, slices * TILE)
     res_out = got_back[:, tiles_dev:].transpose(1, 0, 2).reshape(1, rays_dev, slices * TILE)
     return (vol_out, res_out)
@@ -187,7 +190,7 @@
     n_ang = mesh.shape["ang"]
 
     def body(volume, sinogram, table, blk_ray, blk_pix):
-        if (volume.shape[1] // TILE) % (n_pix * n_ang) == 0:
+        if (volume.shape[1] // TILE) % n_pix == 0:
             return per_device_split(volume, sinogram, table, blk_ray, blk_pix, n_pix, n_ang)
         return per_device_base(volume, sinogram, table, blk_ray, blk_pix)
 

time: 45.2 us -> 46.8 us (1.035)
  matrix products: 7.69 us -> 10.8 us
  blocking collectives: 11.9 us -> 9.02 us
  waiting for transfers between devices: 7.46 us -> 10.2 us
  local copies, waits for them, and re-layouts: 6.77 us -> 5.81 us
    unnamed x6 -> x4, local copies, waits for them, and re-layouts: 3.4 us -> 0.01 us
    all_to_all x1, blocking collectives: 11.9 us -> 9.02 us  [per_device_split(): got_back = lax.all_to_all(back, 'pix', 0, 0, tiled=False)]
    all_to_all x1, waiting for transfers between devices: 7.46 us -> 10.2 us  [per_device_split(): recv = lax.all_to_all(send, ('pix', 'ang'), 0, 0, tiled=False)]
    reshape x0 -> x6, local copies, waits for them, and re-layouts: none -> 2.57 us  [the longest x1 0.95 us: per_device_split(): vol_send = volume.reshape(tiles_dev, n_pix, width).transpose(1, 0, 2)]
    dot_general x2, matrix products: 0.54 us -> 1.86 us  [per_device_split(): jnp.einsum('gvsi,kij->gkvsj', scaled_low, pattern, preferred_element_type...]
    dot_general x2, matrix products: 1.44 us -> 2.56 us  [per_device_split(): jnp.einsum('gkvu,gkvsj->usj', counts, spread, precision=lax.Precision.HIG...]
    broadcast_in_dim x4 -> x3, local copies, waits for them, and re-layouts: 0.16 us -> 0.75 us  [the longest x1 0.72 us: per_device_split(): jnp.broadcast_to(sino_send[:, None], (n_pix, n_ang, rays_dev, width))]
    dot_general x2, matrix products: 0.88 us -> 1.42 us  [per_device_split(): jnp.einsum('gkvsj,kij->gvsi', gathered, pattern_wide, precision=lax.Preci...]
where the time goes in v8:
time: 46.8 us; the launch traced here: 46.4 us
  matrix products  10.8 us (23%)
  waiting for transfers between devices  10.2 us (22%)
  blocking collectives  9.02 us (19%)
  starting transfers between devices  7.25 us (15%)
  local copies, waits for them, and re-layouts  5.81 us (12%)
  other arithmetic  2.45 us (5%)
  between operations  0.94 us (2%)
    all_to_all x1, waiting for transfers between devices, per_device_split(): recv = lax.all_to_all(send, ('pix', 'ang'), 0, 0, tiled=False)  10.2 us
    all_to_all x1, blocking collectives, per_device_split(): got_back = lax.all_to_all(back, 'pix', 0, 0, tiled=False)  9.02 us
    all_to_all x1, starting transfers between devices, per_device_split(): recv = lax.all_to_all(send, ('pix', 'ang'), 0, 0, tiled=False)  7.25 us
    dot_general x1, matrix products, per_device_split(): jnp.einsum('gkbv,gkbu->gkvu', one_ray, one_pix, preferred_element_type=jn...  3.53 us
    dot_general x2, matrix products, per_device_split(): jnp.einsum('gkvu,gkvsj->usj', counts, spread, precision=lax.Precision.HIG...  2.56 us
    dot_general x2, matrix products, per_device_split(): jnp.einsum('gvsi,kij->gkvsj', scaled_low, pattern, preferred_element_type...  1.86 us
    dot_general x2, matrix products, per_device_split(): jnp.einsum('gkvsj,kij->gvsi', gathered, pattern_wide, precision=lax.Preci...  1.42 us
    reshape x2, local copies, waits for them, and re-layouts, per_device_split(): pattern = table.reshape(KINDS, TILE, TILE)  1.07 us
  transfers between devices with their start and end apart: 1, of which 1 were waited for; matrix products, arithmetic and copies ran while one was open for 3% of the time, Pallas kernels for 0%

profile of v8, /device:TPU:0, one launch (start us, length us, event | category | flops | bytes accessed | tf_op | source)
XLA Modules:
  0.0 46.4 jit_solution(12221514519458844505)
XLA Ops:
  0.6 0.8 %add_convert_fusion = f32[2,1408]{1,0:T(2,128)S(1)} fusion(s32[1,1408]{1,0:T(1,128)} %bitcast.138, s32[1,1408]{1,0:T(1,128)} %bitcast.139), kind=kLoop, calls=%fused_computation.55 | loop fusion | flops 5632 | bytes 22528 | tf_op jit(solution)/shard_map/convert_element_type | solution.py:119
  1.4 0.9 %reshape.49 = f32[64,4,128]{2,1,0:T(4,128)S(1)} reshape(f32[64,512]{1,0:T(8,128)} %param.5) | data formatting | bytes 262144 | tf_op jit(solution)/shard_map/reshape | solution.py:115
  2.4 0.7 %broadcast_in_dim.7 = f32[4,2,8,128]{3,2,1,0:T(8,128)S(1)} broadcast(f32[4,8,128]{2,1,0:T(8,128)} %bitcast.137), dimensions={0,2,3} | broadcast | bytes 49152 | tf_op jit(solution)/shard_map/broadcast_in_dim | solution.py:118
  3.2 0.8 %pad_maximum_fusion = f32[4,2,94,128]{3,2,1,0:T(8,128)} fusion(f32[4,2,22,128]{3,2,1,0:T(8,128)S(1)} %broadcast_in_dim.8, f32[4,2,8,128]{3,2,1,0:T(8,128)S(1)} %broadcast_in_dim.7, f32[4,2,64,128]{3,2,1,0:T(8,128)S(1)} %broadcast_in_dim.6), kind=kLoop, calls=%fused_computation.36 | loop fusion | flops 192512 | bytes 770048 | tf_op jit(solution)/shard_map/concatenate | solution.py:123
  3.9 7.3 %all-to-all-start = ((f32[8,94,128]{2,1,0:T(8,128)}), f32[8,94,128]{2,1,0:T(8,128)S(1)}, u32[]{:S(2)}, u32[]{:S(2)}) async-start(f32[8,94,128]{2,1,0:T(8,128)} %bitcast.5), calls=%async_computation | async-start | bytes 786432 | tf_op jit(solution)/shard_map/all_to_all | solution.py:124
  11.2 0.5 %reshape.59 = bf16[32,64,64,1,1]{2,1,0,3,4:T(8,128)(2,1)S(1)} reshape(bf16[32,4096]{1,0:T(8,128)(2,1)S(1)} %copy-done.1) | data formatting | bytes 524288 | tf_op jit(solution)/shard_map/reshape | solution.py:148
  11.8 0.5 %reshape.52 = bf16[32,64,64]{2,1,0:T(8,128)(2,1)S(1)} reshape(bf16[32,4096]{1,0:T(8,128)(2,1)S(1)} %copy-done.1) | data formatting | bytes 524288 | tf_op jit(solution)/shard_map/reshape | solution.py:148
  12.3 0.3 convert_reduce_fusion.2
  12.7 10.2 %all-to-all-done = f32[8,94,128]{2,1,0:T(8,128)S(1)} async-done(((f32[8,94,128]{2,1,0:T(8,128)}), f32[8,94,128]{2,1,0:T(8,128)S(1)}, u32[]{:S(2)}, u32[]{:S(2)}) %all-to-all-start) | async-done | bytes 385056 | tf_op jit(solution)/shard_map/all_to_all | solution.py:124
  24.4 3.5 %fusion.6 = bf16[2,32,32,256]{3,2,1,0:T(8,128)(2,1)S(1)} fusion(s32[2,32,176]{2,1,0:T(8,128)S(1)} %eq.34, s32[2,32,176]{2,1,0:T(8,128)S(1)} %eq.30), kind=kOutput, calls=%fused_computation.10 | convolution fusion | flops 188317696 | bytes 1138688 | tf_op jit(solution)/shard_map/gkbv,gkbu->gkvu/dot_general | solution.py:140
  28.0 0.4 convert_reduce_fusion
  28.4 0.4 fusion.35
  28.9 0.2 fusion.48
  29.1 0.7 %fusion.18 = bf16[2,32,2,64,1]{3,1,2,0,4:T(8,128)(2,1)S(1)} fusion(f32[2,32,32,2,64]{4,2,1,3,0:T(8,128)S(1)} %fusion.35, bf16[32,64,64,1,1]{2,1,0,3,4:T(8,128)(2,1)S(1)} %reshape.59, f32[2,32,2,64]{3,2,1,0:T(2,128)S(1)} %reshape_reshape.4, f32[2,32,64]{2,1,0:T(8,128)S(1)} %fusion.48), kind=kOutput, calls=%fused_computation.22 | convolution fusion | flops 100687872 | bytes 1376256 | tf_op jit(solution)/shard_map/gkvsj,kij->gvsi/dot_general | solution.py:164
  29.8 0.4 fusion.46
  30.2 0.3 fusion.51
  30.5 1.3 %fusion.28 = f32[256,2,64]{0,2,1:T(8,128)S(1)} fusion(f32[256,2,64]{0,2,1:T(8,128)S(1)} %copy.49, f32[2,32,2,32,64]{4,1,3,0,2:T(8,128)S(1)} %fusion.46, bf16[2,32,32,256]{3,2,1,0:T(8,128)(2,1)S(1)} %fusion.6, f32[256,64]{0,1:T(8,128)S(1)} %fusion.51), kind=kOutput, calls=%fused_computation.26 | convolution fusion | flops 402718720 | bytes 2424832 | tf_op jit(solution)/shard_map/gkvu,gkvsj->usj/dot_general | solution.py:171
  31.8 0.5 fusion.33
  32.3 0.7 %fusion.16 = f32[2,32,2,64]{3,1,2,0:T(8,128)S(1)} fusion(f32[2,32,32,2,64]{4,2,1,3,0:T(8,128)S(1)} %fusion.33, bf16[32,64,64,1,1]{2,1,0,3,4:T(8,128)(2,1)S(1)} %reshape.59, f32[2,32,2,64]{3,2,1,0:T(2,128)S(1)} %reshape_reshape.4, f32[2,32,64]{2,1,0:T(8,128)S(1)} %fusion.48), kind=kOutput, calls=%fused_computation.20 | convolution fusion | flops 100679680 | bytes 1392640 | tf_op jit(solution)/shard_map/gkvsj,kij->gvsi/dot_general | solution.py:164
  33.0 1.5 %fusion.44 = f32[2,32,2,32,64]{4,1,3,0,2:T(8,128)S(1)} fusion(bf16[32,64,64,1,1]{2,1,0,3,4:T(8,128)(2,1)} %copy-done, f32[2,32,2,64]{3,1,2,0:T(8,128)S(1)} %fusion.16), kind=kOutput, calls=%fused_computation.47 | convolution fusion | flops 33562624 | bytes 1343488 | tf_op jit(solution)/shard_map/gvsi,kij->gkvsj/dot_general | solution.py:170
  34.6 1.3 %fusion.22 = f32[256,2,64]{0,2,1:T(8,128)S(1)} fusion(f32[256,2,64]{0,2,1:T(8,128)S(1)} %fusion.28, f32[2,32,2,32,64]{4,1,3,0,2:T(8,128)S(1)} %fusion.44, bf16[2,32,32,256]{3,2,1,0:T(8,128)(2,1)S(1)} %fusion.6, f32[256,64]{0,1:T(8,128)S(1)} %fusion.51), kind=kOutput, calls=%fused_computation.24 | convolution fusion | flops 402718720 | bytes 2424832 | tf_op jit(solution)/shard_map/gkvu,gkvsj->usj/dot_general | solution.py:171
  36.2 9.0 %all_to_all.10 = f32[4,72,128]{2,1,0:T(8,128)S(1)} all-to-all(f32[4,72,128]{2,1,0:T(8,128)S(1)} %pad_maximum_fusion.1), channel_id=1, replica_groups=mesh['parts'=2,'pix'=4,'ang'=2,'sl'=2] {'pix'}, dimensions={0} | all-to-all | bytes 294912 | tf_op jit(solution)/shard_map/all_to_all | solution.py:182
  45.2 0.6 %slice_bitcast_fusion.2 = f32[1,8,512]{2,1,0:T(8,128)} fusion(f32[4,72,128]{2,1,0:T(8,128)S(1)} %all_to_all.10), kind=kLoop, calls=%fused_computation.52 | loop fusion | bytes 32768 | tf_op jit(solution)/shard_map/reshape | solution.py:184
  45.8 0.7 %copy_bitcast_fusion = f32[64,512]{1,0:T(8,128)} fusion(f32[4,72,128]{2,1,0:T(8,128)S(1)} %all_to_all.10), kind=kLoop, calls=%fused_computation.38 | loop fusion | bytes 262144 | tf_op jit(solution)/shard_map/reshape | solution.py:183
  (33 shorter events, 1.9 us)
Async XLA Ops:
  0.6 10.6 %copy-start.1 = (bf16[32,4096]{1,0:T(8,128)(2,1)S(1)}, bf16[32,4096]{1,0:T(8,128)(2,1)}, u32[]{:S(2)}) copy-start(bf16[32,4096]{1,0:T(8,128)(2,1)} %param.7) | copy-start | bytes 786436
  3.9 18.9 %all-to-all-start = ((f32[8,94,128]{2,1,0:T(8,128)}), f32[8,94,128]{2,1,0:T(8,128)S(1)}, u32[]{:S(2)}, u32[]{:S(2)}) async-start(f32[8,94,128]{2,1,0:T(8,128)} %bitcast.5), calls=%async_computation | async-start | bytes 786432 | tf_op jit(solution)/shard_map/all_to_all | solution.py:124
  11.8 20.5 %copy-start = (bf16[32,64,64,1,1]{2,1,0,3,4:T(8,128)(2,1)}, bf16[32,64,64,1,1]{2,1,0,3,4:T(8,128)(2,1)S(1)}, u32[]{:S(2)}) copy-start(bf16[32,64,64,1,1]{2,1,0,3,4:T(8,128)(2,1)S(1)} %reshape.59) | copy-start | bytes 786436

commit v9 on v5

--- a/solution.py
+++ b/solution.py
@@ -160,7 +160,7 @@
         low = cur.astype(jnp.bfloat16)
         gathered = jnp.einsum("gkvu,usj->gkvsj", count_low, low, preferred_element_type=jnp.float32)
         proj = jnp.einsum(
-            "gkvsj,kij->gvsi", gathered, pattern_wide, precision=lax.Precision.HIGH,
+            "gkvsj,kij->gvsi", gathered, pattern_wide, precision=lax.Precision.HIGHEST,
             preferred_element_type=jnp.float32,
         )
         scaled = (meas - proj) / rw

time: 45.2 us -> 45.6 us (level)
  no operation moved by 1% of the time
where the time goes in v9:
time: 45.6 us; the launch traced here: 45.2 us
  blocking collectives  11.9 us (26%)
  matrix products  8.11 us (18%)
  waiting for transfers between devices  7.46 us (16%)
  starting transfers between devices  7.25 us (16%)
  local copies, waits for them, and re-layouts  6.77 us (15%)
  other arithmetic  2.75 us (6%)
  between operations  0.9 us (2%)
    all_to_all x1, blocking collectives, per_device_split(): got_back = lax.all_to_all(back, ('pix', 'ang'), 0, 0, tiled=False)  11.9 us
    all_to_all x1, waiting for transfers between devices, per_device_split(): recv = lax.all_to_all(send, ('pix', 'ang'), 0, 0, tiled=False)  7.46 us
    all_to_all x1, starting transfers between devices, per_device_split(): recv = lax.all_to_all(send, ('pix', 'ang'), 0, 0, tiled=False)  7.25 us
    dot_general x1, matrix products, per_device_split(): jnp.einsum('gkbv,gkbu->gkvu', one_ray, one_pix, preferred_element_type=jn...  3.53 us
    unnamed x6, local copies, waits for them, and re-layouts  3.4 us
    dot_general x2, matrix products, per_device_split(): jnp.einsum('gkvu,gkvsj->usj', counts, spread, precision=lax.Precision.HIG...  1.44 us
    dot_general x2, matrix products, per_device_split(): jnp.einsum('gkvsj,kij->gvsi', gathered, pattern_wide, precision=lax.Preci...  1.29 us
    reshape x2, local copies, waits for them, and re-layouts, per_device_split(): pattern = table.reshape(KINDS, TILE, TILE)  1.07 us
  transfers between devices with their start and end apart: 1, of which 1 were waited for; matrix products, arithmetic and copies ran while one was open for 3% of the time, Pallas kernels for 0%

profile of v9, /device:TPU:0, one launch (start us, length us, event | category | flops | bytes accessed | tf_op | source)
XLA Modules:
  0.0 45.2 jit_solution(8727273011607479611)
XLA Ops:
  0.6 0.7 %add_convert_fusion = f32[2,1408]{1,0:T(2,128)S(1)} fusion(s32[1,1408]{1,0:T(1,128)} %bitcast.136, s32[1,1408]{1,0:T(1,128)} %bitcast.137), kind=kLoop, calls=%fused_computation.43 | loop fusion | flops 5632 | bytes 22528 | tf_op jit(solution)/shard_map/convert_element_type | solution.py:117
  1.5 1.0 %copy.42 = f32[64,512]{0,1:T(8,128)S(1)} copy(f32[64,512]{1,0:T(8,128)} %param.5) | data formatting | bytes 262144 | tf_op args[0]
  2.6 0.9 %copy.43 = f32[1,8,512]{1,2,0:T(8,128)S(1)} copy(f32[1,8,512]{2,1,0:T(8,128)} %param.6) | data formatting | bytes 32768 | tf_op args[1]
  3.5 0.9 %pad_maximum_fusion = f32[8,116,64]{1,2,0:T(8,128)} fusion(f32[8,44,64]{1,2,0:T(8,128)S(1)} %broadcast_in_dim.6, f32[8,8,64]{1,2,0:T(8,128)S(1)} %bitcast.132, f32[8,64,64]{1,2,0:T(8,128)S(1)} %bitcast.131), kind=kLoop, calls=%fused_computation.28 | loop fusion | flops 118784 | bytes 475136 | tf_op jit(solution)/shard_map/concatenate | solution.py:121
  4.4 7.3 %all-to-all-start = ((f32[8,116,64]{1,2,0:T(8,128)}), f32[8,116,64]{1,2,0:T(8,128)S(1)}, u32[]{:S(2)}, u32[]{:S(2)}) async-start(f32[8,116,64]{1,2,0:T(8,128)} %pad_maximum_fusion), calls=%async_computation | async-start | bytes 524288 | tf_op jit(solution)/shard_map/all_to_all | solution.py:122
  11.7 0.5 %reshape.96 = bf16[32,64,64,1]{2,1,0,3:T(8,128)(2,1)S(1)} reshape(bf16[32,4096]{1,0:T(8,128)(2,1)S(1)} %copy-done) | data formatting | bytes 524288 | tf_op jit(solution)/shard_map/reshape | solution.py:146
  12.2 0.5 %reshape.88 = bf16[32,64,64]{2,1,0:T(8,128)(2,1)S(1)} reshape(bf16[32,4096]{1,0:T(8,128)(2,1)S(1)} %copy-done) | data formatting | bytes 524288 | tf_op jit(solution)/shard_map/reshape | solution.py:146
  12.8 0.3 convert_reduce_fusion.2
  13.1 7.5 %all-to-all-done = f32[8,116,64]{1,2,0:T(8,128)S(1)} async-done(((f32[8,116,64]{1,2,0:T(8,128)}), f32[8,116,64]{1,2,0:T(8,128)S(1)}, u32[]{:S(2)}, u32[]{:S(2)}) %all-to-all-start) | async-done | bytes 237600 | tf_op jit(solution)/shard_map/all_to_all | solution.py:122
  22.6 3.5 %fusion.2 = bf16[2,32,32,256]{3,2,1,0:T(8,128)(2,1)S(1)} fusion(s32[2,32,176]{2,1,0:T(8,128)S(1)} %eq.34, s32[2,32,176]{2,1,0:T(8,128)S(1)} %eq.30), kind=kOutput, calls=%fused_computation.6 | convolution fusion | flops 188317696 | bytes 1138688 | tf_op jit(solution)/shard_map/gkbv,gkbu->gkvu/dot_general | solution.py:138
  26.1 0.4 convert_reduce_fusion
  26.6 0.4 fusion.16
  27.0 0.2 fusion.21
  27.2 0.6 %fusion.12 = bf16[2,32,64,1]{2,1,3,0:T(8,128)(2,1)S(1)} fusion(f32[2,32,64]{2,1,0:T(8,128)S(1)} %fusion.21, f32[2,32,32,64]{3,2,1,0:T(8,128)S(1)} %fusion.16, bf16[32,64,64,1]{2,1,0,3:T(8,128)(2,1)S(1)} %reshape.96, f32[2,4,8,64]{3,2,1,0:T(8,128)S(1)} %copy.50), kind=kOutput, calls=%fused_computation.24 | convolution fusion | flops 100675584 | bytes 827392 | tf_op jit(solution)/shard_map/gkvsj,kij->gvsi/dot_general | solution.py:162
  27.9 0.3 convolution_bitcast_fusion.1
  28.1 0.3 fusion.24
  28.4 0.7 %fusion.4 = f32[256,64]{0,1:T(8,128)S(1)} fusion(f32[256,64]{0,1:T(8,128)S(1)} %reshape_reshape_squeeze.3, f32[256,64]{0,1:T(8,128)S(1)} %fusion.24, bf16[2,32,32,256]{3,2,1,0:T(8,128)(2,1)S(1)} %fusion.2, f32[2,32,32,64]{3,2,1,0:T(8,128)S(1)} %convolution_bitcast_fusion.1), kind=kOutput, calls=%fused_computation.16 | convolution fusion | flops 201359360 | bytes 1769472 | tf_op jit(solution)/shard_map/gkvu,gkvsj->usj/dot_general | solution.py:169
  29.1 0.4 fusion.14
  29.5 0.6 %fusion.10 = f32[2,32,64]{2,1,0:T(8,128)S(1)} fusion(f32[2,32,64]{2,1,0:T(8,128)S(1)} %fusion.21, f32[2,32,32,64]{3,2,1,0:T(8,128)S(1)} %fusion.14, bf16[32,64,64,1]{2,1,0,3:T(8,128)(2,1)S(1)} %reshape.96, f32[2,4,8,64]{3,2,1,0:T(8,128)S(1)} %copy.50), kind=kOutput, calls=%fused_computation.22 | convolution fusion | flops 100671488 | bytes 835584 | tf_op jit(solution)/shard_map/gkvsj,kij->gvsi/dot_general | solution.py:162
  30.2 0.3 convolution_bitcast_fusion
  30.6 0.7 %fusion.6 = f32[256,64]{0,1:T(8,128)S(1)} fusion(f32[256,64]{0,1:T(8,128)S(1)} %fusion.4, f32[256,64]{0,1:T(8,128)S(1)} %fusion.24, bf16[2,32,32,256]{3,2,1,0:T(8,128)(2,1)S(1)} %fusion.2, f32[2,32,32,64]{3,2,1,0:T(8,128)S(1)} %convolution_bitcast_fusion), kind=kOutput, calls=%fused_computation.18 | convolution fusion | flops 201359360 | bytes 1769472 | tf_op jit(solution)/shard_map/gkvu,gkvsj->usj/dot_general | solution.py:169
  31.6 11.9 %all_to_all.10 = f32[8,72,64]{1,2,0:T(8,128)S(1)} all-to-all(f32[8,72,64]{1,2,0:T(8,128)S(1)} %bitcast.129), channel_id=1, replica_groups=mesh['parts'=2,'pix'=4,'ang'=2,'sl'=2] {'pix','ang'}, dimensions={0} | all-to-all | bytes 294912 | tf_op jit(solution)/shard_map/all_to_all | solution.py:179
  43.6 0.8 %copy.54 = f32[64,512]{1,0:T(8,128)} copy(f32[64,512]{0,1:T(8,128)S(1)} %bitcast.128) | data formatting | bytes 262144
  44.5 0.7 %copy.55 = f32[1,8,512]{2,1,0:T(8,128)} copy(f32[1,8,512]{1,2,0:T(8,128)S(1)} %bitcast.130) | data formatting | bytes 32768
  (29 shorter events, 2.7 us)
Async XLA Ops:
  2.6 9.1 %copy-start = (bf16[32,4096]{1,0:T(8,128)(2,1)S(1)}, bf16[32,4096]{1,0:T(8,128)(2,1)}, u32[]{:S(2)}) copy-start(bf16[32,4096]{1,0:T(8,128)(2,1)} %param.7) | copy-start | bytes 786436
  4.4 16.2 %all-to-all-start = ((f32[8,116,64]{1,2,0:T(8,128)}), f32[8,116,64]{1,2,0:T(8,128)S(1)}, u32[]{:S(2)}, u32[]{:S(2)}) async-start(f32[8,116,64]{1,2,0:T(8,128)} %pad_maximum_fusion), calls=%async_computation | async-start | bytes 524288 | tf_op jit(solution)/shard_map/all_to_all | solution.py:122

commit v10 on v9

--- a/solution.py
+++ b/solution.py
@@ -114,9 +114,9 @@
 
     vol_send = volume.reshape(tiles_dev, n_grp, width).transpose(1, 0, 2)
     sino_send = sinogram[0].reshape(rays_dev, n_grp, width).transpose(1, 0, 2)
-    lists = jnp.stack([blk_ray.reshape(-1), blk_pix.reshape(-1)]).astype(jnp.float32)
-    list_rows = (2 * nbd + width - 1) // width
-    lists = jnp.pad(lists.reshape(-1), (0, list_rows * width - 2 * nbd)).reshape(list_rows, width)
+    cells = (blk_ray.reshape(-1) * tiles_dev + blk_pix.reshape(-1)).astype(jnp.float32)
+    list_rows = (nbd + width - 1) // width
+    lists = jnp.pad(cells, (0, list_rows * width - nbd)).reshape(list_rows, width)
     list_send = jnp.broadcast_to(lists[None], (n_grp, list_rows, width))
     send = jnp.concatenate([vol_send, sino_send, list_send], axis=1)
     recv = lax.all_to_all(send, ("pix", "ang"), 0, 0, tiled=False)
@@ -124,8 +124,9 @@
 
     current = recv[:, 0, :tiles_dev].reshape(pix_total, width)
     measured = recv[:, :, tiles_dev:tiles_dev + rays_dev].transpose(1, 0, 2, 3).reshape(n_ang, ray_total, width)
-    got = recv[:, :, tiles_dev + rays_dev:].reshape(n_pix, n_ang, -1)[:, :, :2 * nbd]
-    got = got.reshape(n_pix, n_ang, 2, nbd).transpose(2, 1, 0, 3).astype(jnp.int32)
+    cells = recv[:, :, tiles_dev + rays_dev:].reshape(n_pix, n_ang, -1)[:, :, :nbd]
+    cells = cells.transpose(1, 0, 2).astype(jnp.int32)
+    got = jnp.stack([cells // tiles_dev, cells % tiles_dev])
     per_kind = nbd // KINDS
     offsets = (jnp.arange(n_pix, dtype=jnp.int32) * tiles_dev)[None, :, None, None]
     ray_ids = got[0].reshape(n_ang, n_pix, KINDS, per_kind)

time: 45.6 us -> 45.6 us (level)
  no operation moved by 1% of the time
where the time goes in v10:
time: 45.6 us; the launch traced here: 45.2 us
  blocking collectives  11.9 us (26%)
  matrix products  8.1 us (18%)
  waiting for transfers between devices  7.46 us (16%)
  starting transfers between devices  7.25 us (16%)
  local copies, waits for them, and re-layouts  6.56 us (14%)
  other arithmetic  2.93 us (6%)
  between operations  0.91 us (2%)
    all_to_all x1, blocking collectives, per_device_split(): got_back = lax.all_to_all(back, ('pix', 'ang'), 0, 0, tiled=False)  11.9 us
    all_to_all x1, waiting for transfers between devices, per_device_split(): recv = lax.all_to_all(send, ('pix', 'ang'), 0, 0, tiled=False)  7.46 us
    all_to_all x1, starting transfers between devices, per_device_split(): recv = lax.all_to_all(send, ('pix', 'ang'), 0, 0, tiled=False)  7.25 us
    dot_general x1, matrix products, per_device_split(): jnp.einsum('gkbv,gkbu->gkvu', one_ray, one_pix, preferred_element_type=jn...  3.53 us
    unnamed x6, local copies, waits for them, and re-layouts  3.4 us
    dot_general x2, matrix products, per_device_split(): jnp.einsum('gkvu,gkvsj->usj', counts, spread, precision=lax.Precision.HIG...  1.44 us
    dot_general x2, matrix products, per_device_split(): jnp.einsum('gkvsj,kij->gvsi', gathered, pattern_wide, precision=lax.Preci...  1.29 us
    reshape x2, local copies, waits for them, and re-layouts, per_device_split(): pattern = table.reshape(KINDS, TILE, TILE)  1.07 us
  transfers between devices with their start and end apart: 1, of which 1 were waited for; matrix products, arithmetic and copies ran while one was open for 3% of the time, Pallas kernels for 0%

profile of v10, /device:TPU:0, one launch (start us, length us, event | category | flops | bytes accessed | tf_op | source)
XLA Modules:
  0.0 45.2 jit_solution(1857887784203222694)
XLA Ops:
  0.6 0.7 %convert_reduce_fusion.4 = f32[1408]{0:T(1024)S(1)} fusion(s32[1,1,1408]{2,1,0:T(1,128)} %param.9, s32[1,1,1408]{2,1,0:T(1,128)} %param.8), kind=kLoop, calls=%fused_computation.50 | loop fusion | flops 4224 | bytes 16896 | tf_op jit(solution)/shard_map/convert_element_type | solution.py:117
  1.5 1.0 %copy.43 = f32[64,512]{0,1:T(8,128)S(1)} copy(f32[64,512]{1,0:T(8,128)} %param.5) | data formatting | bytes 262144 | tf_op args[0]
  2.6 0.9 %copy.44 = f32[1,8,512]{1,2,0:T(8,128)S(1)} copy(f32[1,8,512]{2,1,0:T(8,128)} %param.6) | data formatting | bytes 32768 | tf_op args[1]
  3.5 0.9 %pad_maximum_fusion = f32[8,94,64]{1,2,0:T(8,128)} fusion(f32[8,22,64]{1,2,0:T(8,128)S(1)} %broadcast_in_dim.6, f32[8,8,64]{1,2,0:T(8,128)S(1)} %bitcast.149, f32[8,64,64]{1,2,0:T(8,128)S(1)} %bitcast.148), kind=kLoop, calls=%fused_computation.28 | loop fusion | flops 96256 | bytes 385024 | tf_op jit(solution)/shard_map/concatenate | solution.py:121
  4.4 7.3 %all-to-all-start = ((f32[8,94,64]{1,2,0:T(8,128)}), f32[8,94,64]{1,2,0:T(8,128)S(1)}, u32[]{:S(2)}, u32[]{:S(2)}) async-start(f32[8,94,64]{1,2,0:T(8,128)} %pad_maximum_fusion), calls=%async_computation | async-start | bytes 524288 | tf_op jit(solution)/shard_map/all_to_all | solution.py:122
  11.7 0.5 %reshape.106 = bf16[32,64,64,1]{2,1,0,3:T(8,128)(2,1)S(1)} reshape(bf16[32,4096]{1,0:T(8,128)(2,1)S(1)} %copy-done) | data formatting | bytes 524288 | tf_op jit(solution)/shard_map/reshape | solution.py:147
  12.2 0.5 %reshape.98 = bf16[32,64,64]{2,1,0:T(8,128)(2,1)S(1)} reshape(bf16[32,4096]{1,0:T(8,128)(2,1)S(1)} %copy-done) | data formatting | bytes 524288 | tf_op jit(solution)/shard_map/reshape | solution.py:147
  12.8 0.3 convert_reduce_fusion.2
  13.1 7.5 %all-to-all-done = f32[8,94,64]{1,2,0:T(8,128)S(1)} async-done(((f32[8,94,64]{1,2,0:T(8,128)}), f32[8,94,64]{1,2,0:T(8,128)S(1)}, u32[]{:S(2)}, u32[]{:S(2)}) %all-to-all-start) | async-done | bytes 192544 | tf_op jit(solution)/shard_map/all_to_all | solution.py:122
  22.6 3.5 %fusion.2 = bf16[2,32,32,256]{3,2,1,0:T(8,128)(2,1)S(1)} fusion(s32[2,32,176]{2,1,0:T(8,128)S(1)} %eq.36, s32[2,32,176]{2,1,0:T(8,128)S(1)} %eq.32), kind=kOutput, calls=%fused_computation.6 | convolution fusion | flops 188317696 | bytes 1138688 | tf_op jit(solution)/shard_map/gkbv,gkbu->gkvu/dot_general | solution.py:139
  26.1 0.4 convert_reduce_fusion
  26.5 0.4 fusion.16
  26.9 0.2 fusion.21
  27.2 0.6 %fusion.12 = bf16[2,32,64,1]{2,1,3,0:T(8,128)(2,1)S(1)} fusion(f32[2,32,64]{2,1,0:T(8,128)S(1)} %fusion.21, f32[2,32,32,64]{3,2,1,0:T(8,128)S(1)} %fusion.16, bf16[32,64,64,1]{2,1,0,3:T(8,128)(2,1)S(1)} %reshape.106, f32[2,4,8,64]{3,2,1,0:T(8,128)S(1)} %copy.52), kind=kOutput, calls=%fused_computation.24 | convolution fusion | flops 100675584 | bytes 827392 | tf_op jit(solution)/shard_map/gkvsj,kij->gvsi/dot_general | solution.py:163
  27.8 0.3 convolution_bitcast_fusion.1
  28.1 0.3 fusion.24
  28.4 0.7 %fusion.4 = f32[256,64]{0,1:T(8,128)S(1)} fusion(f32[256,64]{0,1:T(8,128)S(1)} %reshape_reshape_squeeze.3, f32[256,64]{0,1:T(8,128)S(1)} %fusion.24, bf16[2,32,32,256]{3,2,1,0:T(8,128)(2,1)S(1)} %fusion.2, f32[2,32,32,64]{3,2,1,0:T(8,128)S(1)} %convolution_bitcast_fusion.1), kind=kOutput, calls=%fused_computation.16 | convolution fusion | flops 201359360 | bytes 1769472 | tf_op jit(solution)/shard_map/gkvu,gkvsj->usj/dot_general | solution.py:170
  29.1 0.4 fusion.14
  29.5 0.6 %fusion.10 = f32[2,32,64]{2,1,0:T(8,128)S(1)} fusion(f32[2,32,64]{2,1,0:T(8,128)S(1)} %fusion.21, f32[2,32,32,64]{3,2,1,0:T(8,128)S(1)} %fusion.14, bf16[32,64,64,1]{2,1,0,3:T(8,128)(2,1)S(1)} %reshape.106, f32[2,4,8,64]{3,2,1,0:T(8,128)S(1)} %copy.52), kind=kOutput, calls=%fused_computation.22 | convolution fusion | flops 100671488 | bytes 835584 | tf_op jit(solution)/shard_map/gkvsj,kij->gvsi/dot_general | solution.py:163
  30.2 0.3 convolution_bitcast_fusion
  30.6 0.7 %fusion.6 = f32[256,64]{0,1:T(8,128)S(1)} fusion(f32[256,64]{0,1:T(8,128)S(1)} %fusion.4, f32[256,64]{0,1:T(8,128)S(1)} %fusion.24, bf16[2,32,32,256]{3,2,1,0:T(8,128)(2,1)S(1)} %fusion.2, f32[2,32,32,64]{3,2,1,0:T(8,128)S(1)} %convolution_bitcast_fusion), kind=kOutput, calls=%fused_computation.18 | convolution fusion | flops 201359360 | bytes 1769472 | tf_op jit(solution)/shard_map/gkvu,gkvsj->usj/dot_general | solution.py:170
  31.6 11.9 %all_to_all.10 = f32[8,72,64]{1,2,0:T(8,128)S(1)} all-to-all(f32[8,72,64]{1,2,0:T(8,128)S(1)} %bitcast.146), channel_id=1, replica_groups=mesh['parts'=2,'pix'=4,'ang'=2,'sl'=2] {'pix','ang'}, dimensions={0} | all-to-all | bytes 294912 | tf_op jit(solution)/shard_map/all_to_all | solution.py:180
  43.6 0.8 %copy.56 = f32[64,512]{1,0:T(8,128)} copy(f32[64,512]{0,1:T(8,128)S(1)} %bitcast.145) | data formatting | bytes 262144
  44.5 0.7 %copy.57 = f32[1,8,512]{2,1,0:T(8,128)} copy(f32[1,8,512]{1,2,0:T(8,128)S(1)} %bitcast.147) | data formatting | bytes 32768
  (29 shorter events, 2.6 us)
Async XLA Ops:
  2.6 9.1 %copy-start = (bf16[32,4096]{1,0:T(8,128)(2,1)S(1)}, bf16[32,4096]{1,0:T(8,128)(2,1)}, u32[]{:S(2)}) copy-start(bf16[32,4096]{1,0:T(8,128)(2,1)} %param.7) | copy-start | bytes 786436
  4.4 16.2 %all-to-all-start = ((f32[8,94,64]{1,2,0:T(8,128)}), f32[8,94,64]{1,2,0:T(8,128)S(1)}, u32[]{:S(2)}, u32[]{:S(2)}) async-start(f32[8,94,64]{1,2,0:T(8,128)} %pad_maximum_fusion), calls=%async_computation | async-start | bytes 524288 | tf_op jit(solution)/shard_map/all_to_all | solution.py:122

commit v11 on v9

--- a/solution.py
+++ b/solution.py
@@ -140,36 +140,38 @@
     ).astype(jnp.bfloat16)
     count_low = lax.optimization_barrier(count_low)
     counts = count_low.astype(jnp.float32)
-    ray_count = jnp.sum(counts, axis=3)
-    pix_count = jnp.sum(counts, axis=2)
-
     pattern = table.reshape(KINDS, TILE, TILE)
     pattern_wide = pattern.astype(jnp.float32)
-    hi = lax.Precision.HIGHEST
-    ray_weight = jnp.einsum("gkv,ki->gvi", ray_count, jnp.sum(pattern_wide, axis=2), precision=hi)
-    pixel_weight = jnp.einsum("gku,kj->uj", pix_count, jnp.sum(pattern_wide, axis=1), precision=hi)
-    ray_weight = jnp.tile(ray_weight, (1, 1, per_dev))
-    pixel_weight = jnp.tile(pixel_weight, (1, per_dev))
 
     cur = current.reshape(pix_total, per_dev, TILE)
     meas = measured.reshape(n_ang, ray_total, per_dev, TILE)
-    rw = ray_weight.reshape(n_ang, ray_total, per_dev, TILE)
-    pw = pixel_weight.reshape(pix_total, per_dev, TILE)
+    ones_pix = jnp.ones((pix_total, 1, TILE), jnp.bfloat16)
+    ones_ray = jnp.ones((n_ang, ray_total, 1, TILE), jnp.bfloat16)
     scaled = meas
     for iteration in range(ITERS):
         low = cur.astype(jnp.bfloat16)
+        if iteration == 0:
+            low = jnp.concatenate([low, ones_pix], axis=1)
         gathered = jnp.einsum("gkvu,usj->gkvsj", count_low, low, preferred_element_type=jnp.float32)
         proj = jnp.einsum(
             "gkvsj,kij->gvsi", gathered, pattern_wide, precision=lax.Precision.HIGHEST,
             preferred_element_type=jnp.float32,
         )
+        if iteration == 0:
+            rw = jnp.broadcast_to(proj[:, :, per_dev:], meas.shape)
+            proj = proj[:, :, :per_dev]
         scaled = (meas - proj) / rw
         scaled_low = scaled.astype(jnp.bfloat16)
+        if iteration == 0:
+            scaled_low = jnp.concatenate([scaled_low, ones_ray], axis=2)
         spread = jnp.einsum("gvsi,kij->gkvsj", scaled_low, pattern, preferred_element_type=jnp.float32)
         update = jnp.einsum(
             "gkvu,gkvsj->usj", counts, spread, precision=lax.Precision.HIGH,
             preferred_element_type=jnp.float32,
         )
+        if iteration == 0:
+            pw = jnp.broadcast_to(update[:, per_dev:], cur.shape)
+            update = update[:, :per_dev]
         cur = cur + update / pw
 
     vol_back = cur.reshape(n_pix, tiles_dev, width)

time: 45.6 us -> 45.9 us (level)
  matrix products: 8.11 us -> 8.85 us
  other arithmetic: 2.75 us -> 2.06 us
    reduce_sum x2 -> x0, other arithmetic: 0.78 us -> none  [the longest x1 0.43 us: per_device_split(): jnp.einsum('gku,kj->uj', pix_count, jnp.sum(pattern_wide, axis=1), precis...]
    dot_general x2, matrix products: 1.44 us -> 2 us  [per_device_split(): jnp.einsum('gkvu,gkvsj->usj', counts, spread, precision=lax.Precision.HIG...]
    dot_general x2 -> x0, matrix products: 0.49 us -> none  [the longest x1 0.25 us: per_device_split(): jnp.einsum('gku,kj->uj', pix_count, jnp.sum(pattern_wide, axis=1), precis...]
    dot_general x2, matrix products: 1.29 us -> 1.77 us  [per_device_split(): jnp.einsum('gkvsj,kij->gvsi', gathered, pattern_wide, precision=lax.Preci...]
  transfers between devices with their start and end apart: 1 -> 1, of which waited for: 1 -> 1; matrix products, arithmetic and copies ran while one was open for 3% -> 2% of each run, Pallas kernels for 0% -> 0%
where the time goes in v11:
time: 45.9 us; the launch traced here: 45.5 us
  blocking collectives  11.9 us (26%)
  matrix products  8.85 us (19%)
  waiting for transfers between devices  7.81 us (17%)
  starting transfers between devices  7.25 us (16%)
  local copies, waits for them, and re-layouts  6.73 us (15%)
  other arithmetic  2.06 us (4%)
  between operations  0.89 us (2%)
    all_to_all x1, blocking collectives, per_device_split(): got_back = lax.all_to_all(back, ('pix', 'ang'), 0, 0, tiled=False)  11.9 us
    all_to_all x1, waiting for transfers between devices, per_device_split(): recv = lax.all_to_all(send, ('pix', 'ang'), 0, 0, tiled=False)  7.81 us
    all_to_all x1, starting transfers between devices, per_device_split(): recv = lax.all_to_all(send, ('pix', 'ang'), 0, 0, tiled=False)  7.25 us
    dot_general x1, matrix products, per_device_split(): jnp.einsum('gkbv,gkbu->gkvu', one_ray, one_pix, preferred_element_type=jn...  3.53 us
    unnamed x6, local copies, waits for them, and re-layouts  3.36 us
    dot_general x2, matrix products, per_device_split(): jnp.einsum('gkvu,gkvsj->usj', counts, spread, precision=lax.Precision.HIG...  2 us
    dot_general x2, matrix products, per_device_split(): jnp.einsum('gkvsj,kij->gvsi', gathered, pattern_wide, precision=lax.Preci...  1.77 us
    reshape x2, local copies, waits for them, and re-layouts, per_device_split(): pattern = table.reshape(KINDS, TILE, TILE)  1.07 us
  transfers between devices with their start and end apart: 1, of which 1 were waited for; matrix products, arithmetic and copies ran while one was open for 2% of the time, Pallas kernels for 0%

profile of v11, /device:TPU:0, one launch (start us, length us, event | category | flops | bytes accessed | tf_op | source)
XLA Modules:
  0.0 45.5 jit_solution(12239807773968916416)
XLA Ops:
  0.6 0.8 %add_convert_fusion = f32[2,1408]{1,0:T(2,128)S(1)} fusion(s32[1,1408]{1,0:T(1,128)} %bitcast.136, s32[1,1408]{1,0:T(1,128)} %bitcast.137), kind=kLoop, calls=%fused_computation.44 | loop fusion | flops 5632 | bytes 22528 | tf_op jit(solution)/shard_map/convert_element_type | solution.py:117
  1.6 1.0 %copy.48 = f32[64,512]{0,1:T(8,128)S(1)} copy(f32[64,512]{1,0:T(8,128)} %param.5) | data formatting | bytes 262144 | tf_op args[0]
  2.6 0.8 %copy.49 = f32[1,8,512]{1,2,0:T(8,128)S(1)} copy(f32[1,8,512]{2,1,0:T(8,128)} %param.6) | data formatting | bytes 32768 | tf_op args[1]
  3.5 0.9 %pad_maximum_fusion = f32[8,116,64]{1,2,0:T(8,128)} fusion(f32[8,44,64]{1,2,0:T(8,128)S(1)} %broadcast_in_dim.6, f32[8,8,64]{1,2,0:T(8,128)S(1)} %bitcast.132, f32[8,64,64]{1,2,0:T(8,128)S(1)} %bitcast.131), kind=kLoop, calls=%fused_computation.24 | loop fusion | flops 118784 | bytes 475136 | tf_op jit(solution)/shard_map/concatenate | solution.py:121
  4.4 7.3 %all-to-all-start = ((f32[8,116,64]{1,2,0:T(8,128)}), f32[8,116,64]{1,2,0:T(8,128)S(1)}, u32[]{:S(2)}, u32[]{:S(2)}) async-start(f32[8,116,64]{1,2,0:T(8,128)} %pad_maximum_fusion), calls=%async_computation | async-start | bytes 524288 | tf_op jit(solution)/shard_map/all_to_all | solution.py:122
  11.7 0.5 %reshape.82 = bf16[32,64,64,1,1]{2,1,0,3,4:T(8,128)(2,1)S(1)} reshape(bf16[32,4096]{1,0:T(8,128)(2,1)S(1)} %copy-done) | data formatting | bytes 524288 | tf_op jit(solution)/shard_map/reshape | solution.py:143
  12.2 0.5 %reshape.87 = bf16[32,64,64,1]{2,1,0,3:T(8,128)(2,1)S(1)} reshape(bf16[32,4096]{1,0:T(8,128)(2,1)S(1)} %copy-done) | data formatting | bytes 524288 | tf_op jit(solution)/shard_map/reshape | solution.py:143
  12.8 7.8 %all-to-all-done = f32[8,116,64]{1,2,0:T(8,128)S(1)} async-done(((f32[8,116,64]{1,2,0:T(8,128)}), f32[8,116,64]{1,2,0:T(8,128)S(1)}, u32[]{:S(2)}, u32[]{:S(2)}) %all-to-all-start) | async-done | bytes 237600 | tf_op jit(solution)/shard_map/all_to_all | solution.py:122
  20.9 0.2 copy.52
  21.2 0.2 slice_reduce_fusion
  21.3 0.2 reshape_squeeze.11
  21.8 0.2 reshape_squeeze.10
  22.2 3.5 %fusion.4 = bf16[2,32,32,256]{3,2,1,0:T(8,128)(2,1)S(1)} fusion(s32[2,32,176]{2,1,0:T(8,128)S(1)} %eq.34, s32[2,32,176]{2,1,0:T(8,128)S(1)} %eq.30), kind=kOutput, calls=%fused_computation.6 | convolution fusion | flops 188317696 | bytes 1138688 | tf_op jit(solution)/shard_map/gkbv,gkbu->gkvu/dot_general | solution.py:138
  26.1 0.5 fusion.14
  26.6 1.1 %convolution_bitcast_fusion.2 = f32[2,32,2,64]{3,1,2,0:T(8,128)S(1)} fusion(f32[2,32,32,2,64]{4,2,1,3,0:T(8,128)S(1)} %fusion.14, bf16[32,64,64,1,1]{2,1,0,3,4:T(8,128)(2,1)S(1)} %reshape.82), kind=kOutput, calls=%fused_computation.10 | convolution fusion | flops 201326592 | bytes 1343488 | tf_op jit(solution)/shard_map/gkvsj,kij->gvsi/dot_general | solution.py:156
  27.7 0.4 fusion.25
  28.2 1.3 %fusion.5 = f32[256,2,64]{0,2,1:T(8,128)S(1)} fusion(f32[2,32,2,32,64]{4,1,3,0,2:T(8,128)S(1)} %fusion.25, bf16[2,32,32,256]{3,2,1,0:T(8,128)(2,1)S(1)} %fusion.4), kind=kOutput, calls=%fused_computation.8 | convolution fusion | flops 402653184 | bytes 2228224 | tf_op jit(solution)/shard_map/gkvu,gkvsj->usj/dot_general | solution.py:168
  29.5 0.4 fusion.23
  29.9 0.6 %fusion.12 = f32[2,32,1,64]{3,1,2,0:T(8,128)S(1)} fusion(f32[2,32,32,64]{3,2,1,0:T(8,128)S(1)} %fusion.23, bf16[32,64,64,1]{2,1,0,3:T(8,128)(2,1)S(1)} %reshape.87, f32[2,4,8,64]{3,2,1,0:T(8,128)S(1)} %copy.56, f32[2,32,2,64]{3,1,2,0:T(8,128)S(1)} %convolution_bitcast_fusion.2), kind=kOutput, calls=%fused_computation.16 | convolution fusion | flops 100671488 | bytes 835584 | tf_op jit(solution)/shard_map/gkvsj,kij->gvsi/dot_general | solution.py:156
  30.5 0.3 convolution_bitcast_fusion
  30.8 0.7 %fusion.9 = f32[256,1,64]{0,2,1:T(8,128)S(1)} fusion(f32[256,1,64]{0,2,1:T(8,128)S(1)} %fusion.18, bf16[2,32,32,256]{3,2,1,0:T(8,128)(2,1)S(1)} %fusion.4, f32[2,32,32,64]{3,2,1,0:T(8,128)S(1)} %convolution_bitcast_fusion, f32[256,2,64]{0,2,1:T(8,128)S(1)} %fusion.5), kind=kOutput, calls=%fused_computation.13 | convolution fusion | flops 201359360 | bytes 1769472 | tf_op jit(solution)/shard_map/gkvu,gkvsj->usj/dot_general | solution.py:168
  32.0 11.9 %all_to_all.10 = f32[8,72,64]{1,2,0:T(8,128)S(1)} all-to-all(f32[8,72,64]{1,2,0:T(8,128)S(1)} %bitcast.129), channel_id=1, replica_groups=mesh['parts'=2,'pix'=4,'ang'=2,'sl'=2] {'pix','ang'}, dimensions={0} | all-to-all | bytes 294912 | tf_op jit(solution)/shard_map/all_to_all | solution.py:181
  44.1 0.7 %copy.63 = f32[1,8,512]{2,1,0:T(8,128)} copy(f32[1,8,512]{1,2,0:T(8,128)S(1)} %bitcast.130) | data formatting | bytes 32768
  44.8 0.8 %copy.62 = f32[64,512]{1,0:T(8,128)} copy(f32[64,512]{0,1:T(8,128)S(1)} %bitcast.128) | data formatting | bytes 262144
  (28 shorter events, 2.0 us)
Async XLA Ops:
  0.6 11.0 %copy-start = (bf16[32,4096]{1,0:T(8,128)(2,1)S(1)}, bf16[32,4096]{1,0:T(8,128)(2,1)}, u32[]{:S(2)}) copy-start(bf16[32,4096]{1,0:T(8,128)(2,1)} %param.7) | copy-start | bytes 786436
  4.4 16.2 %all-to-all-start = ((f32[8,116,64]{1,2,0:T(8,128)}), f32[8,116,64]{1,2,0:T(8,128)S(1)}, u32[]{:S(2)}, u32[]{:S(2)}) async-start(f32[8,116,64]{1,2,0:T(8,128)} %pad_maximum_fusion), calls=%async_computation | async-start | bytes 524288 | tf_op jit(solution)/shard_map/all_to_all | solution.py:122

commit v12 on v9

--- a/solution.py
+++ b/solution.py
@@ -114,9 +114,12 @@
 
     vol_send = volume.reshape(tiles_dev, n_grp, width).transpose(1, 0, 2)
     sino_send = sinogram[0].reshape(rays_dev, n_grp, width).transpose(1, 0, 2)
+    per_kind = nbd // KINDS
     lists = jnp.stack([blk_ray.reshape(-1), blk_pix.reshape(-1)]).astype(jnp.float32)
-    list_rows = (2 * nbd + width - 1) // width
-    lists = jnp.pad(lists.reshape(-1), (0, list_rows * width - 2 * nbd)).reshape(list_rows, width)
+    lists = lists.reshape(2, KINDS, per_kind)
+    lists = jnp.pad(lists, ((0, 0), (0, 0), (0, width - per_kind)), constant_values=-1.0)
+    list_rows = 2 * KINDS
+    lists = lists.reshape(list_rows, width)
     list_send = jnp.broadcast_to(lists[None], (n_grp, list_rows, width))
     send = jnp.concatenate([vol_send, sino_send, list_send], axis=1)
     recv = lax.all_to_all(send, ("pix", "ang"), 0, 0, tiled=False)
@@ -124,17 +127,13 @@
 
     current = recv[:, 0, :tiles_dev].reshape(pix_total, width)
     measured = recv[:, :, tiles_dev:tiles_dev + rays_dev].transpose(1, 0, 2, 3).reshape(n_ang, ray_total, width)
-    got = recv[:, :, tiles_dev + rays_dev:].reshape(n_pix, n_ang, -1)[:, :, :2 * nbd]
-    got = got.reshape(n_pix, n_ang, 2, nbd).transpose(2, 1, 0, 3).astype(jnp.int32)
-    per_kind = nbd // KINDS
-    offsets = (jnp.arange(n_pix, dtype=jnp.int32) * tiles_dev)[None, :, None, None]
-    ray_ids = got[0].reshape(n_ang, n_pix, KINDS, per_kind)
-    pix_ids = got[1].reshape(n_ang, n_pix, KINDS, per_kind) + offsets
-    ray_ids = ray_ids.transpose(0, 2, 1, 3).reshape(n_ang, KINDS, n_pix * per_kind)
-    pix_ids = pix_ids.transpose(0, 2, 1, 3).reshape(n_ang, KINDS, n_pix * per_kind)
-
-    one_ray = (ray_ids[..., None] == jnp.arange(ray_total, dtype=jnp.int32)).astype(jnp.bfloat16)
-    one_pix = (pix_ids[..., None] == jnp.arange(pix_total, dtype=jnp.int32)).astype(jnp.bfloat16)
+    got = recv[:, :, tiles_dev + rays_dev:].reshape(n_pix, n_ang, 2, KINDS, width)[..., :per_kind]
+    offsets = (jnp.arange(n_pix, dtype=jnp.float32) * tiles_dev)[:, None, None, None]
+    ray_ids = got[:, :, 0].transpose(1, 2, 0, 3).reshape(n_ang, KINDS, n_pix * per_kind)
+    pix_ids = (got[:, :, 1] + offsets).transpose(1, 2, 0, 3).reshape(n_ang, KINDS, n_pix * per_kind)
+
+    one_ray = (ray_ids[..., None] == jnp.arange(ray_total, dtype=jnp.float32)).astype(jnp.bfloat16)
+    one_pix = (pix_ids[..., None] == jnp.arange(pix_total, dtype=jnp.float32)).astype(jnp.bfloat16)
     count_low = jnp.einsum(
         "gkbv,gkbu->gkvu", one_ray, one_pix, preferred_element_type=jnp.float32
     ).astype(jnp.bfloat16)

time: 45.6 us -> 51.4 us (1.13)
  waiting for transfers between devices: 7.46 us -> 13 us
  other arithmetic: 2.75 us -> 3.56 us
  matrix products: 8.11 us -> 7.37 us
  blocking collectives: 11.9 us -> 12.5 us
    all_to_all x1, waiting for transfers between devices: 7.46 us -> 13 us  [per_device_split(): recv = lax.all_to_all(send, ('pix', 'ang'), 0, 0, tiled=False)]
    unnamed x0 -> x2, other arithmetic: none -> 1.43 us
    dot_general x1, matrix products: 3.53 us -> 2.8 us  [per_device_split(): jnp.einsum('gkbv,gkbu->gkvu', one_ray, one_pix, preferred_element_type=jn...]
    convert_element_type x1, other arithmetic: 0.72 us -> 0.01 us  [per_device_split(): jnp.stack([blk_ray.reshape(-1), blk_pix.reshape(-1)]).astype(jnp.float32)]
    all_to_all x1, blocking collectives: 11.9 us -> 12.5 us  [per_device_split(): got_back = lax.all_to_all(back, ('pix', 'ang'), 0, 0, tiled=False)]
where the time goes in v12:
time: 51.4 us; the launch traced here: 50.9 us
  waiting for transfers between devices  13 us (25%)
  blocking collectives  12.5 us (24%)
  matrix products  7.37 us (14%)
  starting transfers between devices  7.25 us (14%)
  local copies, waits for them, and re-layouts  6.28 us (12%)
  other arithmetic  3.56 us (7%)
  between operations  0.91 us (2%)
    all_to_all x1, waiting for transfers between devices, per_device_split(): recv = lax.all_to_all(send, ('pix', 'ang'), 0, 0, tiled=False)  13 us
    all_to_all x1, blocking collectives, per_device_split(): got_back = lax.all_to_all(back, ('pix', 'ang'), 0, 0, tiled=False)  12.5 us
    all_to_all x1, starting transfers between devices, per_device_split(): recv = lax.all_to_all(send, ('pix', 'ang'), 0, 0, tiled=False)  7.25 us
    unnamed x6, local copies, waits for them, and re-layouts  3.37 us
    dot_general x1, matrix products, per_device_split(): jnp.einsum('gkbv,gkbu->gkvu', one_ray, one_pix, preferred_element_type=jn...  2.8 us
    dot_general x2, matrix products, per_device_split(): jnp.einsum('gkvu,gkvsj->usj', counts, spread, precision=lax.Precision.HIG...  1.44 us
    unnamed x2, other arithmetic  1.43 us
    dot_general x2, matrix products, per_device_split(): jnp.einsum('gkvsj,kij->gvsi', gathered, pattern_wide, precision=lax.Preci...  1.29 us
  transfers between devices with their start and end apart: 1, of which 1 were waited for; matrix products, arithmetic and copies ran while one was open for 3% of the time, Pallas kernels for 0%

profile of v12, /device:TPU:0, one launch (start us, length us, event | category | flops | bytes accessed | tf_op | source)
XLA Modules:
  0.0 50.9 jit_solution(16387532025022790556)
XLA Ops:
  0.6 0.7 %reduce.1 = s32[1408]{0:T(1024)S(1)} reduce(s32[1,1,1408]{2,1,0:T(1,128)} %param.8, s32[]{:T(128)} %constant.11), dimensions={0,1}, to_apply=%param.8.reduce_sub_computation | reduce | bytes 11268 | tf_op args[3]
  1.4 0.7 %reduce.2 = s32[1408]{0:T(1024)S(1)} reduce(s32[1,1,1408]{2,1,0:T(1,128)} %param.9, s32[]{:T(128)} %constant.11), dimensions={0,1}, to_apply=%param.9.reduce_sub_computation | reduce | bytes 11268 | tf_op args[4]
  2.4 1.0 %copy.29 = f32[64,512]{0,1:T(8,128)S(1)} copy(f32[64,512]{1,0:T(8,128)} %param.5) | data formatting | bytes 262144 | tf_op args[0]
  3.4 0.8 %copy.30 = f32[1,8,512]{1,2,0:T(8,128)S(1)} copy(f32[1,8,512]{2,1,0:T(8,128)} %param.6) | data formatting | bytes 32768 | tf_op args[1]
  4.3 1.1 %pad_maximum_fusion = f32[8,136,64]{1,2,0:T(8,128)} fusion(f32[8,64,64]{1,2,0:T(8,128)S(1)} %broadcast_in_dim.18, f32[8,8,64]{1,2,0:T(8,128)S(1)} %bitcast.134, f32[8,64,64]{1,2,0:T(8,128)S(1)} %bitcast.133), kind=kLoop, calls=%fused_computation.26 | loop fusion | flops 139264 | bytes 557056 | tf_op jit(solution)/shard_map/concatenate | solution.py:124
  5.4 7.3 %all-to-all-start = ((f32[8,136,64]{1,2,0:T(8,128)}), f32[8,136,64]{1,2,0:T(8,128)S(1)}, u32[]{:S(2)}, u32[]{:S(2)}) async-start(f32[8,136,64]{1,2,0:T(8,128)} %pad_maximum_fusion), calls=%async_computation | async-start | bytes 1048576 | tf_op jit(solution)/shard_map/all_to_all | solution.py:125
  12.7 0.5 %reshape.97 = bf16[32,64,64,1]{2,1,0,3:T(8,128)(2,1)S(1)} reshape(bf16[32,4096]{1,0:T(8,128)(2,1)S(1)} %copy-done) | data formatting | bytes 524288 | tf_op jit(solution)/shard_map/reshape | solution.py:145
  13.2 0.5 %reshape.89 = bf16[32,64,64]{2,1,0:T(8,128)(2,1)S(1)} reshape(bf16[32,4096]{1,0:T(8,128)(2,1)S(1)} %copy-done) | data formatting | bytes 524288 | tf_op jit(solution)/shard_map/reshape | solution.py:145
  13.8 0.3 convert_reduce_fusion.2
  14.1 13.0 %all-to-all-done = f32[8,136,64]{1,2,0:T(8,128)S(1)} async-done(((f32[8,136,64]{1,2,0:T(8,128)}), f32[8,136,64]{1,2,0:T(8,128)S(1)}, u32[]{:S(2)}, u32[]{:S(2)}) %all-to-all-start) | async-done | bytes 278560 | tf_op jit(solution)/shard_map/all_to_all | solution.py:125
  28.5 2.8 %fusion.2 = bf16[2,32,32,256]{3,2,1,0:T(8,128)(2,1)S(1)} fusion(f32[2,32,176]{2,1,0:T(8,128)S(1)} %eq.34, f32[2,32,176]{2,1,0:T(8,128)S(1)} %eq.30), kind=kOutput, calls=%fused_computation.6 | convolution fusion | flops 188317696 | bytes 1138688 | tf_op jit(solution)/shard_map/gkbv,gkbu->gkvu/dot_general | solution.py:137
  31.3 0.4 convert_reduce_fusion
  31.7 0.4 fusion.18
  32.4 0.6 %fusion.12 = bf16[2,32,64,1]{2,1,3,0:T(8,128)(2,1)S(1)} fusion(f32[2,32,64]{2,1,0:T(8,128)S(1)} %fusion.23, f32[2,32,32,64]{3,2,1,0:T(8,128)S(1)} %fusion.18, bf16[32,64,64,1]{2,1,0,3:T(8,128)(2,1)S(1)} %reshape.97, f32[2,4,8,64]{3,2,1,0:T(8,128)S(1)} %copy.36), kind=kOutput, calls=%fused_computation.24 | convolution fusion | flops 100675584 | bytes 827392 | tf_op jit(solution)/shard_map/gkvsj,kij->gvsi/dot_general | solution.py:161
  33.0 0.3 convolution_bitcast_fusion.1
  33.3 0.3 fusion.26
  33.6 0.7 %fusion.4 = f32[256,64]{0,1:T(8,128)S(1)} fusion(f32[256,64]{0,1:T(8,128)S(1)} %reshape_reshape_squeeze.3, f32[256,64]{0,1:T(8,128)S(1)} %fusion.26, bf16[2,32,32,256]{3,2,1,0:T(8,128)(2,1)S(1)} %fusion.2, f32[2,32,32,64]{3,2,1,0:T(8,128)S(1)} %convolution_bitcast_fusion.1), kind=kOutput, calls=%fused_computation.16 | convolution fusion | flops 201359360 | bytes 1769472 | tf_op jit(solution)/shard_map/gkvu,gkvsj->usj/dot_general | solution.py:168
  34.3 0.4 fusion.16
  34.7 0.6 %fusion.10 = f32[2,32,64]{2,1,0:T(8,128)S(1)} fusion(f32[2,32,64]{2,1,0:T(8,128)S(1)} %fusion.23, f32[2,32,32,64]{3,2,1,0:T(8,128)S(1)} %fusion.16, bf16[32,64,64,1]{2,1,0,3:T(8,128)(2,1)S(1)} %reshape.97, f32[2,4,8,64]{3,2,1,0:T(8,128)S(1)} %copy.36), kind=kOutput, calls=%fused_computation.22 | convolution fusion | flops 100671488 | bytes 835584 | tf_op jit(solution)/shard_map/gkvsj,kij->gvsi/dot_general | solution.py:161
  35.4 0.3 convolution_bitcast_fusion
  35.8 0.7 %fusion.6 = f32[256,64]{0,1:T(8,128)S(1)} fusion(f32[256,64]{0,1:T(8,128)S(1)} %fusion.4, f32[256,64]{0,1:T(8,128)S(1)} %fusion.26, bf16[2,32,32,256]{3,2,1,0:T(8,128)(2,1)S(1)} %fusion.2, f32[2,32,32,64]{3,2,1,0:T(8,128)S(1)} %convolution_bitcast_fusion), kind=kOutput, calls=%fused_computation.18 | convolution fusion | flops 201359360 | bytes 1769472 | tf_op jit(solution)/shard_map/gkvu,gkvsj->usj/dot_general | solution.py:168
  36.8 12.5 %all_to_all.10 = f32[8,72,64]{1,2,0:T(8,128)S(1)} all-to-all(f32[8,72,64]{1,2,0:T(8,128)S(1)} %bitcast.135), channel_id=1, replica_groups=mesh['parts'=2,'pix'=4,'ang'=2,'sl'=2] {'pix','ang'}, dimensions={0} | all-to-all | bytes 294912 | tf_op jit(solution)/shard_map/all_to_all | solution.py:178
  49.3 0.8 %copy.40 = f32[64,512]{1,0:T(8,128)} copy(f32[64,512]{0,1:T(8,128)S(1)} %bitcast.132) | data formatting | bytes 262144
  50.2 0.7 %copy.41 = f32[1,8,512]{2,1,0:T(8,128)} copy(f32[1,8,512]{1,2,0:T(8,128)S(1)} %bitcast.138) | data formatting | bytes 32768
  (29 shorter events, 2.3 us)
Async XLA Ops:
  4.3 8.4 %copy-start = (bf16[32,4096]{1,0:T(8,128)(2,1)S(1)}, bf16[32,4096]{1,0:T(8,128)(2,1)}, u32[]{:S(2)}) copy-start(bf16[32,4096]{1,0:T(8,128)(2,1)} %param.7) | copy-start | bytes 786436
  5.4 21.7 %all-to-all-start = ((f32[8,136,64]{1,2,0:T(8,128)}), f32[8,136,64]{1,2,0:T(8,128)S(1)}, u32[]{:S(2)}, u32[]{:S(2)}) async-start(f32[8,136,64]{1,2,0:T(8,128)} %pad_maximum_fusion), calls=%async_computation | async-start | bytes 1048576 | tf_op jit(solution)/shard_map/all_to_all | solution.py:125

commit v13 on v10

--- a/solution.py
+++ b/solution.py
@@ -119,8 +119,11 @@
     lists = jnp.pad(cells, (0, list_rows * width - nbd)).reshape(list_rows, width)
     list_send = jnp.broadcast_to(lists[None], (n_grp, list_rows, width))
     send = jnp.concatenate([vol_send, sino_send, list_send], axis=1)
+    rows = tiles_dev + rays_dev + list_rows
+    paired = rows + rows % 2
+    send = jnp.pad(send, ((0, 0), (0, paired - rows), (0, 0))).reshape(n_grp, paired // 2, 2 * width)
     recv = lax.all_to_all(send, ("pix", "ang"), 0, 0, tiled=False)
-    recv = recv.reshape(n_pix, n_ang, tiles_dev + rays_dev + list_rows, width)
+    recv = recv.reshape(n_pix, n_ang, paired, width)[:, :, :rows]
 
     current = recv[:, 0, :tiles_dev].reshape(pix_total, width)
     measured = recv[:, :, tiles_dev:tiles_dev + rays_dev].transpose(1, 0, 2, 3).reshape(n_ang, ray_total, width)

time: 45.6 us -> 43.5 us (0.954)
  other arithmetic: 2.93 us -> 1.93 us
  waiting for transfers between devices: 7.46 us -> 6.5 us
    reshape x0 -> x4, local copies, waits for them, and re-layouts: none -> 1.97 us  [the longest x2 1.06 us: per_device_split(): vol_send = volume.reshape(tiles_dev, n_grp, width).transpose(1, 0, 2)]
    unnamed x6 -> x4, local copies, waits for them, and re-layouts: 3.4 us -> 1.49 us
    all_to_all x1, waiting for transfers between devices: 7.46 us -> 6.5 us  [per_device_split(): recv = lax.all_to_all(send, ('pix', 'ang'), 0, 0, tiled=False)]
    concatenate x1, other arithmetic: 0.9 us -> 0.03 us  [per_device_split(): send = jnp.concatenate([vol_send, sino_send, list_send], axis=1)]
    another operation x0 -> x2, local copies, waits for them, and re-layouts: none -> 0.8 us  [per_device_split(): sino_send = sinogram[0].reshape(rays_dev, n_grp, width).transpose(1, 0, 2)]
where the time goes in v13:
time: 43.5 us; the launch traced here: 43 us
  blocking collectives  11.6 us (27%)
  matrix products  8.11 us (19%)
  starting transfers between devices  7.25 us (17%)
  local copies, waits for them, and re-layouts  6.78 us (16%)
  waiting for transfers between devices  6.5 us (15%)
  other arithmetic  1.93 us (4%)
  between operations  0.91 us (2%)
    all_to_all x1, blocking collectives, per_device_split(): got_back = lax.all_to_all(back, ('pix', 'ang'), 0, 0, tiled=False)  11.6 us
    all_to_all x1, starting transfers between devices, per_device_split(): recv = lax.all_to_all(send, ('pix', 'ang'), 0, 0, tiled=False)  7.25 us
    all_to_all x1, waiting for transfers between devices, per_device_split(): recv = lax.all_to_all(send, ('pix', 'ang'), 0, 0, tiled=False)  6.5 us
    dot_general x1, matrix products, per_device_split(): jnp.einsum('gkbv,gkbu->gkvu', one_ray, one_pix, preferred_element_type=jn...  3.53 us
    unnamed x4, local copies, waits for them, and re-layouts  1.49 us
    dot_general x2, matrix products, per_device_split(): jnp.einsum('gkvu,gkvsj->usj', counts, spread, precision=lax.Precision.HIG...  1.44 us
    dot_general x2, matrix products, per_device_split(): jnp.einsum('gkvsj,kij->gvsi', gathered, pattern_wide, precision=lax.Preci...  1.29 us
    reshape x2, local copies, waits for them, and re-layouts, per_device_split(): pattern = table.reshape(KINDS, TILE, TILE)  1.07 us
  transfers between devices with their start and end apart: 1, of which 1 were waited for; matrix products, arithmetic and copies ran while one was open for 3% of the time, Pallas kernels for 0%

profile of v13, /device:TPU:0, one launch (start us, length us, event | category | flops | bytes accessed | tf_op | source)
XLA Modules:
  0.0 43.0 jit_solution(893704258980603278)
XLA Ops:
  0.6 0.7 %convert_reduce_fusion.4 = f32[1408]{0:T(1024)S(1)} fusion(s32[1,1,1408]{2,1,0:T(1,128)} %param.9, s32[1,1,1408]{2,1,0:T(1,128)} %param.8), kind=kLoop, calls=%fused_computation.52 | loop fusion | flops 4224 | bytes 16896 | tf_op jit(solution)/shard_map/convert_element_type | solution.py:117
  1.4 0.8 %reshape_squeeze.3 = f32[8,8,64]{2,1,0:T(8,128)S(1)} reshape(f32[1,8,512]{2,1,0:T(8,128)} %param.6) | data formatting | bytes 32768 | tf_op jit(solution)/shard_map/reshape;squeeze | solution.py:116
  2.2 1.0 %reshape.99 = f32[64,8,64]{2,1,0:T(8,128)S(1)} reshape(f32[64,512]{1,0:T(8,128)} %param.5) | data formatting | bytes 262144 | tf_op jit(solution)/shard_map/reshape | solution.py:115
  3.4 0.8 %reshape.100 = f32[8,47,128]{2,1,0:T(8,128)} reshape(f32[8,94,64]{2,1,0:T(8,128)S(1)} %pad_maximum_fusion) | data formatting | bytes 385024 | tf_op jit(solution)/shard_map/reshape | solution.py:124
  4.2 7.3 %all-to-all-start = ((f32[8,47,128]{2,1,0:T(8,128)}), f32[8,47,128]{2,1,0:T(8,128)S(1)}, u32[]{:S(2)}, u32[]{:S(2)}) async-start(f32[8,47,128]{2,1,0:T(8,128)} %reshape.100), calls=%async_computation | async-start | bytes 393216 | tf_op jit(solution)/shard_map/all_to_all | solution.py:125
  11.4 0.5 %reshape.110 = bf16[32,64,64,1]{2,1,0,3:T(8,128)(2,1)S(1)} reshape(bf16[32,4096]{1,0:T(8,128)(2,1)S(1)} %copy-done) | data formatting | bytes 524288 | tf_op jit(solution)/shard_map/reshape | solution.py:150
  12.0 0.5 %reshape.102 = bf16[32,64,64]{2,1,0:T(8,128)(2,1)S(1)} reshape(bf16[32,4096]{1,0:T(8,128)(2,1)S(1)} %copy-done) | data formatting | bytes 524288 | tf_op jit(solution)/shard_map/reshape | solution.py:150
  12.5 0.3 convert_reduce_fusion.2
  12.9 6.5 %all-to-all-done = f32[8,47,128]{2,1,0:T(8,128)S(1)} async-done(((f32[8,47,128]{2,1,0:T(8,128)}), f32[8,47,128]{2,1,0:T(8,128)S(1)}, u32[]{:S(2)}, u32[]{:S(2)}) %all-to-all-start) | async-done | bytes 192544 | tf_op jit(solution)/shard_map/all_to_all | solution.py:125
  20.8 3.5 %fusion.2 = bf16[2,32,32,256]{3,2,1,0:T(8,128)(2,1)S(1)} fusion(s32[2,32,176]{2,1,0:T(8,128)S(1)} %eq.36, s32[2,32,176]{2,1,0:T(8,128)S(1)} %eq.32), kind=kOutput, calls=%fused_computation.6 | convolution fusion | flops 188317696 | bytes 1138688 | tf_op jit(solution)/shard_map/gkbv,gkbu->gkvu/dot_general | solution.py:142
  24.3 0.4 %convert_reduce_fusion = (f32[32,256]{1,0:T(8,128)S(1)}, f32[2,32,32]{2,1,0:T(8,128)S(1)}) fusion(bf16[2,32,32,256]{3,2,1,0:T(8,128)(2,1)S(1)} %fusion.2), kind=kLoop, calls=%fused_computation.3 | loop fusion | flops 1562624 | bytes 1089536 | tf_op jit(solution)/shard_map/gku,kj->uj/reduce_sum | solution.py:154
  24.8 0.4 fusion.16
  25.2 0.2 fusion.21
  25.4 0.6 %fusion.12 = bf16[2,32,64,1]{2,1,3,0:T(8,128)(2,1)S(1)} fusion(f32[2,32,64]{2,1,0:T(8,128)S(1)} %fusion.21, f32[2,32,32,64]{3,2,1,0:T(8,128)S(1)} %fusion.16, bf16[32,64,64,1]{2,1,0,3:T(8,128)(2,1)S(1)} %reshape.110, f32[4,2,94,64]{3,2,1,0:T(8,128)S(1)} %reshape.101), kind=kOutput, calls=%fused_computation.24 | convolution fusion | flops 100675584 | bytes 1646592 | tf_op jit(solution)/shard_map/gkvsj,kij->gvsi/dot_general | solution.py:166
  26.1 0.3 convolution_bitcast_fusion.1
  26.4 0.3 fusion.24
  26.6 0.7 %fusion.4 = f32[256,64]{0,1:T(8,128)S(1)} fusion(f32[256,64]{0,1:T(8,128)S(1)} %copy.58, f32[256,64]{0,1:T(8,128)S(1)} %fusion.24, bf16[2,32,32,256]{3,2,1,0:T(8,128)(2,1)S(1)} %fusion.2, f32[2,32,32,64]{3,2,1,0:T(8,128)S(1)} %convolution_bitcast_fusion.1), kind=kOutput, calls=%fused_computation.16 | convolution fusion | flops 201359360 | bytes 1769472 | tf_op jit(solution)/shard_map/gkvu,gkvsj->usj/dot_general | solution.py:173
  27.4 0.4 fusion.14
  27.8 0.6 %fusion.10 = f32[2,32,64]{2,1,0:T(8,128)S(1)} fusion(f32[2,32,64]{2,1,0:T(8,128)S(1)} %fusion.21, f32[2,32,32,64]{3,2,1,0:T(8,128)S(1)} %fusion.14, bf16[32,64,64,1]{2,1,0,3:T(8,128)(2,1)S(1)} %reshape.110, f32[4,2,94,64]{3,2,1,0:T(8,128)S(1)} %reshape.101), kind=kOutput, calls=%fused_computation.22 | convolution fusion | flops 100671488 | bytes 1654784 | tf_op jit(solution)/shard_map/gkvsj,kij->gvsi/dot_general | solution.py:166
  28.4 0.3 convolution_bitcast_fusion
  28.8 0.7 %fusion.6 = f32[256,64]{0,1:T(8,128)S(1)} fusion(f32[256,64]{0,1:T(8,128)S(1)} %fusion.4, f32[256,64]{0,1:T(8,128)S(1)} %fusion.24, bf16[2,32,32,256]{3,2,1,0:T(8,128)(2,1)S(1)} %fusion.2, f32[2,32,32,64]{3,2,1,0:T(8,128)S(1)} %convolution_bitcast_fusion), kind=kOutput, calls=%fused_computation.18 | convolution fusion | flops 201359360 | bytes 1769472 | tf_op jit(solution)/shard_map/gkvu,gkvsj->usj/dot_general | solution.py:173
  29.9 11.6 %all_to_all.10 = f32[8,72,64]{1,2,0:T(8,128)S(1)} all-to-all(f32[8,72,64]{1,2,0:T(8,128)S(1)} %bitcast.144), channel_id=1, replica_groups=mesh['parts'=2,'pix'=4,'ang'=2,'sl'=2] {'pix','ang'}, dimensions={0} | all-to-all | bytes 294912 | tf_op jit(solution)/shard_map/all_to_all | solution.py:183
  41.4 0.8 %copy.47 = f32[64,512]{1,0:T(8,128)} copy(f32[64,512]{0,1:T(8,128)S(1)} %bitcast.142) | data formatting | bytes 262144
  42.3 0.7 %copy.48 = f32[1,8,512]{2,1,0:T(8,128)} copy(f32[1,8,512]{1,2,0:T(8,128)S(1)} %bitcast.145) | data formatting | bytes 32768
  (28 shorter events, 2.1 us)
Async XLA Ops:
  3.3 8.1 %copy-start = (bf16[32,4096]{1,0:T(8,128)(2,1)S(1)}, bf16[32,4096]{1,0:T(8,128)(2,1)}, u32[]{:S(2)}) copy-start(bf16[32,4096]{1,0:T(8,128)(2,1)} %param.7) | copy-start | bytes 786436
  4.2 15.2 %all-to-all-start = ((f32[8,47,128]{2,1,0:T(8,128)}), f32[8,47,128]{2,1,0:T(8,128)S(1)}, u32[]{:S(2)}, u32[]{:S(2)}) async-start(f32[8,47,128]{2,1,0:T(8,128)} %reshape.100), calls=%async_computation | async-start | bytes 393216 | tf_op jit(solution)/shard_map/all_to_all | solution.py:125

commit v14 on v13

--- a/solution.py
+++ b/solution.py
@@ -180,7 +180,12 @@
     vol_back = jnp.broadcast_to(vol_back[:, None], (n_pix, n_ang, tiles_dev, width))
     res_back = scaled.reshape(n_ang, n_pix, rays_dev, width).transpose(1, 0, 2, 3)
     back = jnp.concatenate([vol_back, res_back], axis=2).reshape(n_grp, tiles_dev + rays_dev, width)
+    rows_back = tiles_dev + rays_dev
+    paired_back = rows_back + rows_back % 2
+    back = jnp.pad(back, ((0, 0), (0, paired_back - rows_back), (0, 0)))
+    back = back.reshape(n_grp, paired_back // 2, 2 * width)
     got_back = lax.all_to_all(back, ("pix", "ang"), 0, 0, tiled=False)
+    got_back = got_back.reshape(n_grp, paired_back, width)[:, :rows_back]
     vol_out = got_back[:, :tiles_dev].transpose(1, 0, 2).reshape(tiles_dev, slices * TILE)
     res_out = got_back[:, tiles_dev:].transpose(1, 0, 2).reshape(1, rays_dev, slices * TILE)
     return (vol_out, res_out)

time: 43.5 us -> 42.4 us (0.975)
  blocking collectives: 11.6 us -> 10.5 us
    reshape x0 -> x4, local copies, waits for them, and re-layouts: none -> 1.65 us  [the longest x1 0.77 us: per_device_split(): got_back[:, :tiles_dev].transpose(1, 0, 2).reshape(tiles_dev, slices * TILE)]
    unnamed x4 -> x2, local copies, waits for them, and re-layouts: 1.49 us -> 0.01 us
    all_to_all x1, blocking collectives: 11.6 us -> 10.5 us  [per_device_split(): got_back = lax.all_to_all(back, ('pix', 'ang'), 0, 0, tiled=False)]
where the time goes in v14:
time: 42.4 us; the launch traced here: 42 us
  blocking collectives  10.5 us (25%)
  matrix products  8.1 us (19%)
  starting transfers between devices  7.25 us (17%)
  local copies, waits for them, and re-layouts  6.86 us (16%)
  waiting for transfers between devices  6.5 us (15%)
  other arithmetic  1.82 us (4%)
  between operations  0.93 us (2%)
    all_to_all x1, blocking collectives, per_device_split(): got_back = lax.all_to_all(back, ('pix', 'ang'), 0, 0, tiled=False)  10.5 us
    all_to_all x1, starting transfers between devices, per_device_split(): recv = lax.all_to_all(send, ('pix', 'ang'), 0, 0, tiled=False)  7.25 us
    all_to_all x1, waiting for transfers between devices, per_device_split(): recv = lax.all_to_all(send, ('pix', 'ang'), 0, 0, tiled=False)  6.5 us
    dot_general x1, matrix products, per_device_split(): jnp.einsum('gkbv,gkbu->gkvu', one_ray, one_pix, preferred_element_type=jn...  3.53 us
    dot_general x2, matrix products, per_device_split(): jnp.einsum('gkvu,gkvsj->usj', counts, spread, precision=lax.Precision.HIG...  1.44 us
    dot_general x2, matrix products, per_device_split(): jnp.einsum('gkvsj,kij->gvsi', gathered, pattern_wide, precision=lax.Preci...  1.29 us
    reshape x2, local copies, waits for them, and re-layouts, per_device_split(): pattern = table.reshape(KINDS, TILE, TILE)  1.07 us
    reshape x2, local copies, waits for them, and re-layouts, per_device_split(): vol_send = volume.reshape(tiles_dev, n_grp, width).transpose(1, 0, 2)  1.06 us
  transfers between devices with their start and end apart: 1, of which 1 were waited for; matrix products, arithmetic and copies ran while one was open for 3% of the time, Pallas kernels for 0%

profile of v14, /device:TPU:0, one launch (start us, length us, event | category | flops | bytes accessed | tf_op | source)
XLA Modules:
  0.0 42.0 jit_solution(13289537870933682202)
XLA Ops:
  0.6 0.7 %convert_reduce_fusion.4 = f32[1408]{0:T(1024)S(1)} fusion(s32[1,1,1408]{2,1,0:T(1,128)} %param.9, s32[1,1,1408]{2,1,0:T(1,128)} %param.8), kind=kLoop, calls=%fused_computation.55 | loop fusion | flops 4224 | bytes 16896 | tf_op jit(solution)/shard_map/convert_element_type | solution.py:117
  1.4 0.8 %reshape_squeeze.3 = f32[8,8,64]{2,1,0:T(8,128)S(1)} reshape(f32[1,8,512]{2,1,0:T(8,128)} %param.6) | data formatting | bytes 32768 | tf_op jit(solution)/shard_map/reshape;squeeze | solution.py:116
  2.2 1.0 %reshape.104 = f32[64,8,64]{2,1,0:T(8,128)S(1)} reshape(f32[64,512]{1,0:T(8,128)} %param.5) | data formatting | bytes 262144 | tf_op jit(solution)/shard_map/reshape | solution.py:115
  3.4 0.8 %reshape.105 = f32[8,47,128]{2,1,0:T(8,128)} reshape(f32[8,94,64]{2,1,0:T(8,128)S(1)} %pad_maximum_fusion) | data formatting | bytes 385024 | tf_op jit(solution)/shard_map/reshape | solution.py:124
  4.2 7.3 %all-to-all-start = ((f32[8,47,128]{2,1,0:T(8,128)}), f32[8,47,128]{2,1,0:T(8,128)S(1)}, u32[]{:S(2)}, u32[]{:S(2)}) async-start(f32[8,47,128]{2,1,0:T(8,128)} %reshape.105), calls=%async_computation | async-start | bytes 393216 | tf_op jit(solution)/shard_map/all_to_all | solution.py:125
  11.4 0.5 %reshape.116 = bf16[32,64,64,1]{2,1,0,3:T(8,128)(2,1)S(1)} reshape(bf16[32,4096]{1,0:T(8,128)(2,1)S(1)} %copy-done) | data formatting | bytes 524288 | tf_op jit(solution)/shard_map/reshape | solution.py:150
  12.0 0.5 %reshape.107 = bf16[32,64,64]{2,1,0:T(8,128)(2,1)S(1)} reshape(bf16[32,4096]{1,0:T(8,128)(2,1)S(1)} %copy-done) | data formatting | bytes 524288 | tf_op jit(solution)/shard_map/reshape | solution.py:150
  12.5 0.3 convert_reduce_fusion.2
  12.9 6.5 %all-to-all-done = f32[8,47,128]{2,1,0:T(8,128)S(1)} async-done(((f32[8,47,128]{2,1,0:T(8,128)}), f32[8,47,128]{2,1,0:T(8,128)S(1)}, u32[]{:S(2)}, u32[]{:S(2)}) %all-to-all-start) | async-done | bytes 192544 | tf_op jit(solution)/shard_map/all_to_all | solution.py:125
  20.8 3.5 %fusion.2 = bf16[2,32,32,256]{3,2,1,0:T(8,128)(2,1)S(1)} fusion(s32[2,32,176]{2,1,0:T(8,128)S(1)} %eq.36, s32[2,32,176]{2,1,0:T(8,128)S(1)} %eq.32), kind=kOutput, calls=%fused_computation.6 | convolution fusion | flops 188317696 | bytes 1138688 | tf_op jit(solution)/shard_map/gkbv,gkbu->gkvu/dot_general | solution.py:142
  24.3 0.4 %convert_reduce_fusion = (f32[32,256]{1,0:T(8,128)S(1)}, f32[2,32,32]{2,1,0:T(8,128)S(1)}) fusion(bf16[2,32,32,256]{3,2,1,0:T(8,128)(2,1)S(1)} %fusion.2), kind=kLoop, calls=%fused_computation.3 | loop fusion | flops 1562624 | bytes 1089536 | tf_op jit(solution)/shard_map/gku,kj->uj/reduce_sum | solution.py:154
  24.8 0.4 fusion.16
  25.2 0.2 fusion.21
  25.4 0.6 %fusion.12 = bf16[2,32,64,1]{2,1,3,0:T(8,128)(2,1)S(1)} fusion(f32[2,32,64]{2,1,0:T(8,128)S(1)} %fusion.21, f32[2,32,32,64]{3,2,1,0:T(8,128)S(1)} %fusion.16, bf16[32,64,64,1]{2,1,0,3:T(8,128)(2,1)S(1)} %reshape.116, f32[4,2,94,64]{3,2,1,0:T(8,128)S(1)} %reshape.106), kind=kOutput, calls=%fused_computation.24 | convolution fusion | flops 100675584 | bytes 1646592 | tf_op jit(solution)/shard_map/gkvsj,kij->gvsi/dot_general | solution.py:166
  26.1 0.3 convolution_bitcast_fusion.1
  26.4 0.3 fusion.24
  26.6 0.7 %fusion.4 = f32[256,64]{0,1:T(8,128)S(1)} fusion(f32[256,64]{0,1:T(8,128)S(1)} %copy.60, f32[256,64]{0,1:T(8,128)S(1)} %fusion.24, bf16[2,32,32,256]{3,2,1,0:T(8,128)(2,1)S(1)} %fusion.2, f32[2,32,32,64]{3,2,1,0:T(8,128)S(1)} %convolution_bitcast_fusion.1), kind=kOutput, calls=%fused_computation.16 | convolution fusion | flops 201359360 | bytes 1769472 | tf_op jit(solution)/shard_map/gkvu,gkvsj->usj/dot_general | solution.py:173
  27.4 0.4 fusion.14
  27.8 0.6 %fusion.10 = f32[2,32,64]{2,1,0:T(8,128)S(1)} fusion(f32[2,32,64]{2,1,0:T(8,128)S(1)} %fusion.21, f32[2,32,32,64]{3,2,1,0:T(8,128)S(1)} %fusion.14, bf16[32,64,64,1]{2,1,0,3:T(8,128)(2,1)S(1)} %reshape.116, f32[4,2,94,64]{3,2,1,0:T(8,128)S(1)} %reshape.106), kind=kOutput, calls=%fused_computation.22 | convolution fusion | flops 100671488 | bytes 1654784 | tf_op jit(solution)/shard_map/gkvsj,kij->gvsi/dot_general | solution.py:166
  28.4 0.3 convolution_bitcast_fusion
  28.7 0.7 %fusion.6 = f32[256,64]{0,1:T(8,128)S(1)} fusion(f32[256,64]{0,1:T(8,128)S(1)} %fusion.4, f32[256,64]{0,1:T(8,128)S(1)} %fusion.24, bf16[2,32,32,256]{3,2,1,0:T(8,128)(2,1)S(1)} %fusion.2, f32[2,32,32,64]{3,2,1,0:T(8,128)S(1)} %convolution_bitcast_fusion), kind=kOutput, calls=%fused_computation.18 | convolution fusion | flops 201359360 | bytes 1769472 | tf_op jit(solution)/shard_map/gkvu,gkvsj->usj/dot_general | solution.py:173
  29.7 10.5 %all_to_all.10 = f32[8,36,128]{2,1,0:T(8,128)S(1)} all-to-all(f32[8,36,128]{2,1,0:T(8,128)S(1)} %reshape.111), channel_id=1, replica_groups=mesh['parts'=2,'pix'=4,'ang'=2,'sl'=2] {'pix','ang'}, dimensions={0} | all-to-all | bytes 294912 | tf_op jit(solution)/shard_map/all_to_all | solution.py:187
  40.5 0.8 %reshape.113 = f32[64,512]{1,0:T(8,128)} reshape(f32[64,8,64]{2,1,0:T(8,128)S(1)} %copy.49) | data formatting | bytes 262144 | tf_op jit(solution)/shard_map/reshape | solution.py:189
  41.3 0.7 %reshape.114 = f32[1,8,512]{2,1,0:T(8,128)} reshape(f32[8,8,64]{2,1,0:T(8,128)S(1)} %copy.50) | data formatting | bytes 32768 | tf_op jit(solution)/shard_map/reshape | solution.py:190
  (32 shorter events, 2.1 us)
Async XLA Ops:
  3.3 8.1 %copy-start = (bf16[32,4096]{1,0:T(8,128)(2,1)S(1)}, bf16[32,4096]{1,0:T(8,128)(2,1)}, u32[]{:S(2)}) copy-start(bf16[32,4096]{1,0:T(8,128)(2,1)} %param.7) | copy-start | bytes 786436
  4.2 15.2 %all-to-all-start = ((f32[8,47,128]{2,1,0:T(8,128)}), f32[8,47,128]{2,1,0:T(8,128)S(1)}, u32[]{:S(2)}, u32[]{:S(2)}) async-start(f32[8,47,128]{2,1,0:T(8,128)} %reshape.105), calls=%async_computation | async-start | bytes 393216 | tf_op jit(solution)/shard_map/all_to_all | solution.py:125

commit v15 on v14

--- a/solution.py
+++ b/solution.py
@@ -118,10 +118,20 @@
     list_rows = (nbd + width - 1) // width
     lists = jnp.pad(cells, (0, list_rows * width - nbd)).reshape(list_rows, width)
     list_send = jnp.broadcast_to(lists[None], (n_grp, list_rows, width))
-    send = jnp.concatenate([vol_send, sino_send, list_send], axis=1)
     rows = tiles_dev + rays_dev + list_rows
     paired = rows + rows % 2
-    send = jnp.pad(send, ((0, 0), (0, paired - rows), (0, 0))).reshape(n_grp, paired // 2, 2 * width)
+    if tiles_dev % 2 == 0 and rays_dev % 2 == 0 and nbd % (2 * width) == 0:
+        send = jnp.concatenate(
+            [
+                vol_send.reshape(n_grp, tiles_dev // 2, 2 * width),
+                sino_send.reshape(n_grp, rays_dev // 2, 2 * width),
+                jnp.broadcast_to(cells.reshape(1, list_rows // 2, 2 * width), (n_grp, list_rows // 2, 2 * width)),
+            ],
+            axis=1,
+        )
+    else:
+        send = jnp.concatenate([vol_send, sino_send, list_send], axis=1)
+        send = jnp.pad(send, ((0, 0), (0, paired - rows), (0, 0))).reshape(n_grp, paired // 2, 2 * width)
     recv = lax.all_to_all(send, ("pix", "ang"), 0, 0, tiled=False)
     recv = recv.reshape(n_pix, n_ang, paired, width)[:, :, :rows]
 

time: 42.4 us -> 41.7 us (0.983)
  local copies, waits for them, and re-layouts: 6.86 us -> 6.24 us
    convert_element_type x1, other arithmetic: 0.73 us -> 0.02 us  [per_device_split(): (blk_ray.reshape(-1) * tiles_dev + blk_pix.reshape(-1)).astype(jnp.float32)]
    concatenate x1, other arithmetic: 0.03 us -> 0.69 us  [per_device_split(): jnp.concatenate([vol_send.reshape(n_grp, tiles_dev // 2, 2 * width), sino...]
    reshape x1 -> x2, local copies, waits for them, and re-layouts: 0.79 us -> 0.18 us  [the longest x1 0.1 us: per_device_split(): vol_send.reshape(n_grp, tiles_dev // 2, 2 * width)]
where the time goes in v15:
time: 41.7 us; the launch traced here: 41.3 us
  blocking collectives  10.5 us (25%)
  matrix products  8.1 us (19%)
  starting transfers between devices  7.25 us (17%)
  waiting for transfers between devices  6.5 us (16%)
  local copies, waits for them, and re-layouts  6.24 us (15%)
  other arithmetic  1.77 us (4%)
  between operations  0.96 us (2%)
    all_to_all x1, blocking collectives, per_device_split(): got_back = lax.all_to_all(back, ('pix', 'ang'), 0, 0, tiled=False)  10.5 us
    all_to_all x1, starting transfers between devices, per_device_split(): recv = lax.all_to_all(send, ('pix', 'ang'), 0, 0, tiled=False)  7.25 us
    all_to_all x1, waiting for transfers between devices, per_device_split(): recv = lax.all_to_all(send, ('pix', 'ang'), 0, 0, tiled=False)  6.5 us
    dot_general x1, matrix products, per_device_split(): jnp.einsum('gkbv,gkbu->gkvu', one_ray, one_pix, preferred_element_type=jn...  3.53 us
    dot_general x2, matrix products, per_device_split(): jnp.einsum('gkvu,gkvsj->usj', counts, spread, precision=lax.Precision.HIG...  1.44 us
    dot_general x2, matrix products, per_device_split(): jnp.einsum('gkvsj,kij->gvsi', gathered, pattern_wide, precision=lax.Preci...  1.29 us
    reshape x2, local copies, waits for them, and re-layouts, per_device_split(): vol_send = volume.reshape(tiles_dev, n_grp, width).transpose(1, 0, 2)  1.1 us
    reshape x2, local copies, waits for them, and re-layouts, per_device_split(): pattern = table.reshape(KINDS, TILE, TILE)  1.07 us
  transfers between devices with their start and end apart: 1, of which 1 were waited for; matrix products, arithmetic and copies ran while one was open for 3% of the time, Pallas kernels for 0%

profile of v15, /device:TPU:0, one launch (start us, length us, event | category | flops | bytes accessed | tf_op | source)
XLA Modules:
  0.0 41.3 jit_solution(14593284507627531717)
XLA Ops:
  0.7 0.8 %reshape_squeeze.3 = f32[8,8,64]{2,1,0:T(8,128)S(1)} reshape(f32[1,8,512]{2,1,0:T(8,128)} %param.6) | data formatting | bytes 32768 | tf_op jit(solution)/shard_map/reshape;squeeze | solution.py:116
  1.5 1.0 %reshape.108 = f32[64,8,64]{2,1,0:T(8,128)S(1)} reshape(f32[64,512]{1,0:T(8,128)} %param.5) | data formatting | bytes 262144 | tf_op jit(solution)/shard_map/reshape | solution.py:115
  2.8 0.7 %pad_maximum_fusion.1 = f32[8,47,128]{2,1,0:T(8,128)} fusion(f32[8,11,128]{2,1,0:T(8,128)S(1)} %broadcast_in_dim.6, f32[8,4,128]{2,1,0:T(4,128)S(1)} %reshape.110, f32[8,32,128]{2,1,0:T(8,128)S(1)} %reshape.109), kind=kLoop, calls=%fused_computation.29 | loop fusion | flops 96256 | bytes 385024 | tf_op jit(solution)/shard_map/concatenate | solution.py:124
  3.5 7.3 %all-to-all-start = ((f32[8,47,128]{2,1,0:T(8,128)}), f32[8,47,128]{2,1,0:T(8,128)S(1)}, u32[]{:S(2)}, u32[]{:S(2)}) async-start(f32[8,47,128]{2,1,0:T(8,128)} %pad_maximum_fusion.1), calls=%async_computation | async-start | bytes 393216 | tf_op jit(solution)/shard_map/all_to_all | solution.py:135
  10.8 0.5 %reshape.121 = bf16[32,64,64,1]{2,1,0,3:T(8,128)(2,1)S(1)} reshape(bf16[32,4096]{1,0:T(8,128)(2,1)S(1)} %copy-done) | data formatting | bytes 524288 | tf_op jit(solution)/shard_map/reshape | solution.py:160
  11.3 0.5 %reshape.112 = bf16[32,64,64]{2,1,0:T(8,128)(2,1)S(1)} reshape(bf16[32,4096]{1,0:T(8,128)(2,1)S(1)} %copy-done) | data formatting | bytes 524288 | tf_op jit(solution)/shard_map/reshape | solution.py:160
  11.9 0.3 convert_reduce_fusion.2
  12.2 6.5 %all-to-all-done = f32[8,47,128]{2,1,0:T(8,128)S(1)} async-done(((f32[8,47,128]{2,1,0:T(8,128)}), f32[8,47,128]{2,1,0:T(8,128)S(1)}, u32[]{:S(2)}, u32[]{:S(2)}) %all-to-all-start) | async-done | bytes 192544 | tf_op jit(solution)/shard_map/all_to_all | solution.py:135
  19.7 0.2 reshape_squeeze_stack.6
  20.2 3.5 %fusion.2 = bf16[2,32,32,256]{3,2,1,0:T(8,128)(2,1)S(1)} fusion(s32[2,32,176]{2,1,0:T(8,128)S(1)} %eq.36, s32[2,32,176]{2,1,0:T(8,128)S(1)} %eq.32), kind=kOutput, calls=%fused_computation.6 | convolution fusion | flops 188317696 | bytes 1138688 | tf_op jit(solution)/shard_map/gkbv,gkbu->gkvu/dot_general | solution.py:152
  23.7 0.4 %convert_reduce_fusion = (f32[32,256]{1,0:T(8,128)S(1)}, f32[2,32,32]{2,1,0:T(8,128)S(1)}) fusion(bf16[2,32,32,256]{3,2,1,0:T(8,128)(2,1)S(1)} %fusion.2), kind=kLoop, calls=%fused_computation.3 | loop fusion | flops 1562624 | bytes 1089536 | tf_op jit(solution)/shard_map/gku,kj->uj/reduce_sum | solution.py:164
  24.1 0.4 fusion.16
  24.5 0.2 fusion.21
  24.8 0.6 %fusion.12 = bf16[2,32,64,1]{2,1,3,0:T(8,128)(2,1)S(1)} fusion(f32[2,32,64]{2,1,0:T(8,128)S(1)} %fusion.21, f32[2,32,32,64]{3,2,1,0:T(8,128)S(1)} %fusion.16, bf16[32,64,64,1]{2,1,0,3:T(8,128)(2,1)S(1)} %reshape.121, f32[4,2,94,64]{3,2,1,0:T(8,128)S(1)} %reshape.111), kind=kOutput, calls=%fused_computation.24 | convolution fusion | flops 100675584 | bytes 1646592 | tf_op jit(solution)/shard_map/gkvsj,kij->gvsi/dot_general | solution.py:176
  25.4 0.3 convolution_bitcast_fusion.1
  25.7 0.3 fusion.24
  26.0 0.7 %fusion.4 = f32[256,64]{0,1:T(8,128)S(1)} fusion(f32[256,64]{0,1:T(8,128)S(1)} %copy.60, f32[256,64]{0,1:T(8,128)S(1)} %fusion.24, bf16[2,32,32,256]{3,2,1,0:T(8,128)(2,1)S(1)} %fusion.2, f32[2,32,32,64]{3,2,1,0:T(8,128)S(1)} %convolution_bitcast_fusion.1), kind=kOutput, calls=%fused_computation.16 | convolution fusion | flops 201359360 | bytes 1769472 | tf_op jit(solution)/shard_map/gkvu,gkvsj->usj/dot_general | solution.py:183
  26.7 0.4 fusion.14
  27.1 0.6 %fusion.10 = f32[2,32,64]{2,1,0:T(8,128)S(1)} fusion(f32[2,32,64]{2,1,0:T(8,128)S(1)} %fusion.21, f32[2,32,32,64]{3,2,1,0:T(8,128)S(1)} %fusion.14, bf16[32,64,64,1]{2,1,0,3:T(8,128)(2,1)S(1)} %reshape.121, f32[4,2,94,64]{3,2,1,0:T(8,128)S(1)} %reshape.111), kind=kOutput, calls=%fused_computation.22 | convolution fusion | flops 100671488 | bytes 1654784 | tf_op jit(solution)/shard_map/gkvsj,kij->gvsi/dot_general | solution.py:176
  27.8 0.3 convolution_bitcast_fusion
  28.1 0.7 %fusion.6 = f32[256,64]{0,1:T(8,128)S(1)} fusion(f32[256,64]{0,1:T(8,128)S(1)} %fusion.4, f32[256,64]{0,1:T(8,128)S(1)} %fusion.24, bf16[2,32,32,256]{3,2,1,0:T(8,128)(2,1)S(1)} %fusion.2, f32[2,32,32,64]{3,2,1,0:T(8,128)S(1)} %convolution_bitcast_fusion), kind=kOutput, calls=%fused_computation.18 | convolution fusion | flops 201359360 | bytes 1769472 | tf_op jit(solution)/shard_map/gkvu,gkvsj->usj/dot_general | solution.py:183
  29.1 10.5 %all_to_all.10 = f32[8,36,128]{2,1,0:T(8,128)S(1)} all-to-all(f32[8,36,128]{2,1,0:T(8,128)S(1)} %reshape.116), channel_id=1, replica_groups=mesh['parts'=2,'pix'=4,'ang'=2,'sl'=2] {'pix','ang'}, dimensions={0} | all-to-all | bytes 294912 | tf_op jit(solution)/shard_map/all_to_all | solution.py:197
  39.9 0.8 %reshape.118 = f32[64,512]{1,0:T(8,128)} reshape(f32[64,8,64]{2,1,0:T(8,128)S(1)} %copy.49) | data formatting | bytes 262144 | tf_op jit(solution)/shard_map/reshape | solution.py:199
  40.7 0.7 %reshape.119 = f32[1,8,512]{2,1,0:T(8,128)} reshape(f32[8,8,64]{2,1,0:T(8,128)S(1)} %copy.50) | data formatting | bytes 32768 | tf_op jit(solution)/shard_map/reshape | solution.py:200
  (36 shorter events, 2.0 us)
Async XLA Ops:
  0.6 2.1 %copy-start.1 = (s32[1,1,1408]{2,1,0:T(1,128)S(1)}, s32[1,1,1408]{2,1,0:T(1,128)}, u32[]{:S(2)}) copy-start(s32[1,1,1408]{2,1,0:T(1,128)} %param.9) | copy-start | bytes 16900
  0.6 2.1 %copy-start.2 = (s32[1,1,1408]{2,1,0:T(1,128)S(1)}, s32[1,1,1408]{2,1,0:T(1,128)}, u32[]{:S(2)}) copy-start(s32[1,1,1408]{2,1,0:T(1,128)} %param.8) | copy-start | bytes 16900
  1.5 9.2 %copy-start = (bf16[32,4096]{1,0:T(8,128)(2,1)S(1)}, bf16[32,4096]{1,0:T(8,128)(2,1)}, u32[]{:S(2)}) copy-start(bf16[32,4096]{1,0:T(8,128)(2,1)} %param.7) | copy-start | bytes 786436
  3.5 15.2 %all-to-all-start = ((f32[8,47,128]{2,1,0:T(8,128)}), f32[8,47,128]{2,1,0:T(8,128)S(1)}, u32[]{:S(2)}, u32[]{:S(2)}) async-start(f32[8,47,128]{2,1,0:T(8,128)} %pad_maximum_fusion.1), calls=%async_computation | async-start | bytes 393216 | tf_op jit(solution)/shard_map/all_to_all | solution.py:135

commit v16 on v15

--- a/solution.py
+++ b/solution.py
@@ -196,8 +196,9 @@
     back = back.reshape(n_grp, paired_back // 2, 2 * width)
     got_back = lax.all_to_all(back, ("pix", "ang"), 0, 0, tiled=False)
     got_back = got_back.reshape(n_grp, paired_back, width)[:, :rows_back]
-    vol_out = got_back[:, :tiles_dev].transpose(1, 0, 2).reshape(tiles_dev, slices * TILE)
-    res_out = got_back[:, tiles_dev:].transpose(1, 0, 2).reshape(1, rays_dev, slices * TILE)
+    both = got_back.transpose(1, 0, 2).reshape(rows_back, slices * TILE)
+    vol_out = both[:tiles_dev]
+    res_out = both[tiles_dev:].reshape(1, rays_dev, slices * TILE)
     return (vol_out, res_out)
 
 

time: 41.7 us -> 41.7 us (level)
    slice x0 -> x5, local copies, waits for them, and re-layouts: none -> 0.96 us  [the longest x3 0.95 us: per_device_split(): vol_out = both[:tiles_dev]]
    reshape x2 -> x1, local copies, waits for them, and re-layouts: 1.45 us -> 0.68 us  [per_device_split(): res_out = both[tiles_dev:].reshape(1, rays_dev, slices * TILE)]
where the time goes in v16:
time: 41.7 us; the launch traced here: 41.3 us
  blocking collectives  10.5 us (25%)
  matrix products  8.1 us (19%)
  starting transfers between devices  7.25 us (17%)
  waiting for transfers between devices  6.5 us (16%)
  local copies, waits for them, and re-layouts  6.24 us (15%)
  other arithmetic  1.77 us (4%)
  between operations  0.96 us (2%)
    all_to_all x1, blocking collectives, per_device_split(): got_back = lax.all_to_all(back, ('pix', 'ang'), 0, 0, tiled=False)  10.5 us
    all_to_all x1, starting transfers between devices, per_device_split(): recv = lax.all_to_all(send, ('pix', 'ang'), 0, 0, tiled=False)  7.25 us
    all_to_all x1, waiting for transfers between devices, per_device_split(): recv = lax.all_to_all(send, ('pix', 'ang'), 0, 0, tiled=False)  6.5 us
    dot_general x1, matrix products, per_device_split(): jnp.einsum('gkbv,gkbu->gkvu', one_ray, one_pix, preferred_element_type=jn...  3.53 us
    dot_general x2, matrix products, per_device_split(): jnp.einsum('gkvu,gkvsj->usj', counts, spread, precision=lax.Precision.HIG...  1.44 us
    dot_general x2, matrix products, per_device_split(): jnp.einsum('gkvsj,kij->gvsi', gathered, pattern_wide, precision=lax.Preci...  1.29 us
    reshape x2, local copies, waits for them, and re-layouts, per_device_split(): vol_send = volume.reshape(tiles_dev, n_grp, width).transpose(1, 0, 2)  1.1 us
    reshape x2, local copies, waits for them, and re-layouts, per_device_split(): pattern = table.reshape(KINDS, TILE, TILE)  1.07 us
  transfers between devices with their start and end apart: 1, of which 1 were waited for; matrix products, arithmetic and copies ran while one was open for 3% of the time, Pallas kernels for 0%

profile of v16, /device:TPU:0, one launch (start us, length us, event | category | flops | bytes accessed | tf_op | source)
XLA Modules:
  0.0 41.3 jit_solution(14593284507627531717)
XLA Ops:
  0.7 0.8 %reshape_squeeze.3 = f32[8,8,64]{2,1,0:T(8,128)S(1)} reshape(f32[1,8,512]{2,1,0:T(8,128)} %param.6) | data formatting | bytes 32768 | tf_op jit(solution)/shard_map/reshape;squeeze | solution.py:116
  1.5 1.0 %reshape.109 = f32[64,8,64]{2,1,0:T(8,128)S(1)} reshape(f32[64,512]{1,0:T(8,128)} %param.5) | data formatting | bytes 262144 | tf_op jit(solution)/shard_map/reshape | solution.py:115
  2.8 0.7 %pad_maximum_fusion.1 = f32[8,47,128]{2,1,0:T(8,128)} fusion(f32[8,11,128]{2,1,0:T(8,128)S(1)} %broadcast_in_dim.6, f32[8,4,128]{2,1,0:T(4,128)S(1)} %reshape.111, f32[8,32,128]{2,1,0:T(8,128)S(1)} %reshape.110), kind=kLoop, calls=%fused_computation.28 | loop fusion | flops 96256 | bytes 385024 | tf_op jit(solution)/shard_map/concatenate | solution.py:124
  3.5 7.3 %all-to-all-start = ((f32[8,47,128]{2,1,0:T(8,128)}), f32[8,47,128]{2,1,0:T(8,128)S(1)}, u32[]{:S(2)}, u32[]{:S(2)}) async-start(f32[8,47,128]{2,1,0:T(8,128)} %pad_maximum_fusion.1), calls=%async_computation | async-start | bytes 393216 | tf_op jit(solution)/shard_map/all_to_all | solution.py:135
  10.8 0.5 %reshape.121 = bf16[32,64,64,1]{2,1,0,3:T(8,128)(2,1)S(1)} reshape(bf16[32,4096]{1,0:T(8,128)(2,1)S(1)} %copy-done) | data formatting | bytes 524288 | tf_op jit(solution)/shard_map/reshape | solution.py:160
  11.3 0.5 %reshape.113 = bf16[32,64,64]{2,1,0:T(8,128)(2,1)S(1)} reshape(bf16[32,4096]{1,0:T(8,128)(2,1)S(1)} %copy-done) | data formatting | bytes 524288 | tf_op jit(solution)/shard_map/reshape | solution.py:160
  11.9 0.3 convert_reduce_fusion.2
  12.2 6.5 %all-to-all-done = f32[8,47,128]{2,1,0:T(8,128)S(1)} async-done(((f32[8,47,128]{2,1,0:T(8,128)}), f32[8,47,128]{2,1,0:T(8,128)S(1)}, u32[]{:S(2)}, u32[]{:S(2)}) %all-to-all-start) | async-done | bytes 192544 | tf_op jit(solution)/shard_map/all_to_all | solution.py:135
  19.7 0.2 reshape_squeeze_stack.6
  20.2 3.5 %fusion.2 = bf16[2,32,32,256]{3,2,1,0:T(8,128)(2,1)S(1)} fusion(s32[2,32,176]{2,1,0:T(8,128)S(1)} %eq.36, s32[2,32,176]{2,1,0:T(8,128)S(1)} %eq.32), kind=kOutput, calls=%fused_computation.6 | convolution fusion | flops 188317696 | bytes 1138688 | tf_op jit(solution)/shard_map/gkbv,gkbu->gkvu/dot_general | solution.py:152
  23.7 0.4 %convert_reduce_fusion = (f32[32,256]{1,0:T(8,128)S(1)}, f32[2,32,32]{2,1,0:T(8,128)S(1)}) fusion(bf16[2,32,32,256]{3,2,1,0:T(8,128)(2,1)S(1)} %fusion.2), kind=kLoop, calls=%fused_computation.3 | loop fusion | flops 1562624 | bytes 1089536 | tf_op jit(solution)/shard_map/gku,kj->uj/reduce_sum | solution.py:164
  24.1 0.4 fusion.16
  24.5 0.2 fusion.21
  24.8 0.6 %fusion.12 = bf16[2,32,64,1]{2,1,3,0:T(8,128)(2,1)S(1)} fusion(f32[2,32,64]{2,1,0:T(8,128)S(1)} %fusion.21, f32[2,32,32,64]{3,2,1,0:T(8,128)S(1)} %fusion.16, bf16[32,64,64,1]{2,1,0,3:T(8,128)(2,1)S(1)} %reshape.121, f32[4,2,94,64]{3,2,1,0:T(8,128)S(1)} %reshape.112), kind=kOutput, calls=%fused_computation.24 | convolution fusion | flops 100675584 | bytes 1646592 | tf_op jit(solution)/shard_map/gkvsj,kij->gvsi/dot_general | solution.py:176
  25.4 0.3 convolution_bitcast_fusion.1
  25.7 0.3 fusion.24
  26.0 0.7 %fusion.4 = f32[256,64]{0,1:T(8,128)S(1)} fusion(f32[256,64]{0,1:T(8,128)S(1)} %copy.60, f32[256,64]{0,1:T(8,128)S(1)} %fusion.24, bf16[2,32,32,256]{3,2,1,0:T(8,128)(2,1)S(1)} %fusion.2, f32[2,32,32,64]{3,2,1,0:T(8,128)S(1)} %convolution_bitcast_fusion.1), kind=kOutput, calls=%fused_computation.16 | convolution fusion | flops 201359360 | bytes 1769472 | tf_op jit(solution)/shard_map/gkvu,gkvsj->usj/dot_general | solution.py:183
  26.7 0.4 fusion.14
  27.1 0.6 %fusion.10 = f32[2,32,64]{2,1,0:T(8,128)S(1)} fusion(f32[2,32,64]{2,1,0:T(8,128)S(1)} %fusion.21, f32[2,32,32,64]{3,2,1,0:T(8,128)S(1)} %fusion.14, bf16[32,64,64,1]{2,1,0,3:T(8,128)(2,1)S(1)} %reshape.121, f32[4,2,94,64]{3,2,1,0:T(8,128)S(1)} %reshape.112), kind=kOutput, calls=%fused_computation.22 | convolution fusion | flops 100671488 | bytes 1654784 | tf_op jit(solution)/shard_map/gkvsj,kij->gvsi/dot_general | solution.py:176
  27.8 0.3 convolution_bitcast_fusion
  28.1 0.7 %fusion.6 = f32[256,64]{0,1:T(8,128)S(1)} fusion(f32[256,64]{0,1:T(8,128)S(1)} %fusion.4, f32[256,64]{0,1:T(8,128)S(1)} %fusion.24, bf16[2,32,32,256]{3,2,1,0:T(8,128)(2,1)S(1)} %fusion.2, f32[2,32,32,64]{3,2,1,0:T(8,128)S(1)} %convolution_bitcast_fusion), kind=kOutput, calls=%fused_computation.18 | convolution fusion | flops 201359360 | bytes 1769472 | tf_op jit(solution)/shard_map/gkvu,gkvsj->usj/dot_general | solution.py:183
  29.1 10.5 %all_to_all.10 = f32[8,36,128]{2,1,0:T(8,128)S(1)} all-to-all(f32[8,36,128]{2,1,0:T(8,128)S(1)} %reshape.117), channel_id=1, replica_groups=mesh['parts'=2,'pix'=4,'ang'=2,'sl'=2] {'pix','ang'}, dimensions={0} | all-to-all | bytes 294912 | tf_op jit(solution)/shard_map/all_to_all | solution.py:197
  39.9 0.8 %slice.23 = f32[64,512]{1,0:T(8,128)} reshape(f32[64,8,64]{2,1,0:T(8,128)S(1)} %copy.49) | data formatting | bytes 262144 | tf_op jit(solution)/shard_map/slice | solution.py:200
  40.7 0.7 %reshape.119 = f32[1,8,512]{2,1,0:T(8,128)} reshape(f32[8,8,64]{2,1,0:T(8,128)S(1)} %copy.50) | data formatting | bytes 32768 | tf_op jit(solution)/shard_map/reshape | solution.py:201
  (36 shorter events, 2.0 us)
Async XLA Ops:
  0.6 2.1 %copy-start.1 = (s32[1,1,1408]{2,1,0:T(1,128)S(1)}, s32[1,1,1408]{2,1,0:T(1,128)}, u32[]{:S(2)}) copy-start(s32[1,1,1408]{2,1,0:T(1,128)} %param.9) | copy-start | bytes 16900
  0.6 2.1 %copy-start.2 = (s32[1,1,1408]{2,1,0:T(1,128)S(1)}, s32[1,1,1408]{2,1,0:T(1,128)}, u32[]{:S(2)}) copy-start(s32[1,1,1408]{2,1,0:T(1,128)} %param.8) | copy-start | bytes 16900
  1.5 9.2 %copy-start = (bf16[32,4096]{1,0:T(8,128)(2,1)S(1)}, bf16[32,4096]{1,0:T(8,128)(2,1)}, u32[]{:S(2)}) copy-start(bf16[32,4096]{1,0:T(8,128)(2,1)} %param.7) | copy-start | bytes 786436
  3.5 15.2 %all-to-all-start = ((f32[8,47,128]{2,1,0:T(8,128)}), f32[8,47,128]{2,1,0:T(8,128)S(1)}, u32[]{:S(2)}, u32[]{:S(2)}) async-start(f32[8,47,128]{2,1,0:T(8,128)} %pad_maximum_fusion.1), calls=%async_computation | async-start | bytes 393216 | tf_op jit(solution)/shard_map/all_to_all | solution.py:135

commit v17 on v16

--- a/solution.py
+++ b/solution.py
@@ -121,10 +121,11 @@
     rows = tiles_dev + rays_dev + list_rows
     paired = rows + rows % 2
     if tiles_dev % 2 == 0 and rays_dev % 2 == 0 and nbd % (2 * width) == 0:
+        joined = jnp.concatenate([volume, sinogram[0]], axis=0)
+        joined = joined.reshape(tiles_dev + rays_dev, n_grp, width).transpose(1, 0, 2)
         send = jnp.concatenate(
             [
-                vol_send.reshape(n_grp, tiles_dev // 2, 2 * width),
-                sino_send.reshape(n_grp, rays_dev // 2, 2 * width),
+                joined.reshape(n_grp, (tiles_dev + rays_dev) // 2, 2 * width),
                 jnp.broadcast_to(cells.reshape(1, list_rows // 2, 2 * width), (n_grp, list_rows // 2, 2 * width)),
             ],
             axis=1,

time: 41.7 us -> 41.6 us (level)
    concatenate x0 -> x4, local copies, waits for them, and re-layouts: none -> 1.87 us  [per_device_split(): joined = jnp.concatenate([volume, sinogram[0]], axis=0)]
    reshape x4 -> x1, local copies, waits for them, and re-layouts: 1.28 us -> 0.1 us  [per_device_split(): joined.reshape(n_grp, (tiles_dev + rays_dev) // 2, 2 * width)]
    another operation x2 -> x0, local copies, waits for them, and re-layouts: 0.81 us -> none  [per_device_split(): sino_send = sinogram[0].reshape(rays_dev, n_grp, width).transpose(1, 0, 2)]
where the time goes in v17:
time: 41.6 us; the launch traced here: 41.3 us
  blocking collectives  10.5 us (25%)
  matrix products  8.11 us (19%)
  starting transfers between devices  7.25 us (17%)
  waiting for transfers between devices  6.5 us (16%)
  local copies, waits for them, and re-layouts  6.13 us (15%)
  other arithmetic  1.8 us (4%)
  between operations  0.98 us (2%)
    all_to_all x1, blocking collectives, per_device_split(): got_back = lax.all_to_all(back, ('pix', 'ang'), 0, 0, tiled=False)  10.5 us
    all_to_all x1, starting transfers between devices, per_device_split(): recv = lax.all_to_all(send, ('pix', 'ang'), 0, 0, tiled=False)  7.25 us
    all_to_all x1, waiting for transfers between devices, per_device_split(): recv = lax.all_to_all(send, ('pix', 'ang'), 0, 0, tiled=False)  6.5 us
    dot_general x1, matrix products, per_device_split(): jnp.einsum('gkbv,gkbu->gkvu', one_ray, one_pix, preferred_element_type=jn...  3.53 us
    concatenate x4, local copies, waits for them, and re-layouts, per_device_split(): joined = jnp.concatenate([volume, sinogram[0]], axis=0)  1.87 us
    dot_general x2, matrix products, per_device_split(): jnp.einsum('gkvu,gkvsj->usj', counts, spread, precision=lax.Precision.HIG...  1.44 us
    dot_general x2, matrix products, per_device_split(): jnp.einsum('gkvsj,kij->gvsi', gathered, pattern_wide, precision=lax.Preci...  1.29 us
    reshape x2, local copies, waits for them, and re-layouts, per_device_split(): pattern = table.reshape(KINDS, TILE, TILE)  1.07 us
  transfers between devices with their start and end apart: 1, of which 1 were waited for; matrix products, arithmetic and copies ran while one was open for 3% of the time, Pallas kernels for 0%

profile of v17, /device:TPU:0, one launch (start us, length us, event | category | flops | bytes accessed | tf_op | source)
XLA Modules:
  0.0 41.3 jit_solution(7527002967374490635)
XLA Ops:
  0.7 0.8 %concatenate.15 = f32[8,8,64]{2,1,0:T(8,128)S(1)} reshape(f32[1,8,512]{2,1,0:T(8,128)} %param.6) | data formatting | bytes 32768 | tf_op jit(solution)/shard_map/concatenate | solution.py:124
  1.5 1.0 %concatenate.14 = f32[64,8,64]{2,1,0:T(8,128)S(1)} reshape(f32[64,512]{1,0:T(8,128)} %param.5) | data formatting | bytes 262144 | tf_op jit(solution)/shard_map/concatenate | solution.py:124
  2.8 0.7 %pad_maximum_fusion.1 = f32[8,47,128]{2,1,0:T(8,128)} fusion(f32[8,11,128]{2,1,0:T(8,128)S(1)} %broadcast_in_dim.6, f32[8,36,128]{2,1,0:T(8,128)S(1)} %reshape.107), kind=kLoop, calls=%fused_computation.28 | loop fusion | flops 48128 | bytes 385024 | tf_op jit(solution)/shard_map/concatenate | solution.py:126
  3.4 7.3 %all-to-all-start = ((f32[8,47,128]{2,1,0:T(8,128)}), f32[8,47,128]{2,1,0:T(8,128)S(1)}, u32[]{:S(2)}, u32[]{:S(2)}) async-start(f32[8,47,128]{2,1,0:T(8,128)} %pad_maximum_fusion.1), calls=%async_computation | async-start | bytes 393216 | tf_op jit(solution)/shard_map/all_to_all | solution.py:136
  10.7 0.5 %reshape.117 = bf16[32,64,64,1]{2,1,0,3:T(8,128)(2,1)S(1)} reshape(bf16[32,4096]{1,0:T(8,128)(2,1)S(1)} %copy-done) | data formatting | bytes 524288 | tf_op jit(solution)/shard_map/reshape | solution.py:161
  11.2 0.5 %reshape.109 = bf16[32,64,64]{2,1,0:T(8,128)(2,1)S(1)} reshape(bf16[32,4096]{1,0:T(8,128)(2,1)S(1)} %copy-done) | data formatting | bytes 524288 | tf_op jit(solution)/shard_map/reshape | solution.py:161
  11.8 0.3 convert_reduce_fusion.2
  12.2 6.5 %all-to-all-done = f32[8,47,128]{2,1,0:T(8,128)S(1)} async-done(((f32[8,47,128]{2,1,0:T(8,128)}), f32[8,47,128]{2,1,0:T(8,128)S(1)}, u32[]{:S(2)}, u32[]{:S(2)}) %all-to-all-start) | async-done | bytes 192544 | tf_op jit(solution)/shard_map/all_to_all | solution.py:136
  19.6 0.2 reshape_squeeze_stack.6
  20.1 3.5 %fusion.2 = bf16[2,32,32,256]{3,2,1,0:T(8,128)(2,1)S(1)} fusion(s32[2,32,176]{2,1,0:T(8,128)S(1)} %eq.36, s32[2,32,176]{2,1,0:T(8,128)S(1)} %eq.32), kind=kOutput, calls=%fused_computation.6 | convolution fusion | flops 188317696 | bytes 1138688 | tf_op jit(solution)/shard_map/gkbv,gkbu->gkvu/dot_general | solution.py:153
  23.6 0.4 %convert_reduce_fusion = (f32[32,256]{1,0:T(8,128)S(1)}, f32[2,32,32]{2,1,0:T(8,128)S(1)}) fusion(bf16[2,32,32,256]{3,2,1,0:T(8,128)(2,1)S(1)} %fusion.2), kind=kLoop, calls=%fused_computation.3 | loop fusion | flops 1562624 | bytes 1089536 | tf_op jit(solution)/shard_map/gku,kj->uj/reduce_sum | solution.py:165
  24.1 0.4 fusion.16
  24.5 0.2 fusion.21
  24.7 0.6 %fusion.12 = bf16[2,32,64,1]{2,1,3,0:T(8,128)(2,1)S(1)} fusion(f32[2,32,64]{2,1,0:T(8,128)S(1)} %fusion.21, f32[2,32,32,64]{3,2,1,0:T(8,128)S(1)} %fusion.16, bf16[32,64,64,1]{2,1,0,3:T(8,128)(2,1)S(1)} %reshape.117, f32[4,2,94,64]{3,2,1,0:T(8,128)S(1)} %reshape.108), kind=kOutput, calls=%fused_computation.24 | convolution fusion | flops 100675584 | bytes 1646592 | tf_op jit(solution)/shard_map/gkvsj,kij->gvsi/dot_general | solution.py:177
  25.4 0.3 convolution_bitcast_fusion.1
  25.6 0.3 fusion.24
  25.9 0.7 %fusion.4 = f32[256,64]{0,1:T(8,128)S(1)} fusion(f32[256,64]{0,1:T(8,128)S(1)} %copy.60, f32[256,64]{0,1:T(8,128)S(1)} %fusion.24, bf16[2,32,32,256]{3,2,1,0:T(8,128)(2,1)S(1)} %fusion.2, f32[2,32,32,64]{3,2,1,0:T(8,128)S(1)} %convolution_bitcast_fusion.1), kind=kOutput, calls=%fused_computation.16 | convolution fusion | flops 201359360 | bytes 1769472 | tf_op jit(solution)/shard_map/gkvu,gkvsj->usj/dot_general | solution.py:184
  26.6 0.4 fusion.14
  27.1 0.6 %fusion.10 = f32[2,32,64]{2,1,0:T(8,128)S(1)} fusion(f32[2,32,64]{2,1,0:T(8,128)S(1)} %fusion.21, f32[2,32,32,64]{3,2,1,0:T(8,128)S(1)} %fusion.14, bf16[32,64,64,1]{2,1,0,3:T(8,128)(2,1)S(1)} %reshape.117, f32[4,2,94,64]{3,2,1,0:T(8,128)S(1)} %reshape.108), kind=kOutput, calls=%fused_computation.22 | convolution fusion | flops 100671488 | bytes 1654784 | tf_op jit(solution)/shard_map/gkvsj,kij->gvsi/dot_general | solution.py:177
  27.7 0.3 convolution_bitcast_fusion
  28.0 0.7 %fusion.6 = f32[256,64]{0,1:T(8,128)S(1)} fusion(f32[256,64]{0,1:T(8,128)S(1)} %fusion.4, f32[256,64]{0,1:T(8,128)S(1)} %fusion.24, bf16[2,32,32,256]{3,2,1,0:T(8,128)(2,1)S(1)} %fusion.2, f32[2,32,32,64]{3,2,1,0:T(8,128)S(1)} %convolution_bitcast_fusion), kind=kOutput, calls=%fused_computation.18 | convolution fusion | flops 201359360 | bytes 1769472 | tf_op jit(solution)/shard_map/gkvu,gkvsj->usj/dot_general | solution.py:184
  29.0 10.5 %all_to_all.10 = f32[8,36,128]{2,1,0:T(8,128)S(1)} all-to-all(f32[8,36,128]{2,1,0:T(8,128)S(1)} %reshape.113), channel_id=1, replica_groups=mesh['parts'=2,'pix'=4,'ang'=2,'sl'=2] {'pix','ang'}, dimensions={0} | all-to-all | bytes 294912 | tf_op jit(solution)/shard_map/all_to_all | solution.py:198
  39.8 0.8 %slice.23 = f32[64,512]{1,0:T(8,128)} reshape(f32[64,8,64]{2,1,0:T(8,128)S(1)} %copy.49) | data formatting | bytes 262144 | tf_op jit(solution)/shard_map/slice | solution.py:201
  40.6 0.7 %reshape.115 = f32[1,8,512]{2,1,0:T(8,128)} reshape(f32[8,8,64]{2,1,0:T(8,128)S(1)} %copy.50) | data formatting | bytes 32768 | tf_op jit(solution)/shard_map/reshape | solution.py:202
  (36 shorter events, 1.9 us)
Async XLA Ops:
  0.6 2.1 %copy-start.1 = (s32[1,1,1408]{2,1,0:T(1,128)S(1)}, s32[1,1,1408]{2,1,0:T(1,128)}, u32[]{:S(2)}) copy-start(s32[1,1,1408]{2,1,0:T(1,128)} %param.9) | copy-start | bytes 16900
  0.6 2.1 %copy-start.2 = (s32[1,1,1408]{2,1,0:T(1,128)S(1)}, s32[1,1,1408]{2,1,0:T(1,128)}, u32[]{:S(2)}) copy-start(s32[1,1,1408]{2,1,0:T(1,128)} %param.8) | copy-start | bytes 16900
  2.5 8.2 %copy-start = (bf16[32,4096]{1,0:T(8,128)(2,1)S(1)}, bf16[32,4096]{1,0:T(8,128)(2,1)}, u32[]{:S(2)}) copy-start(bf16[32,4096]{1,0:T(8,128)(2,1)} %param.7) | copy-start | bytes 786436
  3.4 15.2 %all-to-all-start = ((f32[8,47,128]{2,1,0:T(8,128)}), f32[8,47,128]{2,1,0:T(8,128)S(1)}, u32[]{:S(2)}, u32[]{:S(2)}) async-start(f32[8,47,128]{2,1,0:T(8,128)} %pad_maximum_fusion.1), calls=%async_computation | async-start | bytes 393216 | tf_op jit(solution)/shard_map/all_to_all | solution.py:136

commit v18 on v16

--- a/solution.py
+++ b/solution.py
@@ -138,17 +138,18 @@
     current = recv[:, 0, :tiles_dev].reshape(pix_total, width)
     measured = recv[:, :, tiles_dev:tiles_dev + rays_dev].transpose(1, 0, 2, 3).reshape(n_ang, ray_total, width)
     cells = recv[:, :, tiles_dev + rays_dev:].reshape(n_pix, n_ang, -1)[:, :, :nbd]
-    cells = cells.transpose(1, 0, 2).astype(jnp.int32)
-    got = jnp.stack([cells // tiles_dev, cells % tiles_dev])
+    cells = cells.transpose(1, 0, 2)
+    ray_of = jnp.floor(cells / tiles_dev)
+    got = jnp.stack([ray_of, cells - ray_of * tiles_dev])
     per_kind = nbd // KINDS
-    offsets = (jnp.arange(n_pix, dtype=jnp.int32) * tiles_dev)[None, :, None, None]
+    offsets = (jnp.arange(n_pix, dtype=jnp.float32) * tiles_dev)[None, :, None, None]
     ray_ids = got[0].reshape(n_ang, n_pix, KINDS, per_kind)
     pix_ids = got[1].reshape(n_ang, n_pix, KINDS, per_kind) + offsets
     ray_ids = ray_ids.transpose(0, 2, 1, 3).reshape(n_ang, KINDS, n_pix * per_kind)
     pix_ids = pix_ids.transpose(0, 2, 1, 3).reshape(n_ang, KINDS, n_pix * per_kind)
 
-    one_ray = (ray_ids[..., None] == jnp.arange(ray_total, dtype=jnp.int32)).astype(jnp.bfloat16)
-    one_pix = (pix_ids[..., None] == jnp.arange(pix_total, dtype=jnp.int32)).astype(jnp.bfloat16)
+    one_ray = (ray_ids[..., None] == jnp.arange(ray_total, dtype=jnp.float32)).astype(jnp.bfloat16)
+    one_pix = (pix_ids[..., None] == jnp.arange(pix_total, dtype=jnp.float32)).astype(jnp.bfloat16)
     count_low = jnp.einsum(
         "gkbv,gkbu->gkvu", one_ray, one_pix, preferred_element_type=jnp.float32
     ).astype(jnp.bfloat16)

time: 41.7 us -> 40.8 us (0.978)
  matrix products: 8.1 us -> 7.37 us
    dot_general x1, matrix products: 3.53 us -> 2.8 us  [per_device_split(): jnp.einsum('gkbv,gkbu->gkvu', one_ray, one_pix, preferred_element_type=jn...]
  transfers between devices with their start and end apart: 1 -> 1, of which waited for: 1 -> 1; matrix products, arithmetic and copies ran while one was open for 3% -> 4% of each run, Pallas kernels for 0% -> 0%
where the time goes in v18:
time: 40.8 us; the launch traced here: 40.5 us
  blocking collectives  10.5 us (26%)
  matrix products  7.37 us (18%)
  starting transfers between devices  7.25 us (18%)
  waiting for transfers between devices  6.49 us (16%)
  local copies, waits for them, and re-layouts  6.25 us (15%)
  other arithmetic  1.64 us (4%)
  between operations  0.96 us (2%)
    all_to_all x1, blocking collectives, per_device_split(): got_back = lax.all_to_all(back, ('pix', 'ang'), 0, 0, tiled=False)  10.5 us
    all_to_all x1, starting transfers between devices, per_device_split(): recv = lax.all_to_all(send, ('pix', 'ang'), 0, 0, tiled=False)  7.25 us
    all_to_all x1, waiting for transfers between devices, per_device_split(): recv = lax.all_to_all(send, ('pix', 'ang'), 0, 0, tiled=False)  6.49 us
    dot_general x1, matrix products, per_device_split(): jnp.einsum('gkbv,gkbu->gkvu', one_ray, one_pix, preferred_element_type=jn...  2.8 us
    dot_general x2, matrix products, per_device_split(): jnp.einsum('gkvu,gkvsj->usj', counts, spread, precision=lax.Precision.HIG...  1.44 us
    dot_general x2, matrix products, per_device_split(): jnp.einsum('gkvsj,kij->gvsi', gathered, pattern_wide, precision=lax.Preci...  1.29 us
    reshape x2, local copies, waits for them, and re-layouts, per_device_split(): vol_send = volume.reshape(tiles_dev, n_grp, width).transpose(1, 0, 2)  1.1 us
    reshape x2, local copies, waits for them, and re-layouts, per_device_split(): pattern = table.reshape(KINDS, TILE, TILE)  1.07 us
  transfers between devices with their start and end apart: 1, of which 1 were waited for; matrix products, arithmetic and copies ran while one was open for 4% of the time, Pallas kernels for 0%

profile of v18, /device:TPU:0, one launch (start us, length us, event | category | flops | bytes accessed | tf_op | source)
XLA Modules:
  0.0 40.5 jit_solution(4922586267908230487)
XLA Ops:
  0.7 0.8 %reshape_squeeze.3 = f32[8,8,64]{2,1,0:T(8,128)S(1)} reshape(f32[1,8,512]{2,1,0:T(8,128)} %param.6) | data formatting | bytes 32768 | tf_op jit(solution)/shard_map/reshape;squeeze | solution.py:116
  1.5 1.0 %reshape.110 = f32[64,8,64]{2,1,0:T(8,128)S(1)} reshape(f32[64,512]{1,0:T(8,128)} %param.5) | data formatting | bytes 262144 | tf_op jit(solution)/shard_map/reshape | solution.py:115
  2.8 0.7 %pad_maximum_fusion.1 = f32[8,47,128]{2,1,0:T(8,128)} fusion(f32[8,11,128]{2,1,0:T(8,128)S(1)} %broadcast_in_dim.6, f32[8,4,128]{2,1,0:T(4,128)S(1)} %reshape.112, f32[8,32,128]{2,1,0:T(8,128)S(1)} %reshape.111), kind=kLoop, calls=%fused_computation.28 | loop fusion | flops 96256 | bytes 385024 | tf_op jit(solution)/shard_map/concatenate | solution.py:124
  3.5 7.3 %all-to-all-start = ((f32[8,47,128]{2,1,0:T(8,128)}), f32[8,47,128]{2,1,0:T(8,128)S(1)}, u32[]{:S(2)}, u32[]{:S(2)}) async-start(f32[8,47,128]{2,1,0:T(8,128)} %pad_maximum_fusion.1), calls=%async_computation | async-start | bytes 393216 | tf_op jit(solution)/shard_map/all_to_all | solution.py:135
  10.8 0.5 %reshape.123 = bf16[32,64,64,1]{2,1,0,3:T(8,128)(2,1)S(1)} reshape(bf16[32,4096]{1,0:T(8,128)(2,1)S(1)} %copy-done) | data formatting | bytes 524288 | tf_op jit(solution)/shard_map/reshape | solution.py:161
  11.3 0.5 %reshape.115 = bf16[32,64,64]{2,1,0:T(8,128)(2,1)S(1)} reshape(bf16[32,4096]{1,0:T(8,128)(2,1)S(1)} %copy-done) | data formatting | bytes 524288 | tf_op jit(solution)/shard_map/reshape | solution.py:161
  11.9 0.3 convert_reduce_fusion.2
  12.2 6.5 %all-to-all-done = f32[8,47,128]{2,1,0:T(8,128)S(1)} async-done(((f32[8,47,128]{2,1,0:T(8,128)}), f32[8,47,128]{2,1,0:T(8,128)S(1)}, u32[]{:S(2)}, u32[]{:S(2)}) %all-to-all-start) | async-done | bytes 192544 | tf_op jit(solution)/shard_map/all_to_all | solution.py:135
  19.5 0.2 reshape_squeeze_stack.6
  20.0 2.8 %fusion.2 = bf16[2,32,32,256]{3,2,1,0:T(8,128)(2,1)S(1)} fusion(f32[2,32,176]{2,1,0:T(8,128)S(1)} %eq.34, f32[2,32,176]{2,1,0:T(8,128)S(1)} %eq.30), kind=kOutput, calls=%fused_computation.6 | convolution fusion | flops 188317696 | bytes 1138688 | tf_op jit(solution)/shard_map/gkbv,gkbu->gkvu/dot_general | solution.py:153
  22.8 0.4 %convert_reduce_fusion = (f32[32,256]{1,0:T(8,128)S(1)}, f32[2,32,32]{2,1,0:T(8,128)S(1)}) fusion(bf16[2,32,32,256]{3,2,1,0:T(8,128)(2,1)S(1)} %fusion.2), kind=kLoop, calls=%fused_computation.3 | loop fusion | flops 1562624 | bytes 1089536 | tf_op jit(solution)/shard_map/gku,kj->uj/reduce_sum | solution.py:165
  23.3 0.4 fusion.17
  23.7 0.2 fusion.22
  23.9 0.6 %fusion.12 = bf16[2,32,64,1]{2,1,3,0:T(8,128)(2,1)S(1)} fusion(f32[2,32,64]{2,1,0:T(8,128)S(1)} %fusion.22, f32[2,32,32,64]{3,2,1,0:T(8,128)S(1)} %fusion.17, bf16[32,64,64,1]{2,1,0,3:T(8,128)(2,1)S(1)} %reshape.123, f32[4,2,94,64]{3,2,1,0:T(8,128)S(1)} %reshape.113), kind=kOutput, calls=%fused_computation.24 | convolution fusion | flops 100675584 | bytes 1646592 | tf_op jit(solution)/shard_map/gkvsj,kij->gvsi/dot_general | solution.py:177
  24.6 0.3 convolution_bitcast_fusion.1
  24.9 0.3 fusion.25
  25.1 0.7 %fusion.4 = f32[256,64]{0,1:T(8,128)S(1)} fusion(f32[256,64]{0,1:T(8,128)S(1)} %copy.60, f32[256,64]{0,1:T(8,128)S(1)} %fusion.25, bf16[2,32,32,256]{3,2,1,0:T(8,128)(2,1)S(1)} %fusion.2, f32[2,32,32,64]{3,2,1,0:T(8,128)S(1)} %convolution_bitcast_fusion.1), kind=kOutput, calls=%fused_computation.16 | convolution fusion | flops 201359360 | bytes 1769472 | tf_op jit(solution)/shard_map/gkvu,gkvsj->usj/dot_general | solution.py:184
  25.9 0.4 fusion.15
  26.3 0.6 %fusion.10 = f32[2,32,64]{2,1,0:T(8,128)S(1)} fusion(f32[2,32,64]{2,1,0:T(8,128)S(1)} %fusion.22, f32[2,32,32,64]{3,2,1,0:T(8,128)S(1)} %fusion.15, bf16[32,64,64,1]{2,1,0,3:T(8,128)(2,1)S(1)} %reshape.123, f32[4,2,94,64]{3,2,1,0:T(8,128)S(1)} %reshape.113), kind=kOutput, calls=%fused_computation.22 | convolution fusion | flops 100671488 | bytes 1654784 | tf_op jit(solution)/shard_map/gkvsj,kij->gvsi/dot_general | solution.py:177
  26.9 0.3 convolution_bitcast_fusion
  27.2 0.7 %fusion.6 = f32[256,64]{0,1:T(8,128)S(1)} fusion(f32[256,64]{0,1:T(8,128)S(1)} %fusion.4, f32[256,64]{0,1:T(8,128)S(1)} %fusion.25, bf16[2,32,32,256]{3,2,1,0:T(8,128)(2,1)S(1)} %fusion.2, f32[2,32,32,64]{3,2,1,0:T(8,128)S(1)} %convolution_bitcast_fusion), kind=kOutput, calls=%fused_computation.18 | convolution fusion | flops 201359360 | bytes 1769472 | tf_op jit(solution)/shard_map/gkvu,gkvsj->usj/dot_general | solution.py:184
  28.2 10.5 %all_to_all.10 = f32[8,36,128]{2,1,0:T(8,128)S(1)} all-to-all(f32[8,36,128]{2,1,0:T(8,128)S(1)} %reshape.119), channel_id=1, replica_groups=mesh['parts'=2,'pix'=4,'ang'=2,'sl'=2] {'pix','ang'}, dimensions={0} | all-to-all | bytes 294912 | tf_op jit(solution)/shard_map/all_to_all | solution.py:198
  39.0 0.8 %slice.23 = f32[64,512]{1,0:T(8,128)} reshape(f32[64,8,64]{2,1,0:T(8,128)S(1)} %copy.49) | data formatting | bytes 262144 | tf_op jit(solution)/shard_map/slice | solution.py:201
  39.8 0.7 %reshape.121 = f32[1,8,512]{2,1,0:T(8,128)} reshape(f32[8,8,64]{2,1,0:T(8,128)S(1)} %copy.50) | data formatting | bytes 32768 | tf_op jit(solution)/shard_map/reshape | solution.py:202
  (36 shorter events, 1.9 us)
Async XLA Ops:
  0.6 2.1 %copy-start.1 = (s32[1,1,1408]{2,1,0:T(1,128)S(1)}, s32[1,1,1408]{2,1,0:T(1,128)}, u32[]{:S(2)}) copy-start(s32[1,1,1408]{2,1,0:T(1,128)} %param.9) | copy-start | bytes 16900
  0.6 2.1 %copy-start.2 = (s32[1,1,1408]{2,1,0:T(1,128)S(1)}, s32[1,1,1408]{2,1,0:T(1,128)}, u32[]{:S(2)}) copy-start(s32[1,1,1408]{2,1,0:T(1,128)} %param.8) | copy-start | bytes 16900
  1.5 9.2 %copy-start = (bf16[32,4096]{1,0:T(8,128)(2,1)S(1)}, bf16[32,4096]{1,0:T(8,128)(2,1)}, u32[]{:S(2)}) copy-start(bf16[32,4096]{1,0:T(8,128)(2,1)} %param.7) | copy-start | bytes 786436
  3.5 15.2 %all-to-all-start = ((f32[8,47,128]{2,1,0:T(8,128)}), f32[8,47,128]{2,1,0:T(8,128)S(1)}, u32[]{:S(2)}, u32[]{:S(2)}) async-start(f32[8,47,128]{2,1,0:T(8,128)} %pad_maximum_fusion.1), calls=%async_computation | async-start | bytes 393216 | tf_op jit(solution)/shard_map/all_to_all | solution.py:135

commit v19 on v18

--- a/solution.py
+++ b/solution.py
@@ -121,11 +121,15 @@
     rows = tiles_dev + rays_dev + list_rows
     paired = rows + rows % 2
     if tiles_dev % 2 == 0 and rays_dev % 2 == 0 and nbd % (2 * width) == 0:
+        cell_rows = (
+            blk_ray.reshape(list_rows // 2, 2 * width).astype(jnp.float32) * tiles_dev
+            + blk_pix.reshape(list_rows // 2, 2 * width).astype(jnp.float32)
+        )
         send = jnp.concatenate(
             [
                 vol_send.reshape(n_grp, tiles_dev // 2, 2 * width),
                 sino_send.reshape(n_grp, rays_dev // 2, 2 * width),
-                jnp.broadcast_to(cells.reshape(1, list_rows // 2, 2 * width), (n_grp, list_rows // 2, 2 * width)),
+                jnp.broadcast_to(cell_rows[None], (n_grp, list_rows // 2, 2 * width)),
             ],
             axis=1,
         )

time: 40.8 us -> 40.8 us (level)
  no operation moved by 1% of the time
where the time goes in v19:
time: 40.8 us; the launch traced here: 40.5 us
  blocking collectives  10.5 us (26%)
  matrix products  7.37 us (18%)
  starting transfers between devices  7.25 us (18%)
  waiting for transfers between devices  6.49 us (16%)
  local copies, waits for them, and re-layouts  6.25 us (15%)
  other arithmetic  1.64 us (4%)
  between operations  0.96 us (2%)
    all_to_all x1, blocking collectives, per_device_split(): got_back = lax.all_to_all(back, ('pix', 'ang'), 0, 0, tiled=False)  10.5 us
    all_to_all x1, starting transfers between devices, per_device_split(): recv = lax.all_to_all(send, ('pix', 'ang'), 0, 0, tiled=False)  7.25 us
    all_to_all x1, waiting for transfers between devices, per_device_split(): recv = lax.all_to_all(send, ('pix', 'ang'), 0, 0, tiled=False)  6.49 us
    dot_general x1, matrix products, per_device_split(): jnp.einsum('gkbv,gkbu->gkvu', one_ray, one_pix, preferred_element_type=jn...  2.8 us
    dot_general x2, matrix products, per_device_split(): jnp.einsum('gkvu,gkvsj->usj', counts, spread, precision=lax.Precision.HIG...  1.44 us
    dot_general x2, matrix products, per_device_split(): jnp.einsum('gkvsj,kij->gvsi', gathered, pattern_wide, precision=lax.Preci...  1.29 us
    reshape x2, local copies, waits for them, and re-layouts, per_device_split(): vol_send = volume.reshape(tiles_dev, n_grp, width).transpose(1, 0, 2)  1.1 us
    reshape x2, local copies, waits for them, and re-layouts, per_device_split(): pattern = table.reshape(KINDS, TILE, TILE)  1.07 us
  transfers between devices with their start and end apart: 1, of which 1 were waited for; matrix products, arithmetic and copies ran while one was open for 4% of the time, Pallas kernels for 0%

profile of v19, /device:TPU:0, one launch (start us, length us, event | category | flops | bytes accessed | tf_op | source)
XLA Modules:
  0.0 40.5 jit_solution(2963637094372213060)
XLA Ops:
  0.7 0.8 %reshape_squeeze.3 = f32[8,8,64]{2,1,0:T(8,128)S(1)} reshape(f32[1,8,512]{2,1,0:T(8,128)} %param.6) | data formatting | bytes 32768 | tf_op jit(solution)/shard_map/reshape;squeeze | solution.py:116
  1.5 1.0 %reshape.111 = f32[64,8,64]{2,1,0:T(8,128)S(1)} reshape(f32[64,512]{1,0:T(8,128)} %param.5) | data formatting | bytes 262144 | tf_op jit(solution)/shard_map/reshape | solution.py:115
  2.8 0.7 %pad_maximum_fusion.1 = f32[8,47,128]{2,1,0:T(8,128)} fusion(f32[8,11,128]{2,1,0:T(8,128)S(1)} %broadcast_in_dim.6, f32[8,4,128]{2,1,0:T(4,128)S(1)} %reshape.113, f32[8,32,128]{2,1,0:T(8,128)S(1)} %reshape.112), kind=kLoop, calls=%fused_computation.28 | loop fusion | flops 96256 | bytes 385024 | tf_op jit(solution)/shard_map/concatenate | solution.py:128
  3.5 7.3 %all-to-all-start = ((f32[8,47,128]{2,1,0:T(8,128)}), f32[8,47,128]{2,1,0:T(8,128)S(1)}, u32[]{:S(2)}, u32[]{:S(2)}) async-start(f32[8,47,128]{2,1,0:T(8,128)} %pad_maximum_fusion.1), calls=%async_computation | async-start | bytes 393216 | tf_op jit(solution)/shard_map/all_to_all | solution.py:139
  10.8 0.5 %reshape.124 = bf16[32,64,64,1]{2,1,0,3:T(8,128)(2,1)S(1)} reshape(bf16[32,4096]{1,0:T(8,128)(2,1)S(1)} %copy-done) | data formatting | bytes 524288 | tf_op jit(solution)/shard_map/reshape | solution.py:165
  11.3 0.5 %reshape.116 = bf16[32,64,64]{2,1,0:T(8,128)(2,1)S(1)} reshape(bf16[32,4096]{1,0:T(8,128)(2,1)S(1)} %copy-done) | data formatting | bytes 524288 | tf_op jit(solution)/shard_map/reshape | solution.py:165
  11.9 0.3 convert_reduce_fusion.2
  12.2 6.5 %all-to-all-done = f32[8,47,128]{2,1,0:T(8,128)S(1)} async-done(((f32[8,47,128]{2,1,0:T(8,128)}), f32[8,47,128]{2,1,0:T(8,128)S(1)}, u32[]{:S(2)}, u32[]{:S(2)}) %all-to-all-start) | async-done | bytes 192544 | tf_op jit(solution)/shard_map/all_to_all | solution.py:139
  19.5 0.2 reshape_squeeze_stack.6
  20.0 2.8 %fusion.2 = bf16[2,32,32,256]{3,2,1,0:T(8,128)(2,1)S(1)} fusion(f32[2,32,176]{2,1,0:T(8,128)S(1)} %eq.34, f32[2,32,176]{2,1,0:T(8,128)S(1)} %eq.30), kind=kOutput, calls=%fused_computation.6 | convolution fusion | flops 188317696 | bytes 1138688 | tf_op jit(solution)/shard_map/gkbv,gkbu->gkvu/dot_general | solution.py:157
  22.8 0.4 %convert_reduce_fusion = (f32[32,256]{1,0:T(8,128)S(1)}, f32[2,32,32]{2,1,0:T(8,128)S(1)}) fusion(bf16[2,32,32,256]{3,2,1,0:T(8,128)(2,1)S(1)} %fusion.2), kind=kLoop, calls=%fused_computation.3 | loop fusion | flops 1562624 | bytes 1089536 | tf_op jit(solution)/shard_map/gku,kj->uj/reduce_sum | solution.py:169
  23.3 0.4 fusion.17
  23.7 0.2 fusion.22
  23.9 0.6 %fusion.12 = bf16[2,32,64,1]{2,1,3,0:T(8,128)(2,1)S(1)} fusion(f32[2,32,64]{2,1,0:T(8,128)S(1)} %fusion.22, f32[2,32,32,64]{3,2,1,0:T(8,128)S(1)} %fusion.17, bf16[32,64,64,1]{2,1,0,3:T(8,128)(2,1)S(1)} %reshape.124, f32[4,2,94,64]{3,2,1,0:T(8,128)S(1)} %reshape.114), kind=kOutput, calls=%fused_computation.24 | convolution fusion | flops 100675584 | bytes 1646592 | tf_op jit(solution)/shard_map/gkvsj,kij->gvsi/dot_general | solution.py:181
  24.6 0.3 convolution_bitcast_fusion.1
  24.9 0.3 fusion.25
  25.1 0.7 %fusion.4 = f32[256,64]{0,1:T(8,128)S(1)} fusion(f32[256,64]{0,1:T(8,128)S(1)} %copy.60, f32[256,64]{0,1:T(8,128)S(1)} %fusion.25, bf16[2,32,32,256]{3,2,1,0:T(8,128)(2,1)S(1)} %fusion.2, f32[2,32,32,64]{3,2,1,0:T(8,128)S(1)} %convolution_bitcast_fusion.1), kind=kOutput, calls=%fused_computation.16 | convolution fusion | flops 201359360 | bytes 1769472 | tf_op jit(solution)/shard_map/gkvu,gkvsj->usj/dot_general | solution.py:188
  25.9 0.4 fusion.15
  26.3 0.6 %fusion.10 = f32[2,32,64]{2,1,0:T(8,128)S(1)} fusion(f32[2,32,64]{2,1,0:T(8,128)S(1)} %fusion.22, f32[2,32,32,64]{3,2,1,0:T(8,128)S(1)} %fusion.15, bf16[32,64,64,1]{2,1,0,3:T(8,128)(2,1)S(1)} %reshape.124, f32[4,2,94,64]{3,2,1,0:T(8,128)S(1)} %reshape.114), kind=kOutput, calls=%fused_computation.22 | convolution fusion | flops 100671488 | bytes 1654784 | tf_op jit(solution)/shard_map/gkvsj,kij->gvsi/dot_general | solution.py:181
  26.9 0.3 convolution_bitcast_fusion
  27.2 0.7 %fusion.6 = f32[256,64]{0,1:T(8,128)S(1)} fusion(f32[256,64]{0,1:T(8,128)S(1)} %fusion.4, f32[256,64]{0,1:T(8,128)S(1)} %fusion.25, bf16[2,32,32,256]{3,2,1,0:T(8,128)(2,1)S(1)} %fusion.2, f32[2,32,32,64]{3,2,1,0:T(8,128)S(1)} %convolution_bitcast_fusion), kind=kOutput, calls=%fused_computation.18 | convolution fusion | flops 201359360 | bytes 1769472 | tf_op jit(solution)/shard_map/gkvu,gkvsj->usj/dot_general | solution.py:188
  28.2 10.5 %all_to_all.10 = f32[8,36,128]{2,1,0:T(8,128)S(1)} all-to-all(f32[8,36,128]{2,1,0:T(8,128)S(1)} %reshape.120), channel_id=1, replica_groups=mesh['parts'=2,'pix'=4,'ang'=2,'sl'=2] {'pix','ang'}, dimensions={0} | all-to-all | bytes 294912 | tf_op jit(solution)/shard_map/all_to_all | solution.py:202
  39.0 0.8 %slice.23 = f32[64,512]{1,0:T(8,128)} reshape(f32[64,8,64]{2,1,0:T(8,128)S(1)} %copy.49) | data formatting | bytes 262144 | tf_op jit(solution)/shard_map/slice | solution.py:205
  39.8 0.7 %reshape.122 = f32[1,8,512]{2,1,0:T(8,128)} reshape(f32[8,8,64]{2,1,0:T(8,128)S(1)} %copy.50) | data formatting | bytes 32768 | tf_op jit(solution)/shard_map/reshape | solution.py:206
  (36 shorter events, 1.9 us)
Async XLA Ops:
  0.6 2.1 %copy-start.1 = (s32[1,1,1408]{2,1,0:T(1,128)S(1)}, s32[1,1,1408]{2,1,0:T(1,128)}, u32[]{:S(2)}) copy-start(s32[1,1,1408]{2,1,0:T(1,128)} %param.9) | copy-start | bytes 16900
  0.6 2.1 %copy-start.2 = (s32[1,1,1408]{2,1,0:T(1,128)S(1)}, s32[1,1,1408]{2,1,0:T(1,128)}, u32[]{:S(2)}) copy-start(s32[1,1,1408]{2,1,0:T(1,128)} %param.8) | copy-start | bytes 16900
  1.5 9.2 %copy-start = (bf16[32,4096]{1,0:T(8,128)(2,1)S(1)}, bf16[32,4096]{1,0:T(8,128)(2,1)}, u32[]{:S(2)}) copy-start(bf16[32,4096]{1,0:T(8,128)(2,1)} %param.7) | copy-start | bytes 786436
  3.5 15.2 %all-to-all-start = ((f32[8,47,128]{2,1,0:T(8,128)}), f32[8,47,128]{2,1,0:T(8,128)S(1)}, u32[]{:S(2)}, u32[]{:S(2)}) async-start(f32[8,47,128]{2,1,0:T(8,128)} %pad_maximum_fusion.1), calls=%async_computation | async-start | bytes 393216 | tf_op jit(solution)/shard_map/all_to_all | solution.py:139

commit v20 on v18

--- a/solution.py
+++ b/solution.py
@@ -190,11 +190,20 @@
     vol_back = cur.reshape(n_pix, tiles_dev, width)
     vol_back = jnp.broadcast_to(vol_back[:, None], (n_pix, n_ang, tiles_dev, width))
     res_back = scaled.reshape(n_ang, n_pix, rays_dev, width).transpose(1, 0, 2, 3)
-    back = jnp.concatenate([vol_back, res_back], axis=2).reshape(n_grp, tiles_dev + rays_dev, width)
     rows_back = tiles_dev + rays_dev
     paired_back = rows_back + rows_back % 2
-    back = jnp.pad(back, ((0, 0), (0, paired_back - rows_back), (0, 0)))
-    back = back.reshape(n_grp, paired_back // 2, 2 * width)
+    if tiles_dev % 2 == 0 and rays_dev % 2 == 0:
+        back = jnp.concatenate(
+            [
+                vol_back.reshape(n_pix, n_ang, tiles_dev // 2, 2 * width),
+                res_back.reshape(n_pix, n_ang, rays_dev // 2, 2 * width),
+            ],
+            axis=2,
+        ).reshape(n_grp, paired_back // 2, 2 * width)
+    else:
+        back = jnp.concatenate([vol_back, res_back], axis=2).reshape(n_grp, rows_back, width)
+        back = jnp.pad(back, ((0, 0), (0, paired_back - rows_back), (0, 0)))
+        back = back.reshape(n_grp, paired_back // 2, 2 * width)
     got_back = lax.all_to_all(back, ("pix", "ang"), 0, 0, tiled=False)
     got_back = got_back.reshape(n_grp, paired_back, width)[:, :rows_back]
     both = got_back.transpose(1, 0, 2).reshape(rows_back, slices * TILE)

time: 40.8 us -> 40.8 us (level)
  no operation moved by 1% of the time
where the time goes in v20:
time: 40.8 us; the launch traced here: 40.5 us
  blocking collectives  10.5 us (26%)
  matrix products  7.37 us (18%)
  starting transfers between devices  7.25 us (18%)
  waiting for transfers between devices  6.49 us (16%)
  local copies, waits for them, and re-layouts  6.3 us (15%)
  other arithmetic  1.63 us (4%)
  between operations  0.96 us (2%)
    all_to_all x1, blocking collectives, per_device_split(): got_back = lax.all_to_all(back, ('pix', 'ang'), 0, 0, tiled=False)  10.5 us
    all_to_all x1, starting transfers between devices, per_device_split(): recv = lax.all_to_all(send, ('pix', 'ang'), 0, 0, tiled=False)  7.25 us
    all_to_all x1, waiting for transfers between devices, per_device_split(): recv = lax.all_to_all(send, ('pix', 'ang'), 0, 0, tiled=False)  6.49 us
    dot_general x1, matrix products, per_device_split(): jnp.einsum('gkbv,gkbu->gkvu', one_ray, one_pix, preferred_element_type=jn...  2.8 us
    dot_general x2, matrix products, per_device_split(): jnp.einsum('gkvu,gkvsj->usj', counts, spread, precision=lax.Precision.HIG...  1.43 us
    dot_general x2, matrix products, per_device_split(): jnp.einsum('gkvsj,kij->gvsi', gathered, pattern_wide, precision=lax.Preci...  1.29 us
    reshape x2, local copies, waits for them, and re-layouts, per_device_split(): vol_send = volume.reshape(tiles_dev, n_grp, width).transpose(1, 0, 2)  1.1 us
    reshape x2, local copies, waits for them, and re-layouts, per_device_split(): pattern = table.reshape(KINDS, TILE, TILE)  1.07 us
  transfers between devices with their start and end apart: 1, of which 1 were waited for; matrix products, arithmetic and copies ran while one was open for 4% of the time, Pallas kernels for 0%

profile of v20, /device:TPU:0, one launch (start us, length us, event | category | flops | bytes accessed | tf_op | source)
XLA Modules:
  0.0 40.5 jit_solution(2661247675569639161)
XLA Ops:
  0.7 0.8 %reshape_squeeze.3 = f32[8,8,64]{2,1,0:T(8,128)S(1)} reshape(f32[1,8,512]{2,1,0:T(8,128)} %param.6) | data formatting | bytes 32768 | tf_op jit(solution)/shard_map/reshape;squeeze | solution.py:116
  1.5 1.0 %reshape.113 = f32[64,8,64]{2,1,0:T(8,128)S(1)} reshape(f32[64,512]{1,0:T(8,128)} %param.5) | data formatting | bytes 262144 | tf_op jit(solution)/shard_map/reshape | solution.py:115
  2.8 0.7 %pad_maximum_fusion = f32[8,47,128]{2,1,0:T(8,128)} fusion(f32[8,11,128]{2,1,0:T(8,128)S(1)} %broadcast_in_dim.6, f32[8,4,128]{2,1,0:T(4,128)S(1)} %reshape.115, f32[8,32,128]{2,1,0:T(8,128)S(1)} %reshape.114), kind=kLoop, calls=%fused_computation.27 | loop fusion | flops 96256 | bytes 385024 | tf_op jit(solution)/shard_map/concatenate | solution.py:124
  3.5 7.3 %all-to-all-start = ((f32[8,47,128]{2,1,0:T(8,128)}), f32[8,47,128]{2,1,0:T(8,128)S(1)}, u32[]{:S(2)}, u32[]{:S(2)}) async-start(f32[8,47,128]{2,1,0:T(8,128)} %pad_maximum_fusion), calls=%async_computation | async-start | bytes 393216 | tf_op jit(solution)/shard_map/all_to_all | solution.py:135
  10.8 0.5 %reshape.125 = bf16[32,64,64,1]{2,1,0,3:T(8,128)(2,1)S(1)} reshape(bf16[32,4096]{1,0:T(8,128)(2,1)S(1)} %copy-done) | data formatting | bytes 524288 | tf_op jit(solution)/shard_map/reshape | solution.py:161
  11.3 0.5 %reshape.118 = bf16[32,64,64]{2,1,0:T(8,128)(2,1)S(1)} reshape(bf16[32,4096]{1,0:T(8,128)(2,1)S(1)} %copy-done) | data formatting | bytes 524288 | tf_op jit(solution)/shard_map/reshape | solution.py:161
  11.9 0.3 convert_reduce_fusion.2
  12.2 6.5 %all-to-all-done = f32[8,47,128]{2,1,0:T(8,128)S(1)} async-done(((f32[8,47,128]{2,1,0:T(8,128)}), f32[8,47,128]{2,1,0:T(8,128)S(1)}, u32[]{:S(2)}, u32[]{:S(2)}) %all-to-all-start) | async-done | bytes 192544 | tf_op jit(solution)/shard_map/all_to_all | solution.py:135
  19.5 0.2 reshape_squeeze_stack.6
  20.0 2.8 %fusion.2 = bf16[2,32,32,256]{3,2,1,0:T(8,128)(2,1)S(1)} fusion(f32[2,32,176]{2,1,0:T(8,128)S(1)} %eq.34, f32[2,32,176]{2,1,0:T(8,128)S(1)} %eq.30), kind=kOutput, calls=%fused_computation.6 | convolution fusion | flops 188317696 | bytes 1138688 | tf_op jit(solution)/shard_map/gkbv,gkbu->gkvu/dot_general | solution.py:153
  22.8 0.4 %convert_reduce_fusion = (f32[32,256]{1,0:T(8,128)S(1)}, f32[2,32,32]{2,1,0:T(8,128)S(1)}) fusion(bf16[2,32,32,256]{3,2,1,0:T(8,128)(2,1)S(1)} %fusion.2), kind=kLoop, calls=%fused_computation.3 | loop fusion | flops 1562624 | bytes 1089536 | tf_op jit(solution)/shard_map/gku,kj->uj/reduce_sum | solution.py:165
  23.3 0.4 fusion.17
  23.7 0.2 fusion.22
  23.9 0.6 %fusion.12 = bf16[2,32,64,1]{2,1,3,0:T(8,128)(2,1)S(1)} fusion(f32[2,32,64]{2,1,0:T(8,128)S(1)} %fusion.22, f32[2,32,32,64]{3,2,1,0:T(8,128)S(1)} %fusion.17, bf16[32,64,64,1]{2,1,0,3:T(8,128)(2,1)S(1)} %reshape.125, f32[4,2,94,64]{3,2,1,0:T(8,128)S(1)} %reshape.116), kind=kOutput, calls=%fused_computation.24 | convolution fusion | flops 100675584 | bytes 1646592 | tf_op jit(solution)/shard_map/gkvsj,kij->gvsi/dot_general | solution.py:177
  24.6 0.3 convolution_bitcast_fusion.1
  24.9 0.3 fusion.25
  25.1 0.7 %fusion.4 = f32[256,64]{0,1:T(8,128)S(1)} fusion(f32[256,64]{0,1:T(8,128)S(1)} %copy.58, f32[256,64]{0,1:T(8,128)S(1)} %fusion.25, bf16[2,32,32,256]{3,2,1,0:T(8,128)(2,1)S(1)} %fusion.2, f32[2,32,32,64]{3,2,1,0:T(8,128)S(1)} %convolution_bitcast_fusion.1), kind=kOutput, calls=%fused_computation.16 | convolution fusion | flops 201359360 | bytes 1769472 | tf_op jit(solution)/shard_map/gkvu,gkvsj->usj/dot_general | solution.py:184
  25.9 0.4 fusion.15
  26.3 0.6 %fusion.10 = f32[2,32,64]{2,1,0:T(8,128)S(1)} fusion(f32[2,32,64]{2,1,0:T(8,128)S(1)} %fusion.22, f32[2,32,32,64]{3,2,1,0:T(8,128)S(1)} %fusion.15, bf16[32,64,64,1]{2,1,0,3:T(8,128)(2,1)S(1)} %reshape.125, f32[4,2,94,64]{3,2,1,0:T(8,128)S(1)} %reshape.116), kind=kOutput, calls=%fused_computation.22 | convolution fusion | flops 100671488 | bytes 1654784 | tf_op jit(solution)/shard_map/gkvsj,kij->gvsi/dot_general | solution.py:177
  26.9 0.3 convolution_bitcast_fusion
  27.3 0.7 %fusion.6 = f32[256,64]{0,1:T(8,128)S(1)} fusion(f32[256,64]{0,1:T(8,128)S(1)} %fusion.4, f32[256,64]{0,1:T(8,128)S(1)} %fusion.25, bf16[2,32,32,256]{3,2,1,0:T(8,128)(2,1)S(1)} %fusion.2, f32[2,32,32,64]{3,2,1,0:T(8,128)S(1)} %convolution_bitcast_fusion), kind=kOutput, calls=%fused_computation.18 | convolution fusion | flops 201359360 | bytes 1769472 | tf_op jit(solution)/shard_map/gkvu,gkvsj->usj/dot_general | solution.py:184
  28.2 10.5 %all_to_all.10 = f32[8,36,128]{2,1,0:T(8,128)S(1)} all-to-all(f32[8,36,128]{2,1,0:T(8,128)S(1)} %pad_maximum_fusion.1), channel_id=1, replica_groups=mesh['parts'=2,'pix'=4,'ang'=2,'sl'=2] {'pix','ang'}, dimensions={0} | all-to-all | bytes 294912 | tf_op jit(solution)/shard_map/all_to_all | solution.py:207
  39.0 0.8 %slice.23 = f32[64,512]{1,0:T(8,128)} reshape(f32[64,8,64]{2,1,0:T(8,128)S(1)} %copy.47) | data formatting | bytes 262144 | tf_op jit(solution)/shard_map/slice | solution.py:210
  39.8 0.7 %reshape.123 = f32[1,8,512]{2,1,0:T(8,128)} reshape(f32[8,8,64]{2,1,0:T(8,128)S(1)} %copy.48) | data formatting | bytes 32768 | tf_op jit(solution)/shard_map/reshape | solution.py:211
  (37 shorter events, 1.9 us)
Async XLA Ops:
  0.6 2.1 %copy-start.1 = (s32[1,1,1408]{2,1,0:T(1,128)S(1)}, s32[1,1,1408]{2,1,0:T(1,128)}, u32[]{:S(2)}) copy-start(s32[1,1,1408]{2,1,0:T(1,128)} %param.9) | copy-start | bytes 16900
  0.6 2.1 %copy-start.2 = (s32[1,1,1408]{2,1,0:T(1,128)S(1)}, s32[1,1,1408]{2,1,0:T(1,128)}, u32[]{:S(2)}) copy-start(s32[1,1,1408]{2,1,0:T(1,128)} %param.8) | copy-start | bytes 16900
  1.5 9.2 %copy-start = (bf16[32,4096]{1,0:T(8,128)(2,1)S(1)}, bf16[32,4096]{1,0:T(8,128)(2,1)}, u32[]{:S(2)}) copy-start(bf16[32,4096]{1,0:T(8,128)(2,1)} %param.7) | copy-start | bytes 786436
  3.5 15.2 %all-to-all-start = ((f32[8,47,128]{2,1,0:T(8,128)}), f32[8,47,128]{2,1,0:T(8,128)S(1)}, u32[]{:S(2)}, u32[]{:S(2)}) async-start(f32[8,47,128]{2,1,0:T(8,128)} %pad_maximum_fusion), calls=%async_computation | async-start | bytes 393216 | tf_op jit(solution)/shard_map/all_to_all | solution.py:135

commit v21 on v18

--- a/solution.py
+++ b/solution.py
@@ -153,7 +153,7 @@
     count_low = jnp.einsum(
         "gkbv,gkbu->gkvu", one_ray, one_pix, preferred_element_type=jnp.float32
     ).astype(jnp.bfloat16)
-    count_low = lax.optimization_barrier(count_low)
+
     counts = count_low.astype(jnp.float32)
     ray_count = jnp.sum(counts, axis=3)
     pix_count = jnp.sum(counts, axis=2)

time: 40.8 us -> 40.8 us (level)
  other arithmetic: 1.64 us -> 1.21 us
  matrix products: 7.37 us -> 7.78 us
    reduce_sum x1 -> x0, other arithmetic: 0.43 us -> none  [per_device_split(): jnp.einsum('gku,kj->uj', pix_count, jnp.sum(pattern_wide, axis=1), precis...]
where the time goes in v21:
time: 40.8 us; the launch traced here: 40.4 us
  blocking collectives  10.5 us (26%)
  matrix products  7.78 us (19%)
  starting transfers between devices  7.25 us (18%)
  waiting for transfers between devices  6.49 us (16%)
  local copies, waits for them, and re-layouts  6.25 us (15%)
  other arithmetic  1.21 us (3%)
  between operations  0.95 us (2%)
    all_to_all x1, blocking collectives, per_device_split(): got_back = lax.all_to_all(back, ('pix', 'ang'), 0, 0, tiled=False)  10.5 us
    all_to_all x1, starting transfers between devices, per_device_split(): recv = lax.all_to_all(send, ('pix', 'ang'), 0, 0, tiled=False)  7.25 us
    all_to_all x1, waiting for transfers between devices, per_device_split(): recv = lax.all_to_all(send, ('pix', 'ang'), 0, 0, tiled=False)  6.49 us
    dot_general x1, matrix products, per_device_split(): jnp.einsum('gkbv,gkbu->gkvu', one_ray, one_pix, preferred_element_type=jn...  3.17 us
    dot_general x2, matrix products, per_device_split(): jnp.einsum('gkvu,gkvsj->usj', counts, spread, precision=lax.Precision.HIG...  1.46 us
    dot_general x2, matrix products, per_device_split(): jnp.einsum('gkvsj,kij->gvsi', gathered, pattern_wide, precision=lax.Preci...  1.29 us
    reshape x2, local copies, waits for them, and re-layouts, per_device_split(): vol_send = volume.reshape(tiles_dev, n_grp, width).transpose(1, 0, 2)  1.1 us
    reshape x2, local copies, waits for them, and re-layouts, per_device_split(): pattern = table.reshape(KINDS, TILE, TILE)  1.07 us
  transfers between devices with their start and end apart: 1, of which 1 were waited for; matrix products, arithmetic and copies ran while one was open for 4% of the time, Pallas kernels for 0%

profile of v21, /device:TPU:0, one launch (start us, length us, event | category | flops | bytes accessed | tf_op | source)
XLA Modules:
  0.0 40.4 jit_solution(1518219244483959502)
XLA Ops:
  0.7 0.8 %reshape_squeeze.3 = f32[8,8,64]{2,1,0:T(8,128)S(1)} reshape(f32[1,8,512]{2,1,0:T(8,128)} %param.6) | data formatting | bytes 32768 | tf_op jit(solution)/shard_map/reshape;squeeze | solution.py:116
  1.5 1.0 %reshape.110 = f32[64,8,64]{2,1,0:T(8,128)S(1)} reshape(f32[64,512]{1,0:T(8,128)} %param.5) | data formatting | bytes 262144 | tf_op jit(solution)/shard_map/reshape | solution.py:115
  2.8 0.7 %pad_maximum_fusion.1 = f32[8,47,128]{2,1,0:T(8,128)} fusion(f32[8,11,128]{2,1,0:T(8,128)S(1)} %broadcast_in_dim.6, f32[8,4,128]{2,1,0:T(4,128)S(1)} %reshape.112, f32[8,32,128]{2,1,0:T(8,128)S(1)} %reshape.111), kind=kLoop, calls=%fused_computation.28 | loop fusion | flops 96256 | bytes 385024 | tf_op jit(solution)/shard_map/concatenate | solution.py:124
  3.5 7.3 %all-to-all-start = ((f32[8,47,128]{2,1,0:T(8,128)}), f32[8,47,128]{2,1,0:T(8,128)S(1)}, u32[]{:S(2)}, u32[]{:S(2)}) async-start(f32[8,47,128]{2,1,0:T(8,128)} %pad_maximum_fusion.1), calls=%async_computation | async-start | bytes 393216 | tf_op jit(solution)/shard_map/all_to_all | solution.py:135
  10.8 0.5 %reshape.123 = bf16[32,64,64,1]{2,1,0,3:T(8,128)(2,1)S(1)} reshape(bf16[32,4096]{1,0:T(8,128)(2,1)S(1)} %copy-done) | data formatting | bytes 524288 | tf_op jit(solution)/shard_map/reshape | solution.py:161
  11.3 0.5 %reshape.115 = bf16[32,64,64]{2,1,0:T(8,128)(2,1)S(1)} reshape(bf16[32,4096]{1,0:T(8,128)(2,1)S(1)} %copy-done) | data formatting | bytes 524288 | tf_op jit(solution)/shard_map/reshape | solution.py:161
  11.9 0.3 convert_reduce_fusion.2
  12.2 6.5 %all-to-all-done = f32[8,47,128]{2,1,0:T(8,128)S(1)} async-done(((f32[8,47,128]{2,1,0:T(8,128)}), f32[8,47,128]{2,1,0:T(8,128)S(1)}, u32[]{:S(2)}, u32[]{:S(2)}) %all-to-all-start) | async-done | bytes 192544 | tf_op jit(solution)/shard_map/all_to_all | solution.py:135
  19.1 0.2 reshape_squeeze_stack.7
  19.5 0.2 reshape_squeeze_stack.6
  20.0 3.2 %convert_reduce_fusion = (f32[32,256]{1,0:T(8,128)S(1)}, f32[2,32,32]{2,1,0:T(8,128)S(1)}, bf16[2,32,32,256]{3,2,1,0:T(8,128)(2,1)S(1)}) fusion(f32[2,32,176]{2,1,0:T(8,128)S(1)} %eq.34, f32[2,32,176]{2,1,0:T(8,128)S(1)} %eq.30), kind=kOutput, calls=%fused_computation.3 | convolution fusion | flops 189880320 | bytes 1179648 | tf_op jit(solution)/shard_map/gkbv,gkbu->gkvu/dot_general | solution.py:153
  23.2 0.2 fusion.22
  23.5 0.4 fusion.17
  23.9 0.6 %fusion.12 = bf16[2,32,64,1]{2,1,3,0:T(8,128)(2,1)S(1)} fusion(f32[2,32,64]{2,1,0:T(8,128)S(1)} %fusion.22, f32[2,32,32,64]{3,2,1,0:T(8,128)S(1)} %fusion.17, bf16[32,64,64,1]{2,1,0,3:T(8,128)(2,1)S(1)} %reshape.123, f32[4,2,94,64]{3,2,1,0:T(8,128)S(1)} %reshape.113), kind=kOutput, calls=%fused_computation.24 | convolution fusion | flops 100675584 | bytes 1646592 | tf_op jit(solution)/shard_map/gkvsj,kij->gvsi/dot_general | solution.py:177
  24.5 0.3 convolution_bitcast_fusion.1
  24.8 0.3 fusion.25
  25.1 0.7 %fusion.4 = f32[256,64]{0,1:T(8,128)S(1)} fusion(f32[256,64]{0,1:T(8,128)S(1)} %copy.60, f32[256,64]{0,1:T(8,128)S(1)} %fusion.25, bf16[2,32,32,256]{3,2,1,0:T(8,128)(2,1)S(1)} %get-tuple-element.8, f32[2,32,32,64]{3,2,1,0:T(8,128)S(1)} %convolution_bitcast_fusion.1), kind=kOutput, calls=%fused_computation.16 | convolution fusion | flops 201359360 | bytes 1769472 | tf_op jit(solution)/shard_map/gkvu,gkvsj->usj/dot_general | solution.py:184
  25.8 0.4 %fusion.15 = f32[2,32,32,64]{3,2,1,0:T(8,128)S(1)} fusion(bf16[2,32,32,256]{3,2,1,0:T(8,128)(2,1)S(1)} %get-tuple-element.8, f32[256,64]{0,1:T(8,128)S(1)} %fusion.4), kind=kOutput, calls=%fused_computation.35 | convolution fusion | flops 67125248 | bytes 1638400 | tf_op jit(solution)/shard_map/gkvu,usj->gkvsj/dot_general | solution.py:176
  26.2 0.6 %fusion.10 = f32[2,32,64]{2,1,0:T(8,128)S(1)} fusion(f32[2,32,64]{2,1,0:T(8,128)S(1)} %fusion.22, f32[2,32,32,64]{3,2,1,0:T(8,128)S(1)} %fusion.15, bf16[32,64,64,1]{2,1,0,3:T(8,128)(2,1)S(1)} %reshape.123, f32[4,2,94,64]{3,2,1,0:T(8,128)S(1)} %reshape.113), kind=kOutput, calls=%fused_computation.22 | convolution fusion | flops 100671488 | bytes 1654784 | tf_op jit(solution)/shard_map/gkvsj,kij->gvsi/dot_general | solution.py:177
  26.9 0.3 convolution_bitcast_fusion
  27.1 0.7 %fusion.6 = f32[256,64]{0,1:T(8,128)S(1)} fusion(f32[256,64]{0,1:T(8,128)S(1)} %fusion.4, f32[256,64]{0,1:T(8,128)S(1)} %fusion.25, bf16[2,32,32,256]{3,2,1,0:T(8,128)(2,1)S(1)} %get-tuple-element.8, f32[2,32,32,64]{3,2,1,0:T(8,128)S(1)} %convolution_bitcast_fusion), kind=kOutput, calls=%fused_computation.18 | convolution fusion | flops 201359360 | bytes 1769472 | tf_op jit(solution)/shard_map/gkvu,gkvsj->usj/dot_general | solution.py:184
  28.2 10.5 %all_to_all.10 = f32[8,36,128]{2,1,0:T(8,128)S(1)} all-to-all(f32[8,36,128]{2,1,0:T(8,128)S(1)} %reshape.119), channel_id=1, replica_groups=mesh['parts'=2,'pix'=4,'ang'=2,'sl'=2] {'pix','ang'}, dimensions={0} | all-to-all | bytes 294912 | tf_op jit(solution)/shard_map/all_to_all | solution.py:198
  39.0 0.8 %slice.23 = f32[64,512]{1,0:T(8,128)} reshape(f32[64,8,64]{2,1,0:T(8,128)S(1)} %copy.49) | data formatting | bytes 262144 | tf_op jit(solution)/shard_map/slice | solution.py:201
  39.8 0.7 %reshape.121 = f32[1,8,512]{2,1,0:T(8,128)} reshape(f32[8,8,64]{2,1,0:T(8,128)S(1)} %copy.50) | data formatting | bytes 32768 | tf_op jit(solution)/shard_map/reshape | solution.py:202
  (35 shorter events, 1.7 us)
Async XLA Ops:
  0.6 2.1 %copy-start.1 = (s32[1,1,1408]{2,1,0:T(1,128)S(1)}, s32[1,1,1408]{2,1,0:T(1,128)}, u32[]{:S(2)}) copy-start(s32[1,1,1408]{2,1,0:T(1,128)} %param.9) | copy-start | bytes 16900
  0.6 2.1 %copy-start.2 = (s32[1,1,1408]{2,1,0:T(1,128)S(1)}, s32[1,1,1408]{2,1,0:T(1,128)}, u32[]{:S(2)}) copy-start(s32[1,1,1408]{2,1,0:T(1,128)} %param.8) | copy-start | bytes 16900
  1.5 9.2 %copy-start = (bf16[32,4096]{1,0:T(8,128)(2,1)S(1)}, bf16[32,4096]{1,0:T(8,128)(2,1)}, u32[]{:S(2)}) copy-start(bf16[32,4096]{1,0:T(8,128)(2,1)} %param.7) | copy-start | bytes 786436
  3.5 15.2 %all-to-all-start = ((f32[8,47,128]{2,1,0:T(8,128)}), f32[8,47,128]{2,1,0:T(8,128)S(1)}, u32[]{:S(2)}, u32[]{:S(2)}) async-start(f32[8,47,128]{2,1,0:T(8,128)} %pad_maximum_fusion.1), calls=%async_computation | async-start | bytes 393216 | tf_op jit(solution)/shard_map/all_to_all | solution.py:135
